TPU v7x, 32 devices: a whole 2x2x4 slice. The times are simulated.
32 devices in a mesh: groups: 2 (over y), lat: 4 (over z), slc: 2 (over x), rep: 2 (over core).
Axes of the slice: x: 2, y: 2, z: 4, core: 2. Of those that a mesh axis runs over, the one named last changes fastest.
Arguments:
- atom_xy: float32 [8, 2, 2, 256], P(('groups', 'lat'), 'slc'), parts along dimension 0, may hold values from 0 to 4096, as said below
- atom_species: int32 [8, 2, 256], P(('groups', 'lat'), 'slc'), parts along dimension 0, may hold values from 0 to 7
- atom_slab: int32 [8, 2, 256], P(('groups', 'lat'), 'slc'), parts along dimension 0, may hold values from 0 to 1
- species_amp: float32 [8], replicated, may hold values from 0.5 to 3
- species_spread: float32 [8], replicated, may hold values from 2 to 6
- margin: int32 [8, 2, 2, 2, 3, 128], P(('groups', 'lat'), 'slc', None, 'rep'), parts along dimension 0, may hold values from -1 to 255, as said below
- probe_pos: int32 [64, 2], P(('groups', 'lat', 'slc', 'rep')), parts along dimension 0, may hold values from 0 to 4092, as said below
Outputs:
- exit_wave: bfloat16 [64, 256, 2, 256], P(('groups', 'lat', 'slc', 'rep')), parts along dimension 0
There are 2 independent parts, one for each index of `groups`. A program takes and returns all parts, laid end to end along the dimension named above; an argument that names none is the same for every part. Nothing has to cross between parts.
Inputs may be any that keep to these rules, and one draw needn't show every extreme that they name: `atom_xy`: atom a of tile v has x between (v * 256 + a) b and (v * 256 + a + 1) b with b = 4, and y in [0, 256). `probe_pos`: the 2 probes of one lateral index, slice owner and rep index share their x anchor; the centre of each window lies in tile t, x is a multiple of 4 taken modulo 4096, and y is below 256. `margin`: each block lists a run of consecutive local atom indices in rising order, then -1: the atoms of tile v whose x lies within 128 pixels of the probes' windows (x modulo 4096).
All inputs are finite; a program needn't handle non-finite values.
Results may differ from a plain program's by a relative error of at most 0.03.
Values may be sent and summed in bfloat16 or wider, within the bound.
No kernel may reach another device: no remote copies, remote signals or barrier semaphores. Data moves between devices by JAX's collectives and lax.ppermute only.
A program may use at most 128 MiB of HBM per device.

v0:
```python
import functools
import math

import jax
import jax.numpy as jnp
from jax import lax
from jax.experimental import pallas as pl
from jax.experimental.pallas import tpu as pltpu
from jax.sharding import PartitionSpec as P

W = 256
SL_DEV = 2


PROPAGATION_COEF = 0.001
DEFOCUS_COEF = 4.19


def centered_frequency(window):
    indices = jnp.arange(window, dtype=jnp.int32)
    return jnp.where(indices < window // 2, indices, indices - window).astype(jnp.float32)


def dft_parts(window, direction):
    indices = jnp.arange(window, dtype=jnp.int32)
    product = indices[:, None] * indices[None, :] % window
    angle_table = 2.0 * math.pi / window * product.astype(jnp.float32)
    real_part = (jnp.cos(angle_table) / math.sqrt(window)).astype(jnp.bfloat16)
    imag_part = (direction * jnp.sin(angle_table) / math.sqrt(window)).astype(jnp.bfloat16)
    return real_part, imag_part


def block_tables(window):
    f_re, f_im = dft_parts(window, -1.0)
    i_re, i_im = dft_parts(window, 1.0)

    def right(re, im):
        return jnp.concatenate(
            [jnp.concatenate([re, im], 1), jnp.concatenate([-im, re], 1)], 0
        )

    def left(re, im):
        return jnp.concatenate(
            [jnp.concatenate([re, -im], 1), jnp.concatenate([im, re], 1)], 0
        )

    return left(f_re, f_im), right(f_re, f_im), left(i_re, i_im), right(i_re, i_im)


def propagator(window):
    frequency = centered_frequency(window)
    radius = frequency[:, None] * frequency[:, None] + frequency[None, :] * frequency[None, :]
    inside = (9.0 * radius < window * window).astype(jnp.float32)
    phase_angle = -PROPAGATION_COEF * (65536.0 / (window * window)) * radius
    return jnp.stack([inside * jnp.cos(phase_angle), inside * jnp.sin(phase_angle)], 0)


def start_spectrum(window):
    frequency = centered_frequency(window)
    radius = frequency[:, None] * frequency[:, None] + frequency[None, :] * frequency[None, :]
    inside = (16.0 * radius < window * window).astype(jnp.float32)
    norm_scale = window / jnp.sqrt(jnp.sum(inside))
    phase_angle = -(DEFOCUS_COEF / window) * radius
    spectrum = jnp.concatenate(
        [inside * norm_scale * jnp.cos(phase_angle), inside * norm_scale * jnp.sin(phase_angle)], 0
    )
    return spectrum.astype(jnp.bfloat16)


def atom_fields(positions, species, slab, species_amp, species_spread, layers):
    species_match = (
        species[None, :] == jnp.arange(species_amp.shape[0], dtype=jnp.int32)[:, None]
    ).astype(species_amp.dtype)
    amplitude = jnp.sum(species_match * species_amp[:, None], 0)
    spread = jnp.sum(species_match * species_spread[:, None], 0)
    inverse = 0.5 / (spread * spread)
    slab_match = (slab[None, :] == jnp.arange(layers, dtype=jnp.int32)[:, None]).astype(
        amplitude.dtype
    )
    return jnp.concatenate([positions, inverse[None, :], slab_match * amplitude[None, :]], 0)


def pick_rows(fields, pick_list):
    valid_mask = (pick_list >= 0).astype(fields.dtype)
    safe_index = jnp.maximum(pick_list, 0)
    gathered = fields[:, safe_index]
    return jnp.concatenate([gathered[:3], gathered[3:] * valid_mask[None]], 0)


def slab_potentials(row_block, anchors, window, layers, field_x):
    pixels = jnp.arange(window, dtype=jnp.float32)
    half_width = 0.5 * window
    half_field = 0.5 * field_x
    inverse = row_block[None, :, 2, :, None]
    shift_x = anchors[:, 0].astype(jnp.float32)[:, None, None, None]
    shift_y = anchors[:, 1].astype(jnp.float32)[:, None, None, None]
    dist_x = (
        jnp.mod(row_block[None, :, 0, :, None] - shift_x - pixels + half_field, field_x)
        - half_field
    )
    across = jnp.exp(-dist_x * dist_x * inverse).astype(jnp.bfloat16)
    dist_y = (
        jnp.mod(row_block[None, :, 1, :, None] - shift_y - pixels + half_width, window)
        - half_width
    )
    along = jnp.exp(-dist_y * dist_y * inverse)
    amplitudes = row_block[:, 3 : 3 + layers]
    weighted = (amplitudes[None, :, :, :, None] * along[:, :, None, :, :]).astype(jnp.bfloat16)
    return jnp.einsum("phax,phlay->phlxy", across, weighted, preferred_element_type=jnp.float32)


def slices_kernel(pot_ref, fl_ref, fr_ref, il_ref, ir_ref, prop_ref, spec_ref, out_ref, wave_ref):
    w = pot_ref.shape[-1]
    step = pl.program_id(1)
    f32, bf16 = jnp.float32, jnp.bfloat16

    def dot(a, b):
        return jnp.dot(a, b, preferred_element_type=f32)

    @pl.when(step == 0)
    def _():
        rows = dot(il_ref[...], spec_ref[...]).astype(bf16)
        rows = jnp.concatenate([rows[:w], rows[w:]], 1)
        wave_ref[...] = dot(rows, ir_ref[...]).astype(bf16)

    psi = wave_ref[...]
    wr = psi[:, :w].astype(f32)
    wi = psi[:, w:].astype(f32)
    v = pot_ref[0, 0]
    cv = jnp.cos(v)
    sv = jnp.sin(v)
    tr = (wr * cv - wi * sv).astype(bf16)
    ti = (wr * sv + wi * cv).astype(bf16)
    rw = dot(jnp.concatenate([tr, ti], 1), fr_ref[...]).astype(bf16)
    sp = dot(fl_ref[...], jnp.concatenate([rw[:, :w], rw[:, w:]], 0))
    sr = sp[:w]
    si = sp[w:]
    pr = prop_ref[0]
    pi = prop_ref[1]
    spb = jnp.concatenate(
        [(sr * pr - si * pi).astype(bf16), (sr * pi + si * pr).astype(bf16)], 0
    )
    br = dot(il_ref[...], spb).astype(bf16)
    psi = dot(jnp.concatenate([br[:w], br[w:]], 1), ir_ref[...]).astype(bf16)
    wave_ref[...] = psi

    @pl.when(step == pl.num_programs(1) - 1)
    def _():
        out_ref[0] = psi


def run_slices(pot, tables, prop, spec):
    batch, steps, w, _ = pot.shape
    fl, fr, il, ir = tables
    full = lambda shape: pl.BlockSpec(shape, lambda p, s: (0,) * len(shape))
    flops = batch * steps * 4 * 2 * w * (2 * w) * (2 * w)
    return pl.pallas_call(
        slices_kernel,
        out_shape=jax.ShapeDtypeStruct((batch, w, 2 * w), jnp.bfloat16),
        grid=(batch, steps),
        in_specs=[
            pl.BlockSpec((1, 1, w, w), lambda p, s: (p, s, 0, 0)),
            full((2 * w, 2 * w)),
            full((2 * w, 2 * w)),
            full((2 * w, 2 * w)),
            full((2 * w, 2 * w)),
            full((2, w, w)),
            full((2 * w, w)),
        ],
        out_specs=pl.BlockSpec((1, w, 2 * w), lambda p, s: (p, 0, 0)),
        scratch_shapes=[pltpu.VMEM((w, 2 * w), jnp.bfloat16)],
        compiler_params=pltpu.CompilerParams(
            dimension_semantics=("arbitrary", "arbitrary"),
        ),
        cost_estimate=pl.CostEstimate(
            flops=flops,
            transcendentals=batch * steps * 2 * w * w,
            bytes_accessed=batch * steps * w * w * 4 + 4 * (2 * w) ** 2 * 2 + batch * w * w * 4,
        ),
    )(pot, fl, fr, il, ir, prop, spec)


def shards(atom_xy, atom_species, atom_slab, species_amp, species_spread, margin, probe_pos):
    layers = SL_DEV
    window = W
    atoms = atom_xy.shape[-1]
    cap = margin.shape[-1]
    n_lat = lax.axis_size("lat")
    owners = lax.axis_size("slc")
    field_x = n_lat * atoms * (2 * window // cap)
    fields = atom_fields(
        atom_xy[0, 0], atom_species[0, 0], atom_slab[0, 0], species_amp, species_spread, layers
    )
    field_count = fields.shape[0]
    pick_table = margin[0, 0, :, 0]
    picked = jax.vmap(jax.vmap(lambda lst: pick_rows(fields, lst)))(pick_table)
    to_left = lax.ppermute(
        picked[:, 0], "lat", [((i + 1) % n_lat, i) for i in range(n_lat)]
    )
    to_right = lax.ppermute(
        picked[:, 2], "lat", [(i, (i + 1) % n_lat) for i in range(n_lat)]
    )
    local = jnp.stack([to_right, picked[:, 1], to_left], 1)
    gathered = lax.all_gather(local, "slc", axis=0, tiled=False)
    me = lax.axis_index("slc")
    mine = lax.dynamic_index_in_dim(gathered, me, 1, keepdims=False)
    hop_owner = (me + jnp.arange(owners)) % owners
    rows = jnp.take(mine, hop_owner, axis=0)
    rows = jnp.transpose(rows, (0, 2, 1, 3)).reshape(owners, field_count, 3 * cap)
    pot = slab_potentials(rows, probe_pos, window, layers, field_x)
    batch = probe_pos.shape[0]
    pot = pot.reshape(batch, owners * layers, window, window)
    tables = block_tables(window)
    wave = run_slices(pot, tables, propagator(window), start_spectrum(window))
    return wave.reshape(batch, window, 2, window)


def solution(mesh):
    in_specs = (
        P(("groups", "lat"), "slc", None, None),
        P(("groups", "lat"), "slc", None),
        P(("groups", "lat"), "slc", None),
        P(),
        P(),
        P(("groups", "lat"), "slc", None, "rep", None, None),
        P(("groups", "lat", "slc", "rep"), None),
    )
    out_specs = P(("groups", "lat", "slc", "rep"), None, None, None)
    return jax.shard_map(shards, mesh=mesh, in_specs=in_specs, out_specs=out_specs, check_vma=False)
```

profile of v0, /device:TPU:0, one launch (start us, length us, event | category | flops | bytes accessed | tf_op | source)
XLA Modules:
  0.0 56.9 jit_solution(4221360322253668695)
XLA Ops:
  0.0 0.7 %maximum_reduce_fusion = s32[2,3,128]{2,1,0:T(4,128)S(1)} fusion(s32[1,1,2,1,3,128]{5,3,4,2,1,0:T(1,128)} %param.12), kind=kLoop, calls=%fused_computation.106 | loop fusion | flops 768 | bytes 6144 | tf_op jit(solution)/shard_map/vmap(vmap())/max | solution.py:85
  0.7 0.7 %compare_convert_fusion = f32[1,1,2,1,3,128]{5,3,4,2,1,0:T(1,128)S(1)} fusion(s32[1,1,2,1,3,128]{5,3,4,2,1,0:T(1,128)} %param.12), kind=kLoop, calls=%fused_computation.85 | loop fusion | flops 1536 | bytes 6144 | tf_op jit(solution)/shard_map/vmap(vmap())/convert_element_type | solution.py:84
  1.4 0.8 %select_reduce_fusion.1 = (f32[256]{0:T(256)S(1)}, f32[256]{0:T(256)S(1)}) fusion(f32[8]{0:T(128)} %param.11, s32[256]{0:T(256)} %bitcast.50, f32[8]{0:T(128)} %param.10), kind=kLoop, calls=%fused_computation.88 | loop fusion | flops 9728 | bytes 3136 | tf_op jit(solution)/shard_map/reduce_sum | solution.py:75
  2.2 0.7 %compare_select_fusion.1 = f32[2,256]{1,0:T(2,128)S(1)} fusion(f32[256]{0:T(256)S(1)} %get-tuple-element.8, s32[256]{0:T(256)} %bitcast.51), kind=kLoop, calls=%fused_computation.99 | loop fusion | flops 1024 | bytes 4096 | tf_op jit(solution)/shard_map/mul | solution.py:80
  2.9 0.7 %pad_maximum_fusion.11 = f32[5,256]{1,0:T(8,128)S(1)} fusion(f32[2,256]{1,0:T(2,128)S(1)} %compare_select_fusion.1, f32[1,256]{1,0:T(1,128)S(1)} %bitcast.48, f32[2,256]{1,0:T(2,128)} %bitcast.49), kind=kLoop, calls=%fused_computation.86 | loop fusion | flops 2560 | bytes 10240 | tf_op jit(solution)/shard_map/concatenate | solution.py:80
  3.7 1.6 %gather_fusion = f32[768,5]{1,0:T(8,128)S(1)} fusion(f32[5,256]{0,1:T(8,128)S(1)} %copy.41, s32[1024]{0:T(1024)S(1)} %pad_clamp_fusion.1), kind=kCustom, calls=%fused_computation | custom fusion | bytes 33792 | tf_op jit(solution)/shard_map/vmap(vmap())/gather | solution.py:86
  5.5 5.1 %collective-permute-start.1 = (f32[2,5,128]{2,0,1:T(2,128)S(1)}, f32[2,5,128]{2,0,1:T(2,128)S(1)}, u32[]{:S(2)}, u32[]{:S(2)}) collective-permute-start(f32[2,5,128]{2,0,1:T(2,128)S(1)} %get-tuple-element.19), channel_id=1, source_target_pairs={{4,0},{8,4},{12,8},{0,12},{5,1},{9,5},{13,9},{1,13},{6,2},{10,6},{... | collective-permute-start | bytes 15368 | tf_op jit(solution)/shard_map/ppermute | solution.py:197
  10.6 1.0 %multiply_convert_fusion.2 = (bf16[256,256]{1,0:T(8,128)(2,1)S(1)}, bf16[256,256]{1,0:T(8,128)(2,1)S(1)}) fusion(), kind=kLoop, calls=%fused_computation.69 | loop fusion | flops 1179648 | bytes 262144 | tf_op jit(solution)/shard_map/convert_element_type | solution.py:29
  11.7 1.0 %fusion.44 = (bf16[256,256]{1,0:T(8,128)(2,1)S(1)}, bf16[256,256]{1,0:T(8,128)(2,1)S(1)}) fusion(), kind=kLoop, calls=%fused_computation.76 | loop fusion | flops 1572864 | bytes 262144 | tf_op jit(solution)/shard_map/neg | solution.py:44
  12.7 1.0 %multiply_convert_fusion.4 = bf16[256,256]{1,0:T(8,128)(2,1)S(1)} fusion(), kind=kLoop, calls=%fused_computation.71 | loop fusion | flops 1048576 | bytes 131072 | tf_op jit(solution)/shard_map/convert_element_type | solution.py:28
  13.6 0.7 %convert_reduce_fusion = f32[]{:T(128)} fusion(f32[256]{0:T(256)S(1)} %fusion.51), kind=kLoop, calls=%fused_computation.68 | loop fusion | flops 327679 | bytes 1028 | tf_op jit(solution)/shard_map/reduce_sum | solution.py:62
  14.4 1.0 %fusion.33 = (f32[1,256,256]{2,1,0:T(8,128)S(1)}, f32[1,256,256]{2,1,0:T(8,128)S(1)}) fusion(f32[256]{0:T(256)S(1)} %fusion.51), kind=kLoop, calls=%fused_computation.60 | loop fusion | flops 393216 | bytes 525312 | tf_op jit(solution)/shard_map/mul | solution.py:55
  16.3 1.2 %fusion.31 = (bf16[256,256]{1,0:T(8,128)(2,1)S(1)}, bf16[256,256]{1,0:T(8,128)(2,1)S(1)}) fusion(f32[]{:T(128)S(6)} %div.64, f32[256]{0:T(256)S(1)} %fusion.51), kind=kLoop, calls=%fused_computation.58 | loop fusion | flops 589824 | bytes 263172 | tf_op jit(solution)/shard_map/convert.1
  17.6 0.7 %pad_maximum_fusion.9.spec_ref = bf16[512,256]{1,0:T(8,128)(2,1)} fusion(bf16[256,256]{1,0:T(8,128)(2,1)S(1)} %get-tuple-element.22, bf16[256,256]{1,0:T(8,128)(2,1)S(1)} %get-tuple-element.21), kind=kLoop, calls=%fused_computation.67 | loop fusion | flops 524288 | bytes 524288 | tf_op jit(solution)/shard_map/concatenate | solution.py:64
  18.3 0.8 %pad_maximum_fusion.8.prop_ref = f32[2,256,256]{2,1,0:T(8,128)} fusion(f32[1,256,256]{2,1,0:T(8,128)S(1)} %get-tuple-element.24, f32[1,256,256]{2,1,0:T(8,128)S(1)} %get-tuple-element.23), kind=kLoop, calls=%fused_computation.44 | loop fusion | flops 131072 | bytes 1048576 | tf_op jit(solution)/shard_map/stack | solution.py:55
  19.1 1.4 %fusion.26 = (bf16[512,512]{1,0:T(8,128)(2,1)}, bf16[512,512]{1,0:T(8,128)(2,1)}, bf16[512,512]{1,0:T(8,128)(2,1)}, bf16[512,512]{1,0:T(8,128)(2,1)}) fusion(bf16[256,256]{1,0:T(8,128)(2,1)S(1)} %multiply_convert_fusion.4, bf16[256,256]{1,0:T(8,128)(2,1)S(1)} %get-tuple-element.30, bf16[256,256]{1,0:T(8,128)(2,1)S(1)} %get-tuple-element.27, ...), kind=kLoop, calls=%fused_computation.43 | loop fusion | flops 6815744 | bytes 2752512 | tf_op jit(solution)/shard_map/concatenate | solution.py:38
  20.6 4.5 %all-gather = f32[4,3,5,128]{3,1,2,0:T(4,128)S(1)} all-gather(f32[2,3,5,128]{3,1,2,0:T(4,128)S(1)} %copy.44), channel_id=2, replica_groups=mesh['groups'=2,'lat'=4,'slc'=2,'rep'=2] {'slc'}, dimensions={0}, use_global_device_ids=true | all-gather | bytes 46080 | tf_op jit(solution)/shard_map/all_gather | solution.py:204
  25.1 0.6 %gather_fusion.1 = f32[2,3,5,128]{3,1,2,0:T(4,128)S(1)} fusion(f32[2,3,5,128]{3,1,2,0:T(4,128)S(1)} %dynamic-slice_bitcast_fusion, s32[1024]{0:T(1024)S(1)} %pad_clamp_fusion), kind=kCustom, calls=%fused_computation.1 | custom fusion | bytes 30728 | tf_op jit(solution)/shard_map/jit(_take)/gather | solution.py:208
  25.8 1.2 %fusion.2 = f32[2,2,384,256]{3,2,1,0:T(8,128)S(1)} fusion(f32[2,384]{1,0:T(2,128)S(1)} %get-tuple-element.16, f32[2,2,384]{2,1,0:T(2,128)S(1)} %get-tuple-element.26), kind=kLoop, calls=%fused_computation.10 | loop fusion | flops 4718592 | bytes 1582080 | tf_op jit(solution)/shard_map/exp | solution.py:106
  27.1 1.6 %copy.48 = f32[2,2,384,256]{2,3,1,0:T(8,128)} copy(f32[2,2,384,256]{3,2,1,0:T(8,128)S(1)} %fusion.2) | data formatting | bytes 3145728 | tf_op jit(solution)/shard_map/exp | solution.py:106
  28.7 3.2 %convolution_bitcast_fusion = f32[2,2,2,256,256]{3,4,2,1,0:T(8,128)S(1)} fusion(f32[2,2,384,256]{2,3,1,0:T(8,128)} %copy.48, f32[2,2,384]{2,1,0:T(2,128)S(1)} %copy.47, f32[2,2,384]{2,1,0:T(2,128)S(1)} %get-tuple-element.25, f32[2,384]{1,0:T(2,128)S(1)} %get-tuple-element.16), kind=kOutput, calls=%fused_computation.7 | convolution fusion | flops 409337856 | bytes 3685376 | tf_op jit(solution)/shard_map/phax,phlay->phlxy/dot_general | solution.py:109
  32.0 1.9 %copy.49 = f32[2,2,2,256,256]{4,3,2,1,0:T(8,128)} copy(f32[2,2,2,256,256]{3,4,2,1,0:T(8,128)S(1)} %convolution_bitcast_fusion) | data formatting | bytes 4194304 | tf_op jit(solution)/shard_map/phax,phlay->phlxy/transpose | solution.py:109
  33.8 21.1 %shard_map.73 = bf16[2,256,512]{2,1,0:T(8,128)(2,1)} custom-call(f32[2,4,256,256]{3,2,1,0:T(8,128)} %bitcast.40, bf16[512,512]{1,0:T(8,128)(2,1)} %get-tuple-element.13.fl_ref, bf16[512,512]{1,0:T(8,128)(2,1)} %get-tuple-element.14.fr_ref, bf16[512,512]{1,0:T(8,128)(2,1)} %get-tuple-element.10.il_ref, bf16[512,512]{1,0:T(8,128)(2,1)} %get-tuple-element.9.ir_ref, ...), custom_call_target="tpu_custom_call" | custom-call | flops 4294967296 | bytes 4718592 | tf_op jit(solution)/shard_map/pallas_call | solution.py:157
  55.0 2.0 %reshape.274 = bf16[2,256,2,256]{3,2,1,0:T(2,128)(2,1)} reshape(bf16[2,256,512]{2,1,0:T(8,128)(2,1)} %shard_map.73) | data formatting | bytes 1048576 | tf_op jit(solution)/shard_map/reshape | solution.py:215
  (29 shorter events, 0.8 us)
Async XLA Ops:
  0.0 15.5 %copy-start = (s32[2,2]{1,0:T(2,128)S(1)}, s32[2,2]{1,0:T(2,128)}, u32[]{:S(2)}) copy-start(s32[2,2]{1,0:T(2,128)} %param.13) | copy-start | bytes 52
  5.5 15.0 %collective-permute-start.1 = (f32[2,5,128]{2,0,1:T(2,128)S(1)}, f32[2,5,128]{2,0,1:T(2,128)S(1)}, u32[]{:S(2)}, u32[]{:S(2)}) collective-permute-start(f32[2,5,128]{2,0,1:T(2,128)S(1)} %get-tuple-element.19), channel_id=1, source_target_pairs={{4,0},{8,4},{12,8},{0,12},{5,1},{9,5},{13,9},{1,13},{6,2},{10,6},{... | collective-permute-start | bytes 15368 | tf_op jit(solution)/shard_map/ppermute | solution.py:197
  10.6 9.9 %collective-permute-start = (f32[2,5,128]{2,0,1:T(2,128)S(1)}, f32[2,5,128]{2,0,1:T(2,128)S(1)}, u32[]{:S(2)}, u32[]{:S(2)}) collective-permute-start(f32[2,5,128]{2,0,1:T(2,128)S(1)} %get-tuple-element.18), channel_id=1, source_target_pairs={{0,4},{4,8},{8,12},{12,0},{1,5},{5,9},{9,13},{13,1},{2,6},{6,10},{... | collective-permute-start | bytes 15368 | tf_op jit(solution)/shard_map/ppermute | solution.py:200
where the time goes:
time: 57.2 us; the launch traced here: 56.9 us
  Pallas kernels  21.1 us (37%)
  other arithmetic  14.1 us (25%)
  local copies, waits for them, and re-layouts  7.96 us (14%)
  starting transfers between devices  5.13 us (9%)
  blocking collectives  4.45 us (8%)
  matrix products  3.24 us (6%)
  between operations  0.89 us (2%)
    pallas_call x1, Pallas kernels, run_slices(): pl.pallas_call(slices_kernel, out_shape=jax.ShapeDtypeStruct((batch, w, 2...  21.1 us
    ppermute x1, starting transfers between devices, shards(): lax.ppermute(picked[:, 0], 'lat', [((i + 1) % n_lat, i) for i in range(n_...  5.13 us
    all_gather x1, blocking collectives, shards(): gathered = lax.all_gather(local, 'slc', axis=0, tiled=False)  4.45 us
    dot_general x1, matrix products, slab_potentials(): jnp.einsum('phax,phlay->phlxy', across, weighted, preferred_element_type=...  3.24 us
    reshape x1, local copies, waits for them, and re-layouts, shards(): return wave.reshape(batch, window, 2, window)  1.96 us
    transpose x1, local copies, waits for them, and re-layouts, slab_potentials(): jnp.einsum('phax,phlay->phlxy', across, weighted, preferred_element_type=...  1.88 us
    gather x2, local copies, waits for them, and re-layouts, pick_rows(): gathered = fields[:, safe_index]  1.72 us
    exp x1, local copies, waits for them, and re-layouts, slab_potentials(): along = jnp.exp(-dist_y * dist_y * inverse)  1.63 us
  transfers between devices with their start and end apart: 2, of which 0 were waited for; matrix products, arithmetic and copies ran while one was open for 16% of the time, Pallas kernels for 0%

commit v1 on v0

v1 whole, which is shorter than its diff:
```python
import functools
import math

import jax
import numpy as np
import jax.numpy as jnp
from jax import lax
from jax.experimental import pallas as pl
from jax.experimental.pallas import tpu as pltpu
from jax.sharding import PartitionSpec as P

W = 256
SL_DEV = 2


PROPAGATION_COEF = 0.001
DEFOCUS_COEF = 4.19


def centered_frequency(window):
    indices = np.arange(window, dtype=np.int32)
    return np.where(indices < window // 2, indices, indices - window).astype(np.float32)


def squared_radius(window):
    frequency = centered_frequency(window)
    return frequency[:, None] * frequency[:, None] + frequency[None, :] * frequency[None, :]


def dft_blocks(window):
    indices = np.arange(window, dtype=np.int32)
    product = indices[:, None] * indices[None, :] % window
    angle = np.float32(2.0 * math.pi / window) * product.astype(np.float32)
    scale = np.float32(math.sqrt(window))
    re = (np.cos(angle) / scale).astype(jnp.bfloat16)
    im = (np.sin(angle) / scale).astype(jnp.bfloat16)
    a = np.block([[re, -im], [im, re]])
    b = np.block([[re, im], [-im, re]])
    return a, b


def propagator(window):
    radius = squared_radius(window)
    inside = (np.float32(9.0) * radius < window * window).astype(np.float32)
    phase_angle = np.float32(-PROPAGATION_COEF * (65536.0 / (window * window))) * radius
    return np.stack([inside * np.cos(phase_angle), inside * np.sin(phase_angle)], 0)


def start_spectrum(window):
    radius = squared_radius(window)
    inside = (np.float32(16.0) * radius < window * window).astype(np.float32)
    norm_scale = np.float32(window) / np.sqrt(np.sum(inside, dtype=np.float32))
    phase_angle = np.float32(-(DEFOCUS_COEF / window)) * radius
    spectrum = np.concatenate(
        [inside * norm_scale * np.cos(phase_angle), inside * norm_scale * np.sin(phase_angle)], 0
    )
    return spectrum.astype(jnp.bfloat16)


def atom_fields(positions, species, slab, species_amp, species_spread, layers):
    species_match = (
        species[None, :] == jnp.arange(species_amp.shape[0], dtype=jnp.int32)[:, None]
    ).astype(species_amp.dtype)
    amplitude = jnp.sum(species_match * species_amp[:, None], 0)
    spread = jnp.sum(species_match * species_spread[:, None], 0)
    inverse = 0.5 / (spread * spread)
    slab_match = (slab[None, :] == jnp.arange(layers, dtype=jnp.int32)[:, None]).astype(
        amplitude.dtype
    )
    return jnp.concatenate([positions, inverse[None, :], slab_match * amplitude[None, :]], 0)


def pick_rows(fields, pick_list):
    valid_mask = (pick_list >= 0).astype(fields.dtype)
    safe_index = jnp.maximum(pick_list, 0)
    gathered = fields[:, safe_index]
    return jnp.concatenate([gathered[:3], gathered[3:] * valid_mask[None]], 0)


def wrap(value, period):
    return value - period * jnp.floor(value * (1.0 / period))


def slices_kernel(
    pos_ref, rows_ref, cols_ref, a_ref, b_ref, prop_ref, spec_ref, out_ref, wave_ref, pot_ref,
    *, field_x
):
    w = prop_ref.shape[-1]
    layers = pot_ref.shape[-1] // w
    p = pl.program_id(0)
    hop = pl.program_id(1)
    layer = pl.program_id(2)
    f32, bf16 = jnp.float32, jnp.bfloat16

    def dot(a, b):
        return jnp.dot(a, b, preferred_element_type=f32)

    @pl.when((hop == 0) & (layer == 0))
    def _():
        rows = dot(a_ref[...], spec_ref[...]).astype(bf16)
        rows = jnp.concatenate([rows[:w], rows[w:]], 1)
        wave_ref[...] = dot(rows, b_ref[...]).astype(bf16)

    @pl.when(layer == 0)
    def _():
        shift_x = pos_ref[p, 0].astype(f32)
        shift_y = pos_ref[p, 1].astype(f32)
        atom_x = rows_ref[0, 0:1, :]
        inverse_row = rows_ref[0, 2:3, :]
        pixel_col = lax.broadcasted_iota(jnp.int32, (w, 1), 0).astype(f32)
        dist_x = wrap(atom_x - shift_x - pixel_col + 0.5 * field_x, field_x) - 0.5 * field_x
        across = jnp.exp(-dist_x * dist_x * inverse_row).astype(bf16)
        atom_y = cols_ref[0, :, 1:2]
        inverse_col = cols_ref[0, :, 2:3]
        pixel_row = lax.broadcasted_iota(jnp.int32, (1, w), 1).astype(f32)
        dist_y = wrap(atom_y - shift_y - pixel_row + 0.5 * w, w) - 0.5 * w
        along = jnp.exp(-dist_y * dist_y * inverse_col)
        weighted = jnp.concatenate(
            [(cols_ref[0, :, 3 + l : 4 + l] * along).astype(bf16) for l in range(layers)], 1
        )
        pot_ref[...] = dot(across, weighted)

    psi = wave_ref[...]
    wr = psi[:, :w].astype(f32)
    wi = psi[:, w:].astype(f32)
    v = pot_ref[:, pl.ds(pl.multiple_of(layer * w, w), w)]
    cv = jnp.cos(v)
    sv = jnp.sin(v)
    tr = (wr * cv - wi * sv).astype(bf16)
    ti = (wr * sv + wi * cv).astype(bf16)
    rw = dot(jnp.concatenate([tr, ti], 1), a_ref[...]).astype(bf16)
    sp = dot(b_ref[...], jnp.concatenate([rw[:, :w], rw[:, w:]], 0))
    sr = sp[:w]
    si = sp[w:]
    pr = prop_ref[0]
    pi = prop_ref[1]
    spb = jnp.concatenate(
        [(sr * pr - si * pi).astype(bf16), (sr * pi + si * pr).astype(bf16)], 0
    )
    br = dot(a_ref[...], spb).astype(bf16)
    psi = dot(jnp.concatenate([br[:w], br[w:]], 1), b_ref[...]).astype(bf16)
    wave_ref[...] = psi

    @pl.when((hop == pl.num_programs(1) - 1) & (layer == pl.num_programs(2) - 1))
    def _():
        out_ref[0] = psi


def run_slices(probe_pos, rows, cols, window, layers, field_x):
    batch = probe_pos.shape[0]
    hops, fields, atoms = rows.shape
    w = window
    a, b = dft_blocks(w)
    prop = propagator(w)
    spec = start_spectrum(w)
    full = lambda shape: pl.BlockSpec(shape, lambda p, h, l, pos: (0,) * len(shape))
    steps = batch * hops * layers
    flops = steps * 4 * 2 * w * (2 * w) * (2 * w) + batch * hops * 2 * w * atoms * layers * w
    return pl.pallas_call(
        functools.partial(slices_kernel, field_x=float(field_x)),
        out_shape=jax.ShapeDtypeStruct((batch, w, 2 * w), jnp.bfloat16),
        grid_spec=pltpu.PrefetchScalarGridSpec(
            num_scalar_prefetch=1,
            grid=(batch, hops, layers),
            in_specs=[
                pl.BlockSpec((1, fields, atoms), lambda p, h, l, pos: (h, 0, 0)),
                pl.BlockSpec((1, atoms, fields), lambda p, h, l, pos: (h, 0, 0)),
                full((2 * w, 2 * w)),
                full((2 * w, 2 * w)),
                full((2, w, w)),
                full((2 * w, w)),
            ],
            out_specs=pl.BlockSpec((1, w, 2 * w), lambda p, h, l, pos: (p, 0, 0)),
            scratch_shapes=[
                pltpu.VMEM((w, 2 * w), jnp.bfloat16),
                pltpu.VMEM((w, layers * w), jnp.float32),
            ],
        ),
        compiler_params=pltpu.CompilerParams(
            dimension_semantics=("arbitrary", "arbitrary", "arbitrary"),
        ),
        cost_estimate=pl.CostEstimate(
            flops=flops,
            transcendentals=steps * 2 * w * w + batch * hops * 2 * atoms * w,
            bytes_accessed=2 * (2 * w) ** 2 * 2 + 3 * w * w * 4 + batch * w * w * 4,
        ),
    )(probe_pos, rows, cols, jnp.asarray(a), jnp.asarray(b), jnp.asarray(prop), jnp.asarray(spec))


def shards(atom_xy, atom_species, atom_slab, species_amp, species_spread, margin, probe_pos):
    layers = SL_DEV
    window = W
    atoms = atom_xy.shape[-1]
    cap = margin.shape[-1]
    n_lat = lax.axis_size("lat")
    owners = lax.axis_size("slc")
    field_x = n_lat * atoms * (2 * window // cap)
    fields = atom_fields(
        atom_xy[0, 0], atom_species[0, 0], atom_slab[0, 0], species_amp, species_spread, layers
    )
    field_count = fields.shape[0]
    pick_table = margin[0, 0, :, 0]
    picked = jax.vmap(jax.vmap(lambda lst: pick_rows(fields, lst)))(pick_table)
    to_left = lax.ppermute(
        picked[:, 0], "lat", [((i + 1) % n_lat, i) for i in range(n_lat)]
    )
    to_right = lax.ppermute(
        picked[:, 2], "lat", [(i, (i + 1) % n_lat) for i in range(n_lat)]
    )
    local = jnp.stack([to_right, picked[:, 1], to_left], 1)
    gathered = lax.all_gather(local, "slc", axis=0, tiled=False)
    me = lax.axis_index("slc")
    mine = lax.dynamic_index_in_dim(gathered, me, 1, keepdims=False)
    hop_owner = (me + jnp.arange(owners)) % owners
    rows = jnp.take(mine, hop_owner, axis=0)
    rows = jnp.transpose(rows, (0, 2, 1, 3)).reshape(owners, field_count, 3 * cap)
    cols = jnp.transpose(rows, (0, 2, 1))
    batch = probe_pos.shape[0]
    wave = run_slices(probe_pos, rows, cols, window, layers, field_x)
    return wave.reshape(batch, window, 2, window)


def solution(mesh):
    in_specs = (
        P(("groups", "lat"), "slc", None, None),
        P(("groups", "lat"), "slc", None),
        P(("groups", "lat"), "slc", None),
        P(),
        P(),
        P(("groups", "lat"), "slc", None, "rep", None, None),
        P(("groups", "lat", "slc", "rep"), None),
    )
    out_specs = P(("groups", "lat", "slc", "rep"), None, None, None)
    return jax.shard_map(shards, mesh=mesh, in_specs=in_specs, out_specs=out_specs, check_vma=False)
```

time: 57.2 us -> 44.2 us (0.77)
  other arithmetic: 14.1 us -> 1.03 us
  matrix products: 3.24 us -> 0 us
  Pallas kernels: 21.1 us -> 24.2 us
  waiting for transfers between devices: 0.01 us -> 1.54 us
  between operations: 0.89 us -> 0.12 us
    dot_general x1 -> x0, matrix products: 3.24 us -> none  [slab_potentials(): jnp.einsum('phax,phlay->phlxy', across, weighted, preferred_element_type=...]
    ppermute x1, starting transfers between devices: 0.01 us -> 3.1 us  [shards(): lax.ppermute(picked[:, 2], 'lat', [(i, (i + 1) % n_lat) for i in range(n_...]
    pallas_call x1, Pallas kernels: 21.1 us -> 24.2 us  [run_slices(): pl.pallas_call(functools.partial(slices_kernel, field_x=float(field_x)),...]
    ppermute x1, starting transfers between devices: 5.13 us -> 2.09 us  [shards(): lax.ppermute(picked[:, 0], 'lat', [((i + 1) % n_lat, i) for i in range(n_...]
    convert_element_type x3 -> x0, other arithmetic: 2.16 us -> none  [the longest x1 1 us: dft_parts(): (direction * jnp.sin(angle_table) / math.sqrt(window)).astype(jnp.bfloat16)]
    concatenate x2 -> x0, other arithmetic: 2.12 us -> none  [the longest x1 1.4 us: right(): jnp.concatenate([jnp.concatenate([re, im], 1), jnp.concatenate([-im, re],...]
    another operation x2 -> x0, other arithmetic: 2.06 us -> none
    unnamed x2 -> x14, local copies, waits for them, and re-layouts: 0.01 us -> 2.03 us
  transfers between devices with their start and end apart: 2 -> 2, of which waited for: 0 -> 1; matrix products, arithmetic and copies ran while one was open for 16% -> 0% of each run, Pallas kernels for 0% -> 0%
where the time goes in v1:
time: 44.2 us; the launch traced here: 43.9 us
  Pallas kernels  24.2 us (55%)
  local copies, waits for them, and re-layouts  7.43 us (17%)
  starting transfers between devices  5.2 us (12%)
  blocking collectives  4.45 us (10%)
  waiting for transfers between devices  1.54 us (3%)
  other arithmetic  1.03 us (2%)
    pallas_call x1, Pallas kernels, run_slices(): pl.pallas_call(functools.partial(slices_kernel, field_x=float(field_x)),...  24.2 us
    all_gather x1, blocking collectives, shards(): gathered = lax.all_gather(local, 'slc', axis=0, tiled=False)  4.45 us
    ppermute x1, starting transfers between devices, shards(): lax.ppermute(picked[:, 2], 'lat', [(i, (i + 1) % n_lat) for i in range(n_...  3.1 us
    ppermute x1, starting transfers between devices, shards(): lax.ppermute(picked[:, 0], 'lat', [((i + 1) % n_lat, i) for i in range(n_...  2.09 us
    unnamed x14, local copies, waits for them, and re-layouts  2.03 us
    reshape x1, local copies, waits for them, and re-layouts, shards(): return wave.reshape(batch, window, 2, window)  1.96 us
    gather x2, local copies, waits for them, and re-layouts, pick_rows(): gathered = fields[:, safe_index]  1.72 us
    ppermute x1, waiting for transfers between devices, shards(): lax.ppermute(picked[:, 2], 'lat', [(i, (i + 1) % n_lat) for i in range(n_...  1.54 us
  transfers between devices with their start and end apart: 2, of which 1 were waited for; matrix products, arithmetic and copies ran while one was open for 0% of the time, Pallas kernels for 0%

profile of v1, /device:TPU:0, one launch (start us, length us, event | category | flops | bytes accessed | tf_op | source)
XLA Modules:
  0.0 43.9 jit_solution(371821832098666796)
XLA Ops:
  0.0 0.8 %compare_convert_fusion = f32[1,1,2,1,3,128]{5,3,4,2,1,0:T(1,128)S(1)} fusion(s32[1,1,2,1,3,128]{5,3,4,2,1,0:T(1,128)} %param.16), kind=kLoop, calls=%fused_computation.9 | loop fusion | flops 1536 | bytes 6144 | tf_op jit(solution)/shard_map/vmap(vmap())/convert_element_type | solution.py:74
  0.8 0.0 copy-start.3
  0.8 0.0 copy-start.5
  0.8 0.6 %copy-done.6 = f32[8]{0:T(128)S(1)} copy-done((f32[8]{0:T(128)S(1)}, f32[8]{0:T(128)}, u32[]{:S(2)}) %copy-start.6) | copy-done | bytes 56
  1.4 0.0 copy-done.3
  1.5 0.1 select_reduce_fusion.1
  1.6 0.0 copy-start.4
  1.6 0.7 %copy-done.4 = s32[1,1,256]{2,1,0:T(1,128)S(1)} copy-done((s32[1,1,256]{2,1,0:T(1,128)S(1)}, s32[1,1,256]{2,1,0:T(1,128)}, u32[]{:S(2)}) %copy-start.4) | copy-done | bytes 1048
  2.3 0.7 %copy-done.2 = f32[1,1,2,256]{3,2,1,0:T(2,128)S(1)} copy-done((f32[1,1,2,256]{3,2,1,0:T(2,128)S(1)}, f32[1,1,2,256]{3,2,1,0:T(2,128)}, u32[]{:S(2)}) %copy-start.2) | copy-done | bytes 2072
  3.0 0.1 copy.40
  3.1 1.6 %gather_fusion = f32[768,5]{1,0:T(8,128)S(1)} fusion(f32[5,256]{0,1:T(8,128)S(1)} %copy.40, s32[1024]{0:T(1024)S(1)} %pad_clamp_fusion.1), kind=kCustom, calls=%fused_computation | custom fusion | bytes 33792 | tf_op jit(solution)/shard_map/vmap(vmap())/gather | solution.py:76
  4.7 0.1 copy.41
  4.9 3.1 %collective-permute-start = (f32[2,5,128]{2,0,1:T(2,128)S(1)}, f32[2,5,128]{2,0,1:T(2,128)S(1)}, u32[]{:S(2)}, u32[]{:S(2)}) collective-permute-start(f32[2,5,128]{2,0,1:T(2,128)S(1)} %get-tuple-element.7), channel_id=1, source_target_pairs={{0,4},{4,8},{8,12},{12,0},{1,5},{5,9},{9,13},{13,1},{2,6},{6,10},{... | collective-permute-start | bytes 15368 | tf_op jit(solution)/shard_map/ppermute | solution.py:207
  8.0 2.1 %collective-permute-start.1 = (f32[2,5,128]{2,0,1:T(2,128)S(1)}, f32[2,5,128]{2,0,1:T(2,128)S(1)}, u32[]{:S(2)}, u32[]{:S(2)}) collective-permute-start(f32[2,5,128]{2,0,1:T(2,128)S(1)} %get-tuple-element.8), channel_id=1, source_target_pairs={{4,0},{8,4},{12,8},{0,12},{5,1},{9,5},{13,9},{1,13},{6,2},{10,6},{... | collective-permute-start | bytes 15368 | tf_op jit(solution)/shard_map/ppermute | solution.py:204
  10.1 1.5 %collective-permute-done = f32[2,5,128]{2,0,1:T(2,128)S(1)} collective-permute-done((f32[2,5,128]{2,0,1:T(2,128)S(1)}, f32[2,5,128]{2,0,1:T(2,128)S(1)}, u32[]{:S(2)}, u32[]{:S(2)}) %collective-permute-start) | collective-permute-done | bytes 5152 | tf_op jit(solution)/shard_map/ppermute | solution.py:207
  11.7 0.0 collective-permute-done.1
  11.7 4.5 %all-gather = f32[4,3,5,128]{3,1,2,0:T(4,128)S(1)} all-gather(f32[2,3,5,128]{3,1,2,0:T(4,128)S(1)} %copy.43), channel_id=2, replica_groups=mesh['groups'=2,'lat'=4,'slc'=2,'rep'=2] {'slc'}, dimensions={0}, use_global_device_ids=true | all-gather | bytes 46080 | tf_op jit(solution)/shard_map/all_gather | solution.py:211
  16.1 0.6 %gather_fusion.1 = f32[2,3,5,128]{3,1,2,0:T(4,128)S(1)} fusion(f32[2,3,5,128]{3,1,2,0:T(4,128)S(1)} %dynamic-slice_bitcast_fusion, s32[1024]{0:T(1024)S(1)} %pad_clamp_fusion), kind=kCustom, calls=%fused_computation.1 | custom fusion | bytes 30728 | tf_op jit(solution)/shard_map/jit(_take)/gather | solution.py:215
  16.7 0.1 select_bitcast_fusion
  16.8 0.2 copy.45
  17.0 0.0 copy-start
  17.0 0.8 %copy.46.rows_ref = f32[2,5,384]{2,1,0:T(8,128)} copy(f32[2,5,384]{1,2,0:T(8,128)S(1)} %bitcast.27) | data formatting | bytes 30720 | tf_op jit(solution)/shard_map/reshape | solution.py:216
  17.8 24.2 %shard_map.109 = bf16[2,256,512]{2,1,0:T(8,128)(2,1)} custom-call(s32[2,2]{1,0:T(2,128)} %pos_ref.1, f32[2,5,384]{2,1,0:T(8,128)} %copy.46.rows_ref, f32[2,384,5]{2,1,0:T(8,128)} %bitcast.28, bf16[512,512]{1,0:T(8,128)(2,1)} %constant.56.clone.a_ref, bf16[512,512]{1,0:T(8,128)(2,1)} %constant.57.clone.b_ref, f32[2,256,256]{2,1,0:T(8,128)} %constant.58.clone.prop_ref, ...), custom_call_target="tpu_custom_call" | custom-call | flops 4697620480 | bytes 2359296 | tf_op jit(solution)/shard_map/pallas_call | solution.py:159
  42.0 2.0 %reshape.101 = bf16[2,256,2,256]{3,2,1,0:T(2,128)(2,1)} reshape(bf16[2,256,512]{2,1,0:T(8,128)(2,1)} %shard_map.109) | data formatting | bytes 1048576 | tf_op jit(solution)/shard_map/reshape | solution.py:220
  (22 shorter events, 0.1 us)
Async XLA Ops:
  0.0 0.8 %copy-start.1 = (s32[1,1,2,1,3,128]{5,3,4,2,1,0:T(1,128)S(1)}, s32[1,1,2,1,3,128]{5,3,4,2,1,0:T(1,128)}, u32[]{:S(2)}) copy-start(s32[1,1,2,1,3,128]{5,3,4,2,1,0:T(1,128)} %param.16) | copy-start | bytes 9220
  0.8 0.7 %copy-start.6 = (f32[8]{0:T(128)S(1)}, f32[8]{0:T(128)}, u32[]{:S(2)}) copy-start(f32[8]{0:T(128)} %param.14) | copy-start | bytes 100
  0.8 0.7 %copy-start.3 = (s32[1,1,256]{2,1,0:T(1,128)S(1)}, s32[1,1,256]{2,1,0:T(1,128)}, u32[]{:S(2)}) copy-start(s32[1,1,256]{2,1,0:T(1,128)} %param.12) | copy-start | bytes 3076
  0.8 0.7 %copy-start.5 = (f32[8]{0:T(128)S(1)}, f32[8]{0:T(128)}, u32[]{:S(2)}) copy-start(f32[8]{0:T(128)} %param.15) | copy-start | bytes 100
  1.6 0.7 %copy-start.4 = (s32[1,1,256]{2,1,0:T(1,128)S(1)}, s32[1,1,256]{2,1,0:T(1,128)}, u32[]{:S(2)}) copy-start(s32[1,1,256]{2,1,0:T(1,128)} %param.13) | copy-start | bytes 3076
  2.3 0.7 %copy-start.2 = (f32[1,1,2,256]{3,2,1,0:T(2,128)S(1)}, f32[1,1,2,256]{3,2,1,0:T(2,128)}, u32[]{:S(2)}) copy-start(f32[1,1,2,256]{3,2,1,0:T(2,128)} %param.11) | copy-start | bytes 6148
  4.9 6.8 %collective-permute-start = (f32[2,5,128]{2,0,1:T(2,128)S(1)}, f32[2,5,128]{2,0,1:T(2,128)S(1)}, u32[]{:S(2)}, u32[]{:S(2)}) collective-permute-start(f32[2,5,128]{2,0,1:T(2,128)S(1)} %get-tuple-element.7), channel_id=1, source_target_pairs={{0,4},{4,8},{8,12},{12,0},{1,5},{5,9},{9,13},{13,1},{2,6},{6,10},{... | collective-permute-start | bytes 15368 | tf_op jit(solution)/shard_map/ppermute | solution.py:207
  8.0 3.7 %collective-permute-start.1 = (f32[2,5,128]{2,0,1:T(2,128)S(1)}, f32[2,5,128]{2,0,1:T(2,128)S(1)}, u32[]{:S(2)}, u32[]{:S(2)}) collective-permute-start(f32[2,5,128]{2,0,1:T(2,128)S(1)} %get-tuple-element.8), channel_id=1, source_target_pairs={{4,0},{8,4},{12,8},{0,12},{5,1},{9,5},{13,9},{1,13},{6,2},{10,6},{... | collective-permute-start | bytes 15368 | tf_op jit(solution)/shard_map/ppermute | solution.py:204
  17.0 0.8 %copy-start = (f32[2,5,3,128]{1,3,2,0:T(8,128)}, f32[2,5,3,128]{1,3,2,0:T(8,128)S(1)}, u32[]{:S(2)}) copy-start(f32[2,5,3,128]{1,3,2,0:T(8,128)S(1)} %copy.45) | copy-start | bytes 46084

commit v2 on v1

--- a/solution.py
+++ b/solution.py
@@ -85,11 +85,11 @@
     pos_ref, rows_ref, cols_ref, a_ref, b_ref, prop_ref, spec_ref, out_ref, wave_ref, pot_ref,
     *, field_x
 ):
+    batch = wave_ref.shape[0]
     w = prop_ref.shape[-1]
     layers = pot_ref.shape[-1] // w
-    p = pl.program_id(0)
-    hop = pl.program_id(1)
-    layer = pl.program_id(2)
+    hop = pl.program_id(0)
+    layer = pl.program_id(1)
     f32, bf16 = jnp.float32, jnp.bfloat16
 
     def dot(a, b):
@@ -99,51 +99,56 @@
     def _():
         rows = dot(a_ref[...], spec_ref[...]).astype(bf16)
         rows = jnp.concatenate([rows[:w], rows[w:]], 1)
-        wave_ref[...] = dot(rows, b_ref[...]).astype(bf16)
+        start = dot(rows, b_ref[...]).astype(bf16)
+        for p in range(batch):
+            wave_ref[p] = start
 
     @pl.when(layer == 0)
     def _():
-        shift_x = pos_ref[p, 0].astype(f32)
-        shift_y = pos_ref[p, 1].astype(f32)
         atom_x = rows_ref[0, 0:1, :]
         inverse_row = rows_ref[0, 2:3, :]
-        pixel_col = lax.broadcasted_iota(jnp.int32, (w, 1), 0).astype(f32)
-        dist_x = wrap(atom_x - shift_x - pixel_col + 0.5 * field_x, field_x) - 0.5 * field_x
-        across = jnp.exp(-dist_x * dist_x * inverse_row).astype(bf16)
         atom_y = cols_ref[0, :, 1:2]
         inverse_col = cols_ref[0, :, 2:3]
+        pixel_col = lax.broadcasted_iota(jnp.int32, (w, 1), 0).astype(f32)
         pixel_row = lax.broadcasted_iota(jnp.int32, (1, w), 1).astype(f32)
-        dist_y = wrap(atom_y - shift_y - pixel_row + 0.5 * w, w) - 0.5 * w
-        along = jnp.exp(-dist_y * dist_y * inverse_col)
-        weighted = jnp.concatenate(
-            [(cols_ref[0, :, 3 + l : 4 + l] * along).astype(bf16) for l in range(layers)], 1
-        )
-        pot_ref[...] = dot(across, weighted)
-
-    psi = wave_ref[...]
-    wr = psi[:, :w].astype(f32)
-    wi = psi[:, w:].astype(f32)
-    v = pot_ref[:, pl.ds(pl.multiple_of(layer * w, w), w)]
-    cv = jnp.cos(v)
-    sv = jnp.sin(v)
-    tr = (wr * cv - wi * sv).astype(bf16)
-    ti = (wr * sv + wi * cv).astype(bf16)
-    rw = dot(jnp.concatenate([tr, ti], 1), a_ref[...]).astype(bf16)
-    sp = dot(b_ref[...], jnp.concatenate([rw[:, :w], rw[:, w:]], 0))
-    sr = sp[:w]
-    si = sp[w:]
+        for p in range(batch):
+            shift_x = pos_ref[p, 0].astype(f32)
+            shift_y = pos_ref[p, 1].astype(f32)
+            dist_x = wrap(atom_x - shift_x - pixel_col + 0.5 * field_x, field_x) - 0.5 * field_x
+            across = jnp.exp(-dist_x * dist_x * inverse_row).astype(bf16)
+            dist_y = wrap(atom_y - shift_y - pixel_row + 0.5 * w, w) - 0.5 * w
+            along = jnp.exp(-dist_y * dist_y * inverse_col)
+            weighted = jnp.concatenate(
+                [(cols_ref[0, :, 3 + l : 4 + l] * along).astype(bf16) for l in range(layers)], 1
+            )
+            pot_ref[p] = dot(across, weighted)
+
     pr = prop_ref[0]
     pi = prop_ref[1]
-    spb = jnp.concatenate(
-        [(sr * pr - si * pi).astype(bf16), (sr * pi + si * pr).astype(bf16)], 0
-    )
-    br = dot(a_ref[...], spb).astype(bf16)
-    psi = dot(jnp.concatenate([br[:w], br[w:]], 1), b_ref[...]).astype(bf16)
-    wave_ref[...] = psi
-
-    @pl.when((hop == pl.num_programs(1) - 1) & (layer == pl.num_programs(2) - 1))
+    column = pl.ds(pl.multiple_of(layer * w, w), w)
+    for p in range(batch):
+        psi = wave_ref[p]
+        wr = psi[:, :w].astype(f32)
+        wi = psi[:, w:].astype(f32)
+        v = pot_ref[p, :, column]
+        cv = jnp.cos(v)
+        sv = jnp.sin(v)
+        tr = (wr * cv - wi * sv).astype(bf16)
+        ti = (wr * sv + wi * cv).astype(bf16)
+        rw = dot(jnp.concatenate([tr, ti], 1), a_ref[...]).astype(bf16)
+        sp = dot(b_ref[...], jnp.concatenate([rw[:, :w], rw[:, w:]], 0))
+        sr = sp[:w]
+        si = sp[w:]
+        spb = jnp.concatenate(
+            [(sr * pr - si * pi).astype(bf16), (sr * pi + si * pr).astype(bf16)], 0
+        )
+        br = dot(a_ref[...], spb).astype(bf16)
+        psi = dot(jnp.concatenate([br[:w], br[w:]], 1), b_ref[...]).astype(bf16)
+        wave_ref[p] = psi
+
+    @pl.when((hop == pl.num_programs(0) - 1) & (layer == pl.num_programs(1) - 1))
     def _():
-        out_ref[0] = psi
+        out_ref[...] = wave_ref[...]
 
 
 def run_slices(probe_pos, rows, cols, window, layers, field_x):
@@ -153,7 +158,7 @@
     a, b = dft_blocks(w)
     prop = propagator(w)
     spec = start_spectrum(w)
-    full = lambda shape: pl.BlockSpec(shape, lambda p, h, l, pos: (0,) * len(shape))
+    full = lambda shape: pl.BlockSpec(shape, lambda h, l, pos: (0,) * len(shape))
     steps = batch * hops * layers
     flops = steps * 4 * 2 * w * (2 * w) * (2 * w) + batch * hops * 2 * w * atoms * layers * w
     return pl.pallas_call(
@@ -161,23 +166,23 @@
         out_shape=jax.ShapeDtypeStruct((batch, w, 2 * w), jnp.bfloat16),
         grid_spec=pltpu.PrefetchScalarGridSpec(
             num_scalar_prefetch=1,
-            grid=(batch, hops, layers),
+            grid=(hops, layers),
             in_specs=[
-                pl.BlockSpec((1, fields, atoms), lambda p, h, l, pos: (h, 0, 0)),
-                pl.BlockSpec((1, atoms, fields), lambda p, h, l, pos: (h, 0, 0)),
+                pl.BlockSpec((1, fields, atoms), lambda h, l, pos: (h, 0, 0)),
+                pl.BlockSpec((1, atoms, fields), lambda h, l, pos: (h, 0, 0)),
                 full((2 * w, 2 * w)),
                 full((2 * w, 2 * w)),
                 full((2, w, w)),
                 full((2 * w, w)),
             ],
-            out_specs=pl.BlockSpec((1, w, 2 * w), lambda p, h, l, pos: (p, 0, 0)),
+            out_specs=full((batch, w, 2 * w)),
             scratch_shapes=[
-                pltpu.VMEM((w, 2 * w), jnp.bfloat16),
-                pltpu.VMEM((w, layers * w), jnp.float32),
+                pltpu.VMEM((batch, w, 2 * w), jnp.bfloat16),
+                pltpu.VMEM((batch, w, layers * w), jnp.float32),
             ],
         ),
         compiler_params=pltpu.CompilerParams(
-            dimension_semantics=("arbitrary", "arbitrary", "arbitrary"),
+            dimension_semantics=("arbitrary", "arbitrary"),
         ),
         cost_estimate=pl.CostEstimate(
             flops=flops,

time: 44.2 us -> 41.9 us (0.948)
  Pallas kernels: 24.2 us -> 21.8 us
    pallas_call x1, Pallas kernels: 24.2 us -> 21.8 us  [run_slices(): pl.pallas_call(functools.partial(slices_kernel, field_x=float(field_x)),...]
where the time goes in v2:
time: 41.9 us; the launch traced here: 41.6 us
  Pallas kernels  21.8 us (52%)
  local copies, waits for them, and re-layouts  7.4 us (18%)
  starting transfers between devices  5.2 us (12%)
  blocking collectives  4.45 us (11%)
  waiting for transfers between devices  1.54 us (4%)
  other arithmetic  1.03 us (2%)
    pallas_call x1, Pallas kernels, run_slices(): pl.pallas_call(functools.partial(slices_kernel, field_x=float(field_x)),...  21.8 us
    all_gather x1, blocking collectives, shards(): gathered = lax.all_gather(local, 'slc', axis=0, tiled=False)  4.45 us
    ppermute x1, starting transfers between devices, shards(): lax.ppermute(picked[:, 2], 'lat', [(i, (i + 1) % n_lat) for i in range(n_...  3.1 us
    ppermute x1, starting transfers between devices, shards(): lax.ppermute(picked[:, 0], 'lat', [((i + 1) % n_lat, i) for i in range(n_...  2.09 us
    unnamed x14, local copies, waits for them, and re-layouts  2.03 us
    reshape x1, local copies, waits for them, and re-layouts, shards(): return wave.reshape(batch, window, 2, window)  1.96 us
    gather x2, local copies, waits for them, and re-layouts, pick_rows(): gathered = fields[:, safe_index]  1.72 us
    ppermute x1, waiting for transfers between devices, shards(): lax.ppermute(picked[:, 2], 'lat', [(i, (i + 1) % n_lat) for i in range(n_...  1.54 us
  transfers between devices with their start and end apart: 2, of which 1 were waited for; matrix products, arithmetic and copies ran while one was open for 0% of the time, Pallas kernels for 0%

profile of v2, /device:TPU:0, one launch (start us, length us, event | category | flops | bytes accessed | tf_op | source)
XLA Modules:
  0.0 41.6 jit_solution(674043986140394728)
XLA Ops:
  0.0 0.8 %compare_convert_fusion = f32[1,1,2,1,3,128]{5,3,4,2,1,0:T(1,128)S(1)} fusion(s32[1,1,2,1,3,128]{5,3,4,2,1,0:T(1,128)} %param.16), kind=kLoop, calls=%fused_computation.9 | loop fusion | flops 1536 | bytes 6144 | tf_op jit(solution)/shard_map/vmap(vmap())/convert_element_type | solution.py:74
  0.8 0.0 copy-start.3
  0.8 0.0 copy-start.5
  0.8 0.6 %copy-done.6 = f32[8]{0:T(128)S(1)} copy-done((f32[8]{0:T(128)S(1)}, f32[8]{0:T(128)}, u32[]{:S(2)}) %copy-start.6) | copy-done | bytes 56
  1.4 0.0 copy-done.3
  1.5 0.1 select_reduce_fusion.1
  1.6 0.0 copy-start.4
  1.6 0.7 %copy-done.4 = s32[1,1,256]{2,1,0:T(1,128)S(1)} copy-done((s32[1,1,256]{2,1,0:T(1,128)S(1)}, s32[1,1,256]{2,1,0:T(1,128)}, u32[]{:S(2)}) %copy-start.4) | copy-done | bytes 1048
  2.3 0.7 %copy-done.2 = f32[1,1,2,256]{3,2,1,0:T(2,128)S(1)} copy-done((f32[1,1,2,256]{3,2,1,0:T(2,128)S(1)}, f32[1,1,2,256]{3,2,1,0:T(2,128)}, u32[]{:S(2)}) %copy-start.2) | copy-done | bytes 2072
  3.0 0.1 copy.40
  3.1 1.6 %gather_fusion = f32[768,5]{1,0:T(8,128)S(1)} fusion(f32[5,256]{0,1:T(8,128)S(1)} %copy.40, s32[1024]{0:T(1024)S(1)} %pad_clamp_fusion.1), kind=kCustom, calls=%fused_computation | custom fusion | bytes 33792 | tf_op jit(solution)/shard_map/vmap(vmap())/gather | solution.py:76
  4.7 0.1 copy.41
  4.9 3.1 %collective-permute-start = (f32[2,5,128]{2,0,1:T(2,128)S(1)}, f32[2,5,128]{2,0,1:T(2,128)S(1)}, u32[]{:S(2)}, u32[]{:S(2)}) collective-permute-start(f32[2,5,128]{2,0,1:T(2,128)S(1)} %get-tuple-element.7), channel_id=1, source_target_pairs={{0,4},{4,8},{8,12},{12,0},{1,5},{5,9},{9,13},{13,1},{2,6},{6,10},{... | collective-permute-start | bytes 15368 | tf_op jit(solution)/shard_map/ppermute | solution.py:212
  8.0 2.1 %collective-permute-start.1 = (f32[2,5,128]{2,0,1:T(2,128)S(1)}, f32[2,5,128]{2,0,1:T(2,128)S(1)}, u32[]{:S(2)}, u32[]{:S(2)}) collective-permute-start(f32[2,5,128]{2,0,1:T(2,128)S(1)} %get-tuple-element.8), channel_id=1, source_target_pairs={{4,0},{8,4},{12,8},{0,12},{5,1},{9,5},{13,9},{1,13},{6,2},{10,6},{... | collective-permute-start | bytes 15368 | tf_op jit(solution)/shard_map/ppermute | solution.py:209
  10.1 1.5 %collective-permute-done = f32[2,5,128]{2,0,1:T(2,128)S(1)} collective-permute-done((f32[2,5,128]{2,0,1:T(2,128)S(1)}, f32[2,5,128]{2,0,1:T(2,128)S(1)}, u32[]{:S(2)}, u32[]{:S(2)}) %collective-permute-start) | collective-permute-done | bytes 5152 | tf_op jit(solution)/shard_map/ppermute | solution.py:212
  11.7 0.0 collective-permute-done.1
  11.7 4.5 %all-gather = f32[4,3,5,128]{3,1,2,0:T(4,128)S(1)} all-gather(f32[2,3,5,128]{3,1,2,0:T(4,128)S(1)} %copy.43), channel_id=2, replica_groups=mesh['groups'=2,'lat'=4,'slc'=2,'rep'=2] {'slc'}, dimensions={0}, use_global_device_ids=true | all-gather | bytes 46080 | tf_op jit(solution)/shard_map/all_gather | solution.py:216
  16.1 0.6 %gather_fusion.1 = f32[2,3,5,128]{3,1,2,0:T(4,128)S(1)} fusion(f32[2,3,5,128]{3,1,2,0:T(4,128)S(1)} %dynamic-slice_bitcast_fusion, s32[1024]{0:T(1024)S(1)} %pad_clamp_fusion), kind=kCustom, calls=%fused_computation.1 | custom fusion | bytes 30728 | tf_op jit(solution)/shard_map/jit(_take)/gather | solution.py:220
  16.7 0.1 select_bitcast_fusion
  16.8 0.2 copy.45
  17.0 0.0 copy-start
  17.0 0.8 %copy.46.rows_ref = f32[2,5,384]{2,1,0:T(8,128)} copy(f32[2,5,384]{1,2,0:T(8,128)S(1)} %bitcast.27) | data formatting | bytes 30720 | tf_op jit(solution)/shard_map/reshape | solution.py:221
  17.8 21.8 %shard_map.109 = bf16[2,256,512]{2,1,0:T(8,128)(2,1)} custom-call(s32[2,2]{1,0:T(2,128)} %pos_ref.1, f32[2,5,384]{2,1,0:T(8,128)} %copy.46.rows_ref, f32[2,384,5]{2,1,0:T(8,128)} %bitcast.28, bf16[512,512]{1,0:T(8,128)(2,1)} %constant.56.clone.a_ref, bf16[512,512]{1,0:T(8,128)(2,1)} %constant.57.clone.b_ref, f32[2,256,256]{2,1,0:T(8,128)} %constant.58.clone.prop_ref, ...), custom_call_target="tpu_custom_call" | custom-call | flops 4697620480 | bytes 2359296 | tf_op jit(solution)/shard_map/pallas_call | solution.py:164
  39.6 2.0 %reshape.101 = bf16[2,256,2,256]{3,2,1,0:T(2,128)(2,1)} reshape(bf16[2,256,512]{2,1,0:T(8,128)(2,1)} %shard_map.109) | data formatting | bytes 1048576 | tf_op jit(solution)/shard_map/reshape | solution.py:225
  (22 shorter events, 0.1 us)
Async XLA Ops:
  0.0 0.8 %copy-start.1 = (s32[1,1,2,1,3,128]{5,3,4,2,1,0:T(1,128)S(1)}, s32[1,1,2,1,3,128]{5,3,4,2,1,0:T(1,128)}, u32[]{:S(2)}) copy-start(s32[1,1,2,1,3,128]{5,3,4,2,1,0:T(1,128)} %param.16) | copy-start | bytes 9220
  0.8 0.7 %copy-start.6 = (f32[8]{0:T(128)S(1)}, f32[8]{0:T(128)}, u32[]{:S(2)}) copy-start(f32[8]{0:T(128)} %param.14) | copy-start | bytes 100
  0.8 0.7 %copy-start.3 = (s32[1,1,256]{2,1,0:T(1,128)S(1)}, s32[1,1,256]{2,1,0:T(1,128)}, u32[]{:S(2)}) copy-start(s32[1,1,256]{2,1,0:T(1,128)} %param.12) | copy-start | bytes 3076
  0.8 0.7 %copy-start.5 = (f32[8]{0:T(128)S(1)}, f32[8]{0:T(128)}, u32[]{:S(2)}) copy-start(f32[8]{0:T(128)} %param.15) | copy-start | bytes 100
  1.6 0.7 %copy-start.4 = (s32[1,1,256]{2,1,0:T(1,128)S(1)}, s32[1,1,256]{2,1,0:T(1,128)}, u32[]{:S(2)}) copy-start(s32[1,1,256]{2,1,0:T(1,128)} %param.13) | copy-start | bytes 3076
  2.3 0.7 %copy-start.2 = (f32[1,1,2,256]{3,2,1,0:T(2,128)S(1)}, f32[1,1,2,256]{3,2,1,0:T(2,128)}, u32[]{:S(2)}) copy-start(f32[1,1,2,256]{3,2,1,0:T(2,128)} %param.11) | copy-start | bytes 6148
  4.9 6.8 %collective-permute-start = (f32[2,5,128]{2,0,1:T(2,128)S(1)}, f32[2,5,128]{2,0,1:T(2,128)S(1)}, u32[]{:S(2)}, u32[]{:S(2)}) collective-permute-start(f32[2,5,128]{2,0,1:T(2,128)S(1)} %get-tuple-element.7), channel_id=1, source_target_pairs={{0,4},{4,8},{8,12},{12,0},{1,5},{5,9},{9,13},{13,1},{2,6},{6,10},{... | collective-permute-start | bytes 15368 | tf_op jit(solution)/shard_map/ppermute | solution.py:212
  8.0 3.7 %collective-permute-start.1 = (f32[2,5,128]{2,0,1:T(2,128)S(1)}, f32[2,5,128]{2,0,1:T(2,128)S(1)}, u32[]{:S(2)}, u32[]{:S(2)}) collective-permute-start(f32[2,5,128]{2,0,1:T(2,128)S(1)} %get-tuple-element.8), channel_id=1, source_target_pairs={{4,0},{8,4},{12,8},{0,12},{5,1},{9,5},{13,9},{1,13},{6,2},{10,6},{... | collective-permute-start | bytes 15368 | tf_op jit(solution)/shard_map/ppermute | solution.py:209
  17.0 0.8 %copy-start = (f32[2,5,3,128]{1,3,2,0:T(8,128)}, f32[2,5,3,128]{1,3,2,0:T(8,128)S(1)}, u32[]{:S(2)}) copy-start(f32[2,5,3,128]{1,3,2,0:T(8,128)S(1)} %copy.45) | copy-start | bytes 46084

commit v3 on v2

--- a/solution.py
+++ b/solution.py
@@ -79,6 +79,23 @@
 
 def wrap(value, period):
     return value - period * jnp.floor(value * (1.0 / period))
+
+
+def sincos(v):
+    q = jnp.floor(v * 0.6366197723675814 + 0.5)
+    r = v - q * 1.5703125
+    r = r - q * 4.837512969970703125e-4
+    r = r - q * 7.549789954891882e-8
+    z = r * r
+    s = r + r * z * (-1.6666654611e-1 + z * (8.3321608736e-3 + z * -1.9515295891e-4))
+    c = 1.0 - 0.5 * z + z * z * (4.166664568298827e-2 + z * (-1.388731625493765e-3 + z * 2.443315711809948e-5))
+    n = q.astype(jnp.int32)
+    swap = (n & 1) == 1
+    sin_v = jnp.where(swap, c, s)
+    cos_v = jnp.where(swap, s, c)
+    sin_v = jnp.where((n & 2) == 2, -sin_v, sin_v)
+    cos_v = jnp.where(((n + 1) & 2) == 2, -cos_v, cos_v)
+    return sin_v, cos_v
 
 
 def slices_kernel(
@@ -131,8 +148,7 @@
         wr = psi[:, :w].astype(f32)
         wi = psi[:, w:].astype(f32)
         v = pot_ref[p, :, column]
-        cv = jnp.cos(v)
-        sv = jnp.sin(v)
+        sv, cv = sincos(v)
         tr = (wr * cv - wi * sv).astype(bf16)
         ti = (wr * sv + wi * cv).astype(bf16)
         rw = dot(jnp.concatenate([tr, ti], 1), a_ref[...]).astype(bf16)

time: 41.9 us -> 37.4 us (0.89)
  Pallas kernels: 21.8 us -> 17.4 us
    pallas_call x1, Pallas kernels: 21.8 us -> 17.4 us  [run_slices(): pl.pallas_call(functools.partial(slices_kernel, field_x=float(field_x)),...]
where the time goes in v3:
time: 37.4 us; the launch traced here: 37.1 us
  Pallas kernels  17.4 us (47%)
  local copies, waits for them, and re-layouts  7.4 us (20%)
  starting transfers between devices  5.2 us (14%)
  blocking collectives  4.45 us (12%)
  waiting for transfers between devices  1.54 us (4%)
  other arithmetic  1.03 us (3%)
    pallas_call x1, Pallas kernels, run_slices(): pl.pallas_call(functools.partial(slices_kernel, field_x=float(field_x)),...  17.4 us
    all_gather x1, blocking collectives, shards(): gathered = lax.all_gather(local, 'slc', axis=0, tiled=False)  4.45 us
    ppermute x1, starting transfers between devices, shards(): lax.ppermute(picked[:, 2], 'lat', [(i, (i + 1) % n_lat) for i in range(n_...  3.1 us
    ppermute x1, starting transfers between devices, shards(): lax.ppermute(picked[:, 0], 'lat', [((i + 1) % n_lat, i) for i in range(n_...  2.09 us
    unnamed x14, local copies, waits for them, and re-layouts  2.03 us
    reshape x1, local copies, waits for them, and re-layouts, shards(): return wave.reshape(batch, window, 2, window)  1.96 us
    gather x2, local copies, waits for them, and re-layouts, pick_rows(): gathered = fields[:, safe_index]  1.72 us
    ppermute x1, waiting for transfers between devices, shards(): lax.ppermute(picked[:, 2], 'lat', [(i, (i + 1) % n_lat) for i in range(n_...  1.54 us
  transfers between devices with their start and end apart: 2, of which 1 were waited for; matrix products, arithmetic and copies ran while one was open for 0% of the time, Pallas kernels for 0%

profile of v3, /device:TPU:0, one launch (start us, length us, event | category | flops | bytes accessed | tf_op | source)
XLA Modules:
  0.0 37.1 jit_solution(15187948969611523517)
XLA Ops:
  0.0 0.8 %compare_convert_fusion = f32[1,1,2,1,3,128]{5,3,4,2,1,0:T(1,128)S(1)} fusion(s32[1,1,2,1,3,128]{5,3,4,2,1,0:T(1,128)} %param.16), kind=kLoop, calls=%fused_computation.9 | loop fusion | flops 1536 | bytes 6144 | tf_op jit(solution)/shard_map/vmap(vmap())/convert_element_type | solution.py:74
  0.8 0.0 copy-start.3
  0.8 0.0 copy-start.5
  0.8 0.6 %copy-done.6 = f32[8]{0:T(128)S(1)} copy-done((f32[8]{0:T(128)S(1)}, f32[8]{0:T(128)}, u32[]{:S(2)}) %copy-start.6) | copy-done | bytes 56
  1.4 0.0 copy-done.3
  1.5 0.1 select_reduce_fusion.1
  1.6 0.0 copy-start.4
  1.6 0.7 %copy-done.4 = s32[1,1,256]{2,1,0:T(1,128)S(1)} copy-done((s32[1,1,256]{2,1,0:T(1,128)S(1)}, s32[1,1,256]{2,1,0:T(1,128)}, u32[]{:S(2)}) %copy-start.4) | copy-done | bytes 1048
  2.3 0.7 %copy-done.2 = f32[1,1,2,256]{3,2,1,0:T(2,128)S(1)} copy-done((f32[1,1,2,256]{3,2,1,0:T(2,128)S(1)}, f32[1,1,2,256]{3,2,1,0:T(2,128)}, u32[]{:S(2)}) %copy-start.2) | copy-done | bytes 2072
  3.0 0.1 copy.40
  3.1 1.6 %gather_fusion = f32[768,5]{1,0:T(8,128)S(1)} fusion(f32[5,256]{0,1:T(8,128)S(1)} %copy.40, s32[1024]{0:T(1024)S(1)} %pad_clamp_fusion.1), kind=kCustom, calls=%fused_computation | custom fusion | bytes 33792 | tf_op jit(solution)/shard_map/vmap(vmap())/gather | solution.py:76
  4.7 0.1 copy.41
  4.9 3.1 %collective-permute-start = (f32[2,5,128]{2,0,1:T(2,128)S(1)}, f32[2,5,128]{2,0,1:T(2,128)S(1)}, u32[]{:S(2)}, u32[]{:S(2)}) collective-permute-start(f32[2,5,128]{2,0,1:T(2,128)S(1)} %get-tuple-element.7), channel_id=1, source_target_pairs={{0,4},{4,8},{8,12},{12,0},{1,5},{5,9},{9,13},{13,1},{2,6},{6,10},{... | collective-permute-start | bytes 15368 | tf_op jit(solution)/shard_map/ppermute | solution.py:228
  8.0 2.1 %collective-permute-start.1 = (f32[2,5,128]{2,0,1:T(2,128)S(1)}, f32[2,5,128]{2,0,1:T(2,128)S(1)}, u32[]{:S(2)}, u32[]{:S(2)}) collective-permute-start(f32[2,5,128]{2,0,1:T(2,128)S(1)} %get-tuple-element.8), channel_id=1, source_target_pairs={{4,0},{8,4},{12,8},{0,12},{5,1},{9,5},{13,9},{1,13},{6,2},{10,6},{... | collective-permute-start | bytes 15368 | tf_op jit(solution)/shard_map/ppermute | solution.py:225
  10.1 1.5 %collective-permute-done = f32[2,5,128]{2,0,1:T(2,128)S(1)} collective-permute-done((f32[2,5,128]{2,0,1:T(2,128)S(1)}, f32[2,5,128]{2,0,1:T(2,128)S(1)}, u32[]{:S(2)}, u32[]{:S(2)}) %collective-permute-start) | collective-permute-done | bytes 5152 | tf_op jit(solution)/shard_map/ppermute | solution.py:228
  11.7 0.0 collective-permute-done.1
  11.7 4.5 %all-gather = f32[4,3,5,128]{3,1,2,0:T(4,128)S(1)} all-gather(f32[2,3,5,128]{3,1,2,0:T(4,128)S(1)} %copy.43), channel_id=2, replica_groups=mesh['groups'=2,'lat'=4,'slc'=2,'rep'=2] {'slc'}, dimensions={0}, use_global_device_ids=true | all-gather | bytes 46080 | tf_op jit(solution)/shard_map/all_gather | solution.py:232
  16.1 0.6 %gather_fusion.1 = f32[2,3,5,128]{3,1,2,0:T(4,128)S(1)} fusion(f32[2,3,5,128]{3,1,2,0:T(4,128)S(1)} %dynamic-slice_bitcast_fusion, s32[1024]{0:T(1024)S(1)} %pad_clamp_fusion), kind=kCustom, calls=%fused_computation.1 | custom fusion | bytes 30728 | tf_op jit(solution)/shard_map/jit(_take)/gather | solution.py:236
  16.7 0.1 select_bitcast_fusion
  16.8 0.2 copy.45
  17.0 0.0 copy-start
  17.0 0.8 %copy.46.rows_ref = f32[2,5,384]{2,1,0:T(8,128)} copy(f32[2,5,384]{1,2,0:T(8,128)S(1)} %bitcast.27) | data formatting | bytes 30720 | tf_op jit(solution)/shard_map/reshape | solution.py:237
  17.8 17.4 %shard_map.109 = bf16[2,256,512]{2,1,0:T(8,128)(2,1)} custom-call(s32[2,2]{1,0:T(2,128)} %pos_ref.1, f32[2,5,384]{2,1,0:T(8,128)} %copy.46.rows_ref, f32[2,384,5]{2,1,0:T(8,128)} %bitcast.28, bf16[512,512]{1,0:T(8,128)(2,1)} %constant.56.clone.a_ref, bf16[512,512]{1,0:T(8,128)(2,1)} %constant.57.clone.b_ref, f32[2,256,256]{2,1,0:T(8,128)} %constant.58.clone.prop_ref, ...), custom_call_target="tpu_custom_call" | custom-call | flops 4697620480 | bytes 2359296 | tf_op jit(solution)/shard_map/pallas_call | solution.py:180
  35.1 2.0 %reshape.101 = bf16[2,256,2,256]{3,2,1,0:T(2,128)(2,1)} reshape(bf16[2,256,512]{2,1,0:T(8,128)(2,1)} %shard_map.109) | data formatting | bytes 1048576 | tf_op jit(solution)/shard_map/reshape | solution.py:241
  (22 shorter events, 0.1 us)
Async XLA Ops:
  0.0 0.8 %copy-start.1 = (s32[1,1,2,1,3,128]{5,3,4,2,1,0:T(1,128)S(1)}, s32[1,1,2,1,3,128]{5,3,4,2,1,0:T(1,128)}, u32[]{:S(2)}) copy-start(s32[1,1,2,1,3,128]{5,3,4,2,1,0:T(1,128)} %param.16) | copy-start | bytes 9220
  0.8 0.7 %copy-start.6 = (f32[8]{0:T(128)S(1)}, f32[8]{0:T(128)}, u32[]{:S(2)}) copy-start(f32[8]{0:T(128)} %param.14) | copy-start | bytes 100
  0.8 0.7 %copy-start.3 = (s32[1,1,256]{2,1,0:T(1,128)S(1)}, s32[1,1,256]{2,1,0:T(1,128)}, u32[]{:S(2)}) copy-start(s32[1,1,256]{2,1,0:T(1,128)} %param.12) | copy-start | bytes 3076
  0.8 0.7 %copy-start.5 = (f32[8]{0:T(128)S(1)}, f32[8]{0:T(128)}, u32[]{:S(2)}) copy-start(f32[8]{0:T(128)} %param.15) | copy-start | bytes 100
  1.6 0.7 %copy-start.4 = (s32[1,1,256]{2,1,0:T(1,128)S(1)}, s32[1,1,256]{2,1,0:T(1,128)}, u32[]{:S(2)}) copy-start(s32[1,1,256]{2,1,0:T(1,128)} %param.13) | copy-start | bytes 3076
  2.3 0.7 %copy-start.2 = (f32[1,1,2,256]{3,2,1,0:T(2,128)S(1)}, f32[1,1,2,256]{3,2,1,0:T(2,128)}, u32[]{:S(2)}) copy-start(f32[1,1,2,256]{3,2,1,0:T(2,128)} %param.11) | copy-start | bytes 6148
  4.9 6.8 %collective-permute-start = (f32[2,5,128]{2,0,1:T(2,128)S(1)}, f32[2,5,128]{2,0,1:T(2,128)S(1)}, u32[]{:S(2)}, u32[]{:S(2)}) collective-permute-start(f32[2,5,128]{2,0,1:T(2,128)S(1)} %get-tuple-element.7), channel_id=1, source_target_pairs={{0,4},{4,8},{8,12},{12,0},{1,5},{5,9},{9,13},{13,1},{2,6},{6,10},{... | collective-permute-start | bytes 15368 | tf_op jit(solution)/shard_map/ppermute | solution.py:228
  8.0 3.7 %collective-permute-start.1 = (f32[2,5,128]{2,0,1:T(2,128)S(1)}, f32[2,5,128]{2,0,1:T(2,128)S(1)}, u32[]{:S(2)}, u32[]{:S(2)}) collective-permute-start(f32[2,5,128]{2,0,1:T(2,128)S(1)} %get-tuple-element.8), channel_id=1, source_target_pairs={{4,0},{8,4},{12,8},{0,12},{5,1},{9,5},{13,9},{1,13},{6,2},{10,6},{... | collective-permute-start | bytes 15368 | tf_op jit(solution)/shard_map/ppermute | solution.py:225
  17.0 0.8 %copy-start = (f32[2,5,3,128]{1,3,2,0:T(8,128)}, f32[2,5,3,128]{1,3,2,0:T(8,128)S(1)}, u32[]{:S(2)}) copy-start(f32[2,5,3,128]{1,3,2,0:T(8,128)S(1)} %copy.45) | copy-start | bytes 46084

commit v4 on v3

--- a/solution.py
+++ b/solution.py
@@ -98,10 +98,11 @@
     return sin_v, cos_v
 
 
-def slices_kernel(
-    pos_ref, rows_ref, cols_ref, a_ref, b_ref, prop_ref, spec_ref, out_ref, wave_ref, pot_ref,
-    *, field_x
-):
+def slices_kernel(*refs, field_x, carried):
+    if carried:
+        pos_ref, rows_ref, cols_ref, a_ref, b_ref, prop_ref, start_ref, out_ref, wave_ref, pot_ref = refs
+    else:
+        pos_ref, rows_ref, cols_ref, a_ref, b_ref, prop_ref, spec_ref, out_ref, wave_ref, pot_ref = refs
     batch = wave_ref.shape[0]
     w = prop_ref.shape[-1]
     layers = pot_ref.shape[-1] // w
@@ -114,11 +115,14 @@
 
     @pl.when((hop == 0) & (layer == 0))
     def _():
-        rows = dot(a_ref[...], spec_ref[...]).astype(bf16)
-        rows = jnp.concatenate([rows[:w], rows[w:]], 1)
-        start = dot(rows, b_ref[...]).astype(bf16)
-        for p in range(batch):
-            wave_ref[p] = start
+        if carried:
+            wave_ref[...] = start_ref[...]
+        else:
+            rows = dot(a_ref[...], spec_ref[...]).astype(bf16)
+            rows = jnp.concatenate([rows[:w], rows[w:]], 1)
+            start = dot(rows, b_ref[...]).astype(bf16)
+            for p in range(batch):
+                wave_ref[p] = start
 
     @pl.when(layer == 0)
     def _():
@@ -167,18 +171,21 @@
         out_ref[...] = wave_ref[...]
 
 
-def run_slices(probe_pos, rows, cols, window, layers, field_x):
+def run_slices(probe_pos, rows, window, layers, field_x, wave=None):
     batch = probe_pos.shape[0]
     hops, fields, atoms = rows.shape
+    cols = jnp.transpose(rows, (0, 2, 1))
     w = window
     a, b = dft_blocks(w)
     prop = propagator(w)
-    spec = start_spectrum(w)
     full = lambda shape: pl.BlockSpec(shape, lambda h, l, pos: (0,) * len(shape))
+    carried = wave is not None
+    last = wave if carried else jnp.asarray(start_spectrum(w))
+    last_spec = full((batch, w, 2 * w)) if carried else full((2 * w, w))
     steps = batch * hops * layers
     flops = steps * 4 * 2 * w * (2 * w) * (2 * w) + batch * hops * 2 * w * atoms * layers * w
     return pl.pallas_call(
-        functools.partial(slices_kernel, field_x=float(field_x)),
+        functools.partial(slices_kernel, field_x=float(field_x), carried=carried),
         out_shape=jax.ShapeDtypeStruct((batch, w, 2 * w), jnp.bfloat16),
         grid_spec=pltpu.PrefetchScalarGridSpec(
             num_scalar_prefetch=1,
@@ -189,7 +196,7 @@
                 full((2 * w, 2 * w)),
                 full((2 * w, 2 * w)),
                 full((2, w, w)),
-                full((2 * w, w)),
+                last_spec,
             ],
             out_specs=full((batch, w, 2 * w)),
             scratch_shapes=[
@@ -205,7 +212,7 @@
             transcendentals=steps * 2 * w * w + batch * hops * 2 * atoms * w,
             bytes_accessed=2 * (2 * w) ** 2 * 2 + 3 * w * w * 4 + batch * w * w * 4,
         ),
-    )(probe_pos, rows, cols, jnp.asarray(a), jnp.asarray(b), jnp.asarray(prop), jnp.asarray(spec))
+    )(probe_pos, rows, cols, jnp.asarray(a), jnp.asarray(b), jnp.asarray(prop), last)
 
 
 def shards(atom_xy, atom_species, atom_slab, species_amp, species_spread, margin, probe_pos):
@@ -216,28 +223,46 @@
     n_lat = lax.axis_size("lat")
     owners = lax.axis_size("slc")
     field_x = n_lat * atoms * (2 * window // cap)
-    fields = atom_fields(
-        atom_xy[0, 0], atom_species[0, 0], atom_slab[0, 0], species_amp, species_spread, layers
-    )
-    field_count = fields.shape[0]
-    pick_table = margin[0, 0, :, 0]
-    picked = jax.vmap(jax.vmap(lambda lst: pick_rows(fields, lst)))(pick_table)
-    to_left = lax.ppermute(
-        picked[:, 0], "lat", [((i + 1) % n_lat, i) for i in range(n_lat)]
-    )
-    to_right = lax.ppermute(
-        picked[:, 2], "lat", [(i, (i + 1) % n_lat) for i in range(n_lat)]
-    )
-    local = jnp.stack([to_right, picked[:, 1], to_left], 1)
-    gathered = lax.all_gather(local, "slc", axis=0, tiled=False)
+    f32 = jnp.float32
+    raw = jnp.concatenate(
+        [atom_xy[0, 0], atom_species[0, 0][None].astype(f32), atom_slab[0, 0][None].astype(f32)], 0
+    )
+    marg = margin[0, 0, :, 0].astype(f32)
+    size = raw.size
+
+    def pack(o):
+        return jnp.concatenate([raw.reshape(-1), marg[:, o].reshape(-1)])
+
+    from_left = lax.ppermute(pack(2), "lat", [(i, (i + 1) % n_lat) for i in range(n_lat)])
+    from_right = lax.ppermute(pack(0), "lat", [((i + 1) % n_lat, i) for i in range(n_lat)])
+
+    def unpack(packed):
+        return packed[:size].reshape(raw.shape), packed[size:].reshape(marg.shape[0], cap)
+
+    left_raw, left_marg = unpack(from_left)
+    right_raw, right_marg = unpack(from_right)
+    raws = jnp.stack([left_raw, raw, right_raw], 0)
+    margs = jnp.stack([left_marg, marg[:, 1], right_marg], 0).astype(jnp.int32)
+    fields = jax.vmap(
+        lambda r: atom_fields(
+            r[:2], r[2].astype(jnp.int32), r[3].astype(jnp.int32), species_amp, species_spread, layers
+        )
+    )(raws)
+    picked = jax.vmap(lambda f, m: jax.vmap(lambda lst: pick_rows(f, lst))(m))(fields, margs)
+    field_count = picked.shape[2]
+    rows_all = jnp.transpose(picked, (1, 2, 0, 3)).reshape(-1, field_count, 3 * cap)
     me = lax.axis_index("slc")
-    mine = lax.dynamic_index_in_dim(gathered, me, 1, keepdims=False)
-    hop_owner = (me + jnp.arange(owners)) % owners
-    rows = jnp.take(mine, hop_owner, axis=0)
-    rows = jnp.transpose(rows, (0, 2, 1, 3)).reshape(owners, field_count, 3 * cap)
-    cols = jnp.transpose(rows, (0, 2, 1))
+    first = lax.dynamic_index_in_dim(rows_all, me, 0, keepdims=True)
+    later = []
+    for hop in range(1, owners):
+        outgoing = lax.dynamic_index_in_dim(rows_all, (me - hop) % owners, 0, keepdims=True)
+        later.append(
+            lax.ppermute(outgoing, "slc", [(i, (i - hop) % owners) for i in range(owners)])
+        )
     batch = probe_pos.shape[0]
-    wave = run_slices(probe_pos, rows, cols, window, layers, field_x)
+    wave = run_slices(probe_pos, first, window, layers, field_x)
+    if later:
+        wave = run_slices(probe_pos, jnp.concatenate(later, 0), window, layers, field_x, wave)
     return wave.reshape(batch, window, 2, window)
 
 

time: 37.4 us -> 43.5 us (1.16)
  local copies, waits for them, and re-layouts: 7.4 us -> 12.5 us
  blocking collectives: 4.45 us -> 0 us
  Pallas kernels: 17.4 us -> 20.5 us
  starting transfers between devices: 5.2 us -> 6.82 us
    all_gather x1 -> x0, blocking collectives: 4.45 us -> none  [shards(): gathered = lax.all_gather(local, 'slc', axis=0, tiled=False)]
    gather x2 -> x3, local copies, waits for them, and re-layouts: 1.72 us -> 5.28 us  [pick_rows(): gathered = fields[:, safe_index]]
    pallas_call x1 -> x2, Pallas kernels: 17.4 us -> 20.5 us  [run_slices(): pl.pallas_call(functools.partial(slices_kernel, field_x=float(field_x), c...]
    ppermute x2 -> x3, starting transfers between devices: 5.2 us -> 6.82 us  [the longest x1 3.1 us: shards(): lax.ppermute(pack(2), 'lat', [(i, (i + 1) % n_lat) for i in range(n_lat)])]
    slice x0 -> x7, local copies, waits for them, and re-layouts: none -> 0.86 us  [the longest x3 0.85 us: shards(): r[:2]]
    reshape x1 -> x0, local copies, waits for them, and re-layouts: 0.77 us -> none  [shards(): jnp.transpose(rows, (0, 2, 1, 3)).reshape(owners, field_count, 3 * cap)]
    convert_element_type x1, other arithmetic: 0.76 us -> 0.02 us  [pick_rows(): valid_mask = (pick_list >= 0).astype(fields.dtype)]
    dynamic_slice x0 -> x2, local copies, waits for them, and re-layouts: none -> 0.74 us  [shards(): first = lax.dynamic_index_in_dim(rows_all, me, 0, keepdims=True)]
  transfers between devices with their start and end apart: 2 -> 3, of which waited for: 1 -> 1; matrix products, arithmetic and copies ran while one was open for 0% -> 0% of each run, Pallas kernels for 0% -> 24%
where the time goes in v4:
time: 43.5 us; the launch traced here: 43.1 us
  Pallas kernels  20.5 us (47%)
  local copies, waits for them, and re-layouts  12.5 us (29%)
  starting transfers between devices  6.82 us (16%)
  waiting for transfers between devices  1.65 us (4%)
  other arithmetic  1.41 us (3%)
    pallas_call x2, Pallas kernels, run_slices(): pl.pallas_call(functools.partial(slices_kernel, field_x=float(field_x), c...  20.5 us
    gather x3, local copies, waits for them, and re-layouts, pick_rows(): gathered = fields[:, safe_index]  5.28 us
    ppermute x1, starting transfers between devices, shards(): lax.ppermute(pack(2), 'lat', [(i, (i + 1) % n_lat) for i in range(n_lat)])  3.1 us
    unnamed x19, local copies, waits for them, and re-layouts  2.58 us
    ppermute x1, starting transfers between devices, shards(): lax.ppermute(pack(0), 'lat', [((i + 1) % n_lat, i) for i in range(n_lat)])  2.09 us
    reshape x1, local copies, waits for them, and re-layouts, shards(): return wave.reshape(batch, window, 2, window)  1.96 us
    ppermute x1, waiting for transfers between devices, shards(): lax.ppermute(pack(2), 'lat', [(i, (i + 1) % n_lat) for i in range(n_lat)])  1.65 us
    ppermute x1, starting transfers between devices, shards(): lax.ppermute(outgoing, 'slc', [(i, (i - hop) % owners) for i in range(own...  1.62 us
  transfers between devices with their start and end apart: 3, of which 1 were waited for; matrix products, arithmetic and copies ran while one was open for 0% of the time, Pallas kernels for 24%

profile of v4, /device:TPU:0, one launch (start us, length us, event | category | flops | bytes accessed | tf_op | source)
XLA Modules:
  0.0 43.1 jit_solution(6276832391527289388)
XLA Ops:
  0.0 0.7 %convert_element_type.71 = f32[1,1,2,1,3,128]{5,3,4,2,1,0:T(1,128)S(1)} convert(s32[1,1,2,1,3,128]{5,3,4,2,1,0:T(1,128)} %param.19) | non-fusion elementwise | flops 768 | bytes 6144 | tf_op jit(solution)/shard_map/convert_element_type | solution.py:230
  0.7 0.7 %copy-done.4 = s32[1,1,256]{2,1,0:T(1,128)S(1)} copy-done((s32[1,1,256]{2,1,0:T(1,128)S(1)}, s32[1,1,256]{2,1,0:T(1,128)}, u32[]{:S(2)}) %copy-start.4) | copy-done | bytes 1048
  1.4 0.0 copy-done.5
  1.4 0.7 %copy-done.3 = f32[1,1,2,256]{3,2,1,0:T(2,128)S(1)} copy-done((f32[1,1,2,256]{3,2,1,0:T(2,128)S(1)}, f32[1,1,2,256]{3,2,1,0:T(2,128)}, u32[]{:S(2)}) %copy-start.3) | copy-done | bytes 2072
  2.1 3.1 %collective-permute-start = (f32[1280]{0:T(1024)S(1)}, f32[1280]{0:T(1024)S(1)}, u32[]{:S(2)}, u32[]{:S(2)}) collective-permute-start(f32[1280]{0:T(1024)S(1)} %get-tuple-element.15), channel_id=1, source_target_pairs={{0,4},{4,8},{8,12},{12,0},{1,5},{5,9},{9,13},{13,1},{2,6},{6,10},{... | collective-permute-start | bytes 15368 | tf_op jit(solution)/shard_map/ppermute | solution.py:236
  5.2 2.1 %collective-permute-start.1 = (f32[1280]{0:T(1024)S(1)}, f32[1280]{0:T(1024)S(1)}, u32[]{:S(2)}, u32[]{:S(2)}) collective-permute-start(f32[1280]{0:T(1024)S(1)} %get-tuple-element.16), channel_id=1, source_target_pairs={{4,0},{8,4},{12,8},{0,12},{5,1},{9,5},{13,9},{1,13},{6,2},{10,6},{... | collective-permute-start | bytes 15368 | tf_op jit(solution)/shard_map/ppermute | solution.py:237
  7.3 1.6 %collective-permute-done = f32[1280]{0:T(1024)S(1)} collective-permute-done((f32[1280]{0:T(1024)S(1)}, f32[1280]{0:T(1024)S(1)}, u32[]{:S(2)}, u32[]{:S(2)}) %collective-permute-start) | collective-permute-done | bytes 5152 | tf_op jit(solution)/shard_map/ppermute | solution.py:236
  9.1 0.5 %copy-done.2 = f32[3,4,256]{2,1,0:T(4,128)} copy-done((f32[3,4,256]{2,1,0:T(4,128)}, f32[3,4,256]{2,1,0:T(4,128)S(1)}, u32[]{:S(2)}) %copy-start.2) | copy-done | bytes 12312
  9.6 0.6 %copy-done.6 = f32[8]{0:T(128)S(1)} copy-done((f32[8]{0:T(128)S(1)}, f32[8]{0:T(128)}, u32[]{:S(2)}) %copy-start.6) | copy-done | bytes 56
  10.3 0.1 select_reduce_fusion.1
  10.4 0.7 %slice-done = f32[3,2,256]{2,1,0:T(2,128)S(1)} async-done(((f32[3,4,256]{2,1,0:T(4,128)}), f32[3,2,256]{2,1,0:T(2,128)S(1)}, s32[]{:S(2)}) %slice-start) | async-done | bytes 6168 | tf_op jit(solution)/shard_map/vmap()/slice | solution.py:248
  11.1 0.2 copy.40
  11.3 0.2 copy.41
  11.5 0.3 fusion
  11.8 0.3 pad_maximum_fusion
  12.0 5.1 %gather_fusion = f32[768,5]{1,0:T(8,128)S(1)} fusion(f32[3,5,256]{1,2,0:T(8,128)S(1)} %pad_maximum_fusion, s32[768]{0:T(1024)S(1)} %reshape.159), kind=kCustom, calls=%fused_computation | custom fusion | bytes 36864 | tf_op jit(solution)/shard_map/vmap(vmap())/gather | solution.py:76
  17.2 0.1 copy.42
  17.4 0.2 copy.43
  17.6 0.7 %copy.44.refs_1_ = f32[1,5,384]{2,1,0:T(8,128)} copy(f32[1,5,384]{1,2,0:T(8,128)S(1)} %get-tuple-element.7) | data formatting | bytes 15360 | tf_op jit(solution)/shard_map/jit(dynamic_index_in_dim)/dynamic_slice | solution.py:255
  18.3 1.6 %collective-permute-start.2 = (f32[1,5,384]{1,2,0:T(8,128)S(1)}, f32[1,5,384]{1,2,0:T(8,128)S(1)}, u32[]{:S(2)}, u32[]{:S(2)}) collective-permute-start(f32[1,5,384]{1,2,0:T(8,128)S(1)} %get-tuple-element.8), channel_id=1, source_target_pairs={{0,2},{2,0},{1,3},{3,1},{4,6},{6,4},{5,7},{7,5},{8,10},{10,8},{9,1... | collective-permute-start | bytes 23048 | tf_op jit(solution)/shard_map/ppermute | solution.py:260
  19.9 10.5 %shard_map.136.refs_6_ = bf16[2,256,512]{2,1,0:T(8,128)(2,1)} custom-call(s32[2,2]{1,0:T(2,128)} %refs_0_.3, f32[1,5,384]{2,1,0:T(8,128)} %copy.44.refs_1_, f32[1,384,5]{2,1,0:T(8,128)} %bitcast.47, bf16[512,512]{1,0:T(8,128)(2,1)} %constant.45.clone.refs_3_, bf16[512,512]{1,0:T(8,128)(2,1)} %constant.46.clone.refs_4_, ...), custom_call_target="tpu_custom_call" | custom-call | flops 2348810240 | bytes 2359296 | tf_op jit(solution)/shard_map/pallas_call | solution.py:187
  30.5 0.7 %copy.45.refs_1_ = f32[1,5,384]{2,1,0:T(8,128)} copy(f32[1,5,384]{1,2,0:T(8,128)S(1)} %collective-permute-done.2) | data formatting | bytes 15360 | tf_op jit(solution)/shard_map/ppermute | solution.py:260
  31.2 10.0 %shard_map.137 = bf16[2,256,512]{2,1,0:T(8,128)(2,1)} custom-call(s32[2,2]{1,0:T(2,128)} %refs_0_.3, f32[1,5,384]{2,1,0:T(8,128)} %copy.45.refs_1_, f32[1,384,5]{2,1,0:T(8,128)} %bitcast.49, bf16[512,512]{1,0:T(8,128)(2,1)} %constant.45.clone.refs_3_, bf16[512,512]{1,0:T(8,128)(2,1)} %constant.46.clone.refs_4_, f32[2,256,256]{2,1,0:T(8,128)} %constant.47.clone.refs_5_, ...), custom_call_target="tpu_custom_call" | custom-call | flops 2348810240 | bytes 2359296 | tf_op jit(solution)/shard_map/pallas_call | solution.py:187
  41.2 2.0 %reshape.158 = bf16[2,256,2,256]{3,2,1,0:T(2,128)(2,1)} reshape(bf16[2,256,512]{2,1,0:T(8,128)(2,1)} %shard_map.137) | data formatting | bytes 1048576 | tf_op jit(solution)/shard_map/reshape | solution.py:266
  (38 shorter events, 0.2 us)
Async XLA Ops:
  0.7 0.7 %copy-start.4 = (s32[1,1,256]{2,1,0:T(1,128)S(1)}, s32[1,1,256]{2,1,0:T(1,128)}, u32[]{:S(2)}) copy-start(s32[1,1,256]{2,1,0:T(1,128)} %param.16) | copy-start | bytes 3076
  0.7 0.7 %copy-start.5 = (s32[1,1,256]{2,1,0:T(1,128)S(1)}, s32[1,1,256]{2,1,0:T(1,128)}, u32[]{:S(2)}) copy-start(s32[1,1,256]{2,1,0:T(1,128)} %param.15) | copy-start | bytes 3076
  1.4 0.7 %copy-start.3 = (f32[1,1,2,256]{3,2,1,0:T(2,128)S(1)}, f32[1,1,2,256]{3,2,1,0:T(2,128)}, u32[]{:S(2)}) copy-start(f32[1,1,2,256]{3,2,1,0:T(2,128)} %param.14) | copy-start | bytes 6148
  2.1 6.8 %collective-permute-start = (f32[1280]{0:T(1024)S(1)}, f32[1280]{0:T(1024)S(1)}, u32[]{:S(2)}, u32[]{:S(2)}) collective-permute-start(f32[1280]{0:T(1024)S(1)} %get-tuple-element.15), channel_id=1, source_target_pairs={{0,4},{4,8},{8,12},{12,0},{1,5},{5,9},{9,13},{13,1},{2,6},{6,10},{... | collective-permute-start | bytes 15368 | tf_op jit(solution)/shard_map/ppermute | solution.py:236
  5.2 3.8 %collective-permute-start.1 = (f32[1280]{0:T(1024)S(1)}, f32[1280]{0:T(1024)S(1)}, u32[]{:S(2)}, u32[]{:S(2)}) collective-permute-start(f32[1280]{0:T(1024)S(1)} %get-tuple-element.16), channel_id=1, source_target_pairs={{4,0},{8,4},{12,8},{0,12},{5,1},{9,5},{13,9},{1,13},{6,2},{10,6},{... | collective-permute-start | bytes 15368 | tf_op jit(solution)/shard_map/ppermute | solution.py:237
  9.0 0.6 %copy-start.2 = (f32[3,4,256]{2,1,0:T(4,128)}, f32[3,4,256]{2,1,0:T(4,128)S(1)}, u32[]{:S(2)}) copy-start(f32[3,4,256]{2,1,0:T(4,128)S(1)} %pad_maximum_fusion.1) | copy-start | bytes 36868
  9.6 0.7 %copy-start.6 = (f32[8]{0:T(128)S(1)}, f32[8]{0:T(128)}, u32[]{:S(2)}) copy-start(f32[8]{0:T(128)} %param.18) | copy-start | bytes 100
  9.6 0.7 %copy-start.7 = (f32[8]{0:T(128)S(1)}, f32[8]{0:T(128)}, u32[]{:S(2)}) copy-start(f32[8]{0:T(128)} %param.17) | copy-start | bytes 100
  10.4 0.7 %slice-start = ((f32[3,4,256]{2,1,0:T(4,128)}), f32[3,2,256]{2,1,0:T(2,128)S(1)}, s32[]{:S(2)}) async-start(f32[3,4,256]{2,1,0:T(4,128)} %copy-done.2), calls=%async_computation | async-start | bytes 12288 | tf_op jit(solution)/shard_map/vmap()/slice | solution.py:248
  17.6 2.3 %copy-start = (f32[1,5,384]{1,2,0:T(8,128)}, f32[1,5,384]{1,2,0:T(8,128)S(1)}, u32[]{:S(2)}) copy-start(f32[1,5,384]{1,2,0:T(8,128)S(1)} %get-tuple-element.7) | copy-start | bytes 23044
  18.3 12.2 %collective-permute-start.2 = (f32[1,5,384]{1,2,0:T(8,128)S(1)}, f32[1,5,384]{1,2,0:T(8,128)S(1)}, u32[]{:S(2)}, u32[]{:S(2)}) collective-permute-start(f32[1,5,384]{1,2,0:T(8,128)S(1)} %get-tuple-element.8), channel_id=1, source_target_pairs={{0,2},{2,0},{1,3},{3,1},{4,6},{6,4},{5,7},{7,5},{8,10},{10,8},{9,1... | collective-permute-start | bytes 23048 | tf_op jit(solution)/shard_map/ppermute | solution.py:260
  30.5 0.7 %copy-start.1 = (f32[1,5,384]{1,2,0:T(8,128)}, f32[1,5,384]{1,2,0:T(8,128)S(1)}, u32[]{:S(2)}) copy-start(f32[1,5,384]{1,2,0:T(8,128)S(1)} %collective-permute-done.2) | copy-start | bytes 23044

commit v5 on v3

--- a/solution.py
+++ b/solution.py
@@ -98,13 +98,13 @@
     return sin_v, cos_v
 
 
-def slices_kernel(
-    pos_ref, rows_ref, cols_ref, a_ref, b_ref, prop_ref, spec_ref, out_ref, wave_ref, pot_ref,
-    *, field_x
-):
+def slices_kernel(*refs, field_x, carried, cap):
+    (pos_ref, owner_ref, table_ref, pk_ref, a_ref, b_ref, prop_ref, last_ref,
+     out_ref, wave_ref, pot_ref) = refs
     batch = wave_ref.shape[0]
     w = prop_ref.shape[-1]
     layers = pot_ref.shape[-1] // w
+    species_count = table_ref.shape[1]
     hop = pl.program_id(0)
     layer = pl.program_id(1)
     f32, bf16 = jnp.float32, jnp.bfloat16
@@ -114,18 +114,51 @@
 
     @pl.when((hop == 0) & (layer == 0))
     def _():
-        rows = dot(a_ref[...], spec_ref[...]).astype(bf16)
-        rows = jnp.concatenate([rows[:w], rows[w:]], 1)
-        start = dot(rows, b_ref[...]).astype(bf16)
-        for p in range(batch):
-            wave_ref[p] = start
+        if carried:
+            wave_ref[...] = last_ref[...]
+        else:
+            rows = dot(a_ref[...], last_ref[...]).astype(bf16)
+            rows = jnp.concatenate([rows[:w], rows[w:]], 1)
+            start = dot(rows, b_ref[...]).astype(bf16)
+            for p in range(batch):
+                wave_ref[p] = start
 
     @pl.when(layer == 0)
     def _():
-        atom_x = rows_ref[0, 0:1, :]
-        inverse_row = rows_ref[0, 2:3, :]
-        atom_y = cols_ref[0, :, 1:2]
-        inverse_col = cols_ref[0, :, 2:3]
+        entry = owner_ref[0]
+        blocks = []
+        for slot in range(3):
+            raw = pk_ref[0, slot, 0:4, :]
+            listed = pk_ref[0, slot, pl.ds(4 + entry, 1), :][:, :cap]
+            species = raw[2:3]
+            slab = raw[3:4]
+            amplitude = jnp.zeros_like(species)
+            inverse = jnp.zeros_like(species)
+            for k in range(species_count):
+                match = species == float(k)
+                amplitude = jnp.where(match, table_ref[0, k], amplitude)
+                inverse = jnp.where(match, table_ref[1, k], inverse)
+            zero = jnp.zeros_like(species)
+            per_layer = [jnp.where(slab == float(l), amplitude, zero) for l in range(layers)]
+            fields = jnp.concatenate(
+                [raw[0:2], inverse] + per_layer + [zero] * (8 - 3 - layers), 0
+            )
+            atoms = fields.shape[1]
+            safe = jnp.maximum(listed, 0.0).astype(jnp.int32)
+            onehot = (lax.broadcasted_iota(jnp.int32, (atoms, cap), 0) == safe).astype(f32)
+            picked = jnp.dot(
+                fields, onehot, preferred_element_type=f32, precision=lax.Precision.HIGHEST
+            )
+            valid = (listed >= 0.0).astype(f32)
+            keep = lax.broadcasted_iota(jnp.int32, (8, 1), 0) < 3
+            picked = jnp.where(keep, picked, picked * valid)
+            blocks.append(picked)
+        rows = jnp.concatenate(blocks, 1)
+        cols = rows.T
+        atom_x = rows[0:1]
+        inverse_row = rows[2:3]
+        atom_y = cols[:, 1:2]
+        inverse_col = cols[:, 2:3]
         pixel_col = lax.broadcasted_iota(jnp.int32, (w, 1), 0).astype(f32)
         pixel_row = lax.broadcasted_iota(jnp.int32, (1, w), 1).astype(f32)
         for p in range(batch):
@@ -136,7 +169,7 @@
             dist_y = wrap(atom_y - shift_y - pixel_row + 0.5 * w, w) - 0.5 * w
             along = jnp.exp(-dist_y * dist_y * inverse_col)
             weighted = jnp.concatenate(
-                [(cols_ref[0, :, 3 + l : 4 + l] * along).astype(bf16) for l in range(layers)], 1
+                [(cols[:, 3 + l : 4 + l] * along).astype(bf16) for l in range(layers)], 1
             )
             pot_ref[p] = dot(across, weighted)
 
@@ -167,29 +200,31 @@
         out_ref[...] = wave_ref[...]
 
 
-def run_slices(probe_pos, rows, cols, window, layers, field_x):
+def run_slices(probe_pos, entry, table, packs, window, layers, field_x, cap, wave=None):
     batch = probe_pos.shape[0]
-    hops, fields, atoms = rows.shape
+    hops = packs.shape[0]
     w = window
     a, b = dft_blocks(w)
     prop = propagator(w)
-    spec = start_spectrum(w)
-    full = lambda shape: pl.BlockSpec(shape, lambda h, l, pos: (0,) * len(shape))
+    full = lambda shape: pl.BlockSpec(shape, lambda h, l, *_: (0,) * len(shape))
+    carried = wave is not None
+    last = wave if carried else jnp.asarray(start_spectrum(w))
+    atoms = 3 * cap
     steps = batch * hops * layers
     flops = steps * 4 * 2 * w * (2 * w) * (2 * w) + batch * hops * 2 * w * atoms * layers * w
     return pl.pallas_call(
-        functools.partial(slices_kernel, field_x=float(field_x)),
+        functools.partial(slices_kernel, field_x=float(field_x), carried=carried, cap=cap),
         out_shape=jax.ShapeDtypeStruct((batch, w, 2 * w), jnp.bfloat16),
         grid_spec=pltpu.PrefetchScalarGridSpec(
-            num_scalar_prefetch=1,
+            num_scalar_prefetch=2,
             grid=(hops, layers),
             in_specs=[
-                pl.BlockSpec((1, fields, atoms), lambda h, l, pos: (h, 0, 0)),
-                pl.BlockSpec((1, atoms, fields), lambda h, l, pos: (h, 0, 0)),
+                pl.BlockSpec(memory_space=pltpu.SMEM),
+                pl.BlockSpec((1,) + packs.shape[1:], lambda h, l, *_: (h, 0, 0, 0)),
                 full((2 * w, 2 * w)),
                 full((2 * w, 2 * w)),
                 full((2, w, w)),
-                full((2 * w, w)),
+                full(last.shape),
             ],
             out_specs=full((batch, w, 2 * w)),
             scratch_shapes=[
@@ -205,7 +240,7 @@
             transcendentals=steps * 2 * w * w + batch * hops * 2 * atoms * w,
             bytes_accessed=2 * (2 * w) ** 2 * 2 + 3 * w * w * 4 + batch * w * w * 4,
         ),
-    )(probe_pos, rows, cols, jnp.asarray(a), jnp.asarray(b), jnp.asarray(prop), jnp.asarray(spec))
+    )(probe_pos, entry, table, packs, jnp.asarray(a), jnp.asarray(b), jnp.asarray(prop), last)
 
 
 def shards(atom_xy, atom_species, atom_slab, species_amp, species_spread, margin, probe_pos):
@@ -216,28 +251,29 @@
     n_lat = lax.axis_size("lat")
     owners = lax.axis_size("slc")
     field_x = n_lat * atoms * (2 * window // cap)
-    fields = atom_fields(
-        atom_xy[0, 0], atom_species[0, 0], atom_slab[0, 0], species_amp, species_spread, layers
-    )
-    field_count = fields.shape[0]
-    pick_table = margin[0, 0, :, 0]
-    picked = jax.vmap(jax.vmap(lambda lst: pick_rows(fields, lst)))(pick_table)
-    to_left = lax.ppermute(
-        picked[:, 0], "lat", [((i + 1) % n_lat, i) for i in range(n_lat)]
-    )
-    to_right = lax.ppermute(
-        picked[:, 2], "lat", [(i, (i + 1) % n_lat) for i in range(n_lat)]
-    )
-    local = jnp.stack([to_right, picked[:, 1], to_left], 1)
-    gathered = lax.all_gather(local, "slc", axis=0, tiled=False)
+    f32 = jnp.float32
+    raw = jnp.concatenate(
+        [atom_xy[0, 0], atom_species[0, 0][None].astype(f32), atom_slab[0, 0][None].astype(f32)], 0
+    )
+    marg = jnp.transpose(margin[0, 0, :, 0], (1, 0, 2)).astype(f32)
+    marg = jnp.pad(marg, ((0, 0), (0, 0), (0, atoms - cap)), constant_values=-1.0)
+    packs = jnp.concatenate([jnp.broadcast_to(raw[None], (3,) + raw.shape), marg], 1)
+    from_left = lax.ppermute(packs[2], "lat", [(i, (i + 1) % n_lat) for i in range(n_lat)])
+    from_right = lax.ppermute(packs[0], "lat", [((i + 1) % n_lat, i) for i in range(n_lat)])
+    local = jnp.stack([from_left, packs[1], from_right], 0)[None]
     me = lax.axis_index("slc")
-    mine = lax.dynamic_index_in_dim(gathered, me, 1, keepdims=False)
-    hop_owner = (me + jnp.arange(owners)) % owners
-    rows = jnp.take(mine, hop_owner, axis=0)
-    rows = jnp.transpose(rows, (0, 2, 1, 3)).reshape(owners, field_count, 3 * cap)
-    cols = jnp.transpose(rows, (0, 2, 1))
+    entry = jnp.reshape(me, (1,)).astype(jnp.int32)
+    later = [
+        lax.ppermute(local, "slc", [(i, (i - hop) % owners) for i in range(owners)])
+        for hop in range(1, owners)
+    ]
+    table = jnp.stack([species_amp, 0.5 / (species_spread * species_spread)], 0)
     batch = probe_pos.shape[0]
-    wave = run_slices(probe_pos, rows, cols, window, layers, field_x)
+    wave = run_slices(probe_pos, entry, table, local, window, layers, field_x, cap)
+    if later:
+        wave = run_slices(
+            probe_pos, entry, table, jnp.concatenate(later, 0), window, layers, field_x, cap, wave
+        )
     return wave.reshape(batch, window, 2, window)
 
 

time: 37.4 us -> 33.8 us (0.904)
  blocking collectives: 4.45 us -> 0 us
  Pallas kernels: 17.4 us -> 20.9 us
  local copies, waits for them, and re-layouts: 7.4 us -> 3.92 us
  starting transfers between devices: 5.2 us -> 6.89 us
  waiting for transfers between devices: 1.54 us -> 0.4 us
    all_gather x1 -> x0, blocking collectives: 4.45 us -> none  [shards(): gathered = lax.all_gather(local, 'slc', axis=0, tiled=False)]
    pallas_call x1 -> x2, Pallas kernels: 17.4 us -> 20.9 us  [run_slices(): pl.pallas_call(functools.partial(slices_kernel, field_x=float(field_x), c...]
    gather x3 -> x0, local copies, waits for them, and re-layouts: 2.29 us -> none  [the longest x2 1.72 us: pick_rows(): gathered = fields[:, safe_index]]
    ppermute x2 -> x3, starting transfers between devices: 5.2 us -> 6.89 us  [the longest x1 3.1 us: shards(): lax.ppermute(packs[2], 'lat', [(i, (i + 1) % n_lat) for i in range(n_lat)])]
    ppermute x2 -> x3, waiting for transfers between devices: 1.54 us -> 0.4 us  [the longest x1 0.4 us: shards(): lax.ppermute(packs[2], 'lat', [(i, (i + 1) % n_lat) for i in range(n_lat)])]
    reshape x1 -> x0, local copies, waits for them, and re-layouts: 0.77 us -> none  [shards(): jnp.transpose(rows, (0, 2, 1, 3)).reshape(owners, field_count, 3 * cap)]
    another operation x1 -> x2, other arithmetic: 0.01 us -> 0.59 us  [shards(): table = jnp.stack([species_amp, 0.5 / (species_spread * species_spread)], 0)]
    convert_element_type x1 -> x2, other arithmetic: 0.76 us -> 0.72 us  [the longest x1 0.71 us: shards(): marg = jnp.transpose(margin[0, 0, :, 0], (1, 0, 2)).astype(f32)]
  transfers between devices with their start and end apart: 2 -> 3, of which waited for: 1 -> 1; matrix products, arithmetic and copies ran while one was open for 0% -> 2% of each run, Pallas kernels for 0% -> 32%
where the time goes in v5:
time: 33.8 us; the launch traced here: 33.5 us
  Pallas kernels  20.9 us (62%)
  starting transfers between devices  6.89 us (20%)
  local copies, waits for them, and re-layouts  3.92 us (12%)
  other arithmetic  1.33 us (4%)
  waiting for transfers between devices  0.4 us (1%)
    pallas_call x2, Pallas kernels, run_slices(): pl.pallas_call(functools.partial(slices_kernel, field_x=float(field_x), c...  20.9 us
    ppermute x1, starting transfers between devices, shards(): lax.ppermute(packs[2], 'lat', [(i, (i + 1) % n_lat) for i in range(n_lat)])  3.1 us
    ppermute x1, starting transfers between devices, shards(): lax.ppermute(packs[0], 'lat', [((i + 1) % n_lat, i) for i in range(n_lat)])  2.09 us
    reshape x1, local copies, waits for them, and re-layouts, shards(): return wave.reshape(batch, window, 2, window)  1.96 us
    unnamed x14, local copies, waits for them, and re-layouts  1.95 us
    ppermute x1, starting transfers between devices, shards(): lax.ppermute(local, 'slc', [(i, (i - hop) % owners) for i in range(owners)])  1.69 us
    convert_element_type x1, other arithmetic, shards(): marg = jnp.transpose(margin[0, 0, :, 0], (1, 0, 2)).astype(f32)  0.71 us
  transfers between devices with their start and end apart: 3, of which 1 were waited for; matrix products, arithmetic and copies ran while one was open for 2% of the time, Pallas kernels for 32%

profile of v5, /device:TPU:0, one launch (start us, length us, event | category | flops | bytes accessed | tf_op | source)
XLA Modules:
  0.0 33.5 jit_solution(11585488934974032364)
XLA Ops:
  0.0 0.0 copy-start.2
  0.0 0.0 copy-start.3
  0.0 0.7 %fusion = f32[3,2,128]{2,1,0:T(2,128)S(1)} fusion(s32[1,1,2,1,3,128]{5,3,4,2,1,0:T(1,128)} %param.19), kind=kLoop, calls=%fused_computation.7 | loop fusion | flops 768 | bytes 6144 | tf_op jit(solution)/shard_map/convert_element_type | solution.py:258
  0.7 0.0 copy-done.2
  0.7 0.0 copy-done.3
  0.7 0.0 copy-start.1
  0.7 0.7 %copy-done.1 = f32[1,1,2,256]{3,2,1,0:T(2,128)S(1)} copy-done((f32[1,1,2,256]{3,2,1,0:T(2,128)S(1)}, f32[1,1,2,256]{3,2,1,0:T(2,128)}, u32[]{:S(2)}) %copy-start.1) | copy-done | bytes 2072
  1.5 0.0 copy-start.6
  1.5 3.1 %collective-permute-start = (f32[6,256]{1,0:T(8,128)S(1)}, f32[6,256]{1,0:T(8,128)S(1)}, u32[]{:S(2)}, u32[]{:S(2)}) collective-permute-start(f32[6,256]{1,0:T(8,128)S(1)} %get-tuple-element.5), channel_id=1, source_target_pairs={{0,4},{4,8},{8,12},{12,0},{1,5},{5,9},{9,13},{13,1},{2,6},{6,10},{... | collective-permute-start | bytes 18440 | tf_op jit(solution)/shard_map/ppermute | solution.py:261
  4.6 2.1 %collective-permute-start.1 = (f32[6,256]{1,0:T(8,128)S(1)}, f32[6,256]{1,0:T(8,128)S(1)}, u32[]{:S(2)}, u32[]{:S(2)}) collective-permute-start(f32[6,256]{1,0:T(8,128)S(1)} %get-tuple-element.6), channel_id=1, source_target_pairs={{4,0},{8,4},{12,8},{0,12},{5,1},{9,5},{13,9},{1,13},{6,2},{10,6},{... | collective-permute-start | bytes 18440 | tf_op jit(solution)/shard_map/ppermute | solution.py:262
  6.7 0.0 copy-done.6
  6.7 0.0 copy-start.4
  6.7 0.7 %copy-done.4 = f32[8]{0:T(128)S(1)} copy-done((f32[8]{0:T(128)S(1)}, f32[8]{0:T(128)}, u32[]{:S(2)}) %copy-start.4) | copy-done | bytes 56
  7.3 0.6 %pad_maximum_fusion.1.refs_2_ = f32[2,8]{1,0:T(2,128)} fusion(f32[1,8]{1,0:T(1,128)S(1)} %divide_bitcast_fusion, f32[1,8]{1,0:T(1,128)S(1)} %bitcast.24), kind=kLoop, calls=%fused_computation.8 | loop fusion | flops 16 | bytes 128 | tf_op jit(solution)/shard_map/stack | solution.py:270
  7.9 0.4 %collective-permute-done = f32[6,256]{1,0:T(8,128)S(1)} collective-permute-done((f32[6,256]{1,0:T(8,128)S(1)}, f32[6,256]{1,0:T(8,128)S(1)}, u32[]{:S(2)}, u32[]{:S(2)}) %collective-permute-start) | collective-permute-done | bytes 6176 | tf_op jit(solution)/shard_map/ppermute | solution.py:261
  8.3 0.0 collective-permute-done.1
  8.3 0.0 copy-start
  8.3 1.7 %collective-permute-start.2 = (f32[1,3,6,256]{3,2,1,0:T(8,128)S(1)}, f32[1,3,6,256]{3,2,1,0:T(8,128)S(1)}, u32[]{:S(2)}, u32[]{:S(2)}) collective-permute-start(f32[1,3,6,256]{3,2,1,0:T(8,128)S(1)} %maximum_bitcast_fusion.refs_3_), channel_id=1, source_target_pairs={{0,2},{2,0},{1,3},{3,1},{4,6},{6,4},{5,7},{7,5},{8,10},{10,8},{9,1... | collective-permute-start | bytes 55304 | tf_op jit(solution)/shard_map/ppermute | solution.py:267
  10.0 0.0 copy-done
  10.0 10.7 %shard_map.136.refs_7_ = bf16[2,256,512]{2,1,0:T(8,128)(2,1)} custom-call(s32[2,2]{1,0:T(2,128)} %refs_0_.3, s32[1]{0:T(128)} %bitcast.refs_1_, f32[2,8]{1,0:T(2,128)} %pad_maximum_fusion.1.refs_2_, f32[1,3,6,256]{3,2,1,0:T(8,128)} %copy-done, bf16[512,512]{1,0:T(8,128)(2,1)} %constant.17.clone.refs_4_, bf16[512,512]{1,0:T(8,128)(2,1)} %constant.18.clone.refs_5_, ...), custom_call_target="tpu_custom_call" | custom-call | flops 2348810240 | bytes 2359296 | tf_op jit(solution)/shard_map/pallas_call | solution.py:215
  20.8 0.0 collective-permute-done.2.refs_3_
  20.8 0.6 %copy-done.5 = f32[1,3,6,256]{3,2,1,0:T(8,128)} copy-done((f32[1,3,6,256]{3,2,1,0:T(8,128)}, f32[1,3,6,256]{3,2,1,0:T(8,128)S(1)}, u32[]{:S(2)}) %copy-start.5) | copy-done | bytes 18456
  21.4 10.2 %shard_map.137 = bf16[2,256,512]{2,1,0:T(8,128)(2,1)} custom-call(s32[2,2]{1,0:T(2,128)} %refs_0_.3, s32[1]{0:T(128)} %bitcast.refs_1_, f32[2,8]{1,0:T(2,128)} %pad_maximum_fusion.1.refs_2_, f32[1,3,6,256]{3,2,1,0:T(8,128)} %copy-done.5, bf16[512,512]{1,0:T(8,128)(2,1)} %constant.17.clone.refs_4_, bf16[512,512]{1,0:T(8,128)(2,1)} %constant.18.clone.refs_5_, ...), custom_call_target="tpu_custom_call" | custom-call | flops 2348810240 | bytes 2359296 | tf_op jit(solution)/shard_map/pallas_call | solution.py:215
  31.5 2.0 %reshape.35 = bf16[2,256,2,256]{3,2,1,0:T(2,128)(2,1)} reshape(bf16[2,256,512]{2,1,0:T(8,128)(2,1)} %shard_map.137) | data formatting | bytes 1048576 | tf_op jit(solution)/shard_map/reshape | solution.py:277
  (8 shorter events, 0.0 us)
Async XLA Ops:
  0.0 0.7 %copy-start.2 = (s32[1,1,256]{2,1,0:T(1,128)S(1)}, s32[1,1,256]{2,1,0:T(1,128)}, u32[]{:S(2)}) copy-start(s32[1,1,256]{2,1,0:T(1,128)} %param.16) | copy-start | bytes 3076
  0.0 0.7 %copy-start.3 = (s32[1,1,256]{2,1,0:T(1,128)S(1)}, s32[1,1,256]{2,1,0:T(1,128)}, u32[]{:S(2)}) copy-start(s32[1,1,256]{2,1,0:T(1,128)} %param.15) | copy-start | bytes 3076
  0.7 0.7 %copy-start.1 = (f32[1,1,2,256]{3,2,1,0:T(2,128)S(1)}, f32[1,1,2,256]{3,2,1,0:T(2,128)}, u32[]{:S(2)}) copy-start(f32[1,1,2,256]{3,2,1,0:T(2,128)} %param.14) | copy-start | bytes 6148
  1.5 5.2 %copy-start.6 = (f32[8]{0:T(128)S(1)}, f32[8]{0:T(128)}, u32[]{:S(2)}) copy-start(f32[8]{0:T(128)} %param.18) | copy-start | bytes 100
  1.5 6.8 %collective-permute-start = (f32[6,256]{1,0:T(8,128)S(1)}, f32[6,256]{1,0:T(8,128)S(1)}, u32[]{:S(2)}, u32[]{:S(2)}) collective-permute-start(f32[6,256]{1,0:T(8,128)S(1)} %get-tuple-element.5), channel_id=1, source_target_pairs={{0,4},{4,8},{8,12},{12,0},{1,5},{5,9},{9,13},{13,1},{2,6},{6,10},{... | collective-permute-start | bytes 18440 | tf_op jit(solution)/shard_map/ppermute | solution.py:261
  4.6 3.7 %collective-permute-start.1 = (f32[6,256]{1,0:T(8,128)S(1)}, f32[6,256]{1,0:T(8,128)S(1)}, u32[]{:S(2)}, u32[]{:S(2)}) collective-permute-start(f32[6,256]{1,0:T(8,128)S(1)} %get-tuple-element.6), channel_id=1, source_target_pairs={{4,0},{8,4},{12,8},{0,12},{5,1},{9,5},{13,9},{1,13},{6,2},{10,6},{... | collective-permute-start | bytes 18440 | tf_op jit(solution)/shard_map/ppermute | solution.py:262
  6.7 0.7 %copy-start.4 = (f32[8]{0:T(128)S(1)}, f32[8]{0:T(128)}, u32[]{:S(2)}) copy-start(f32[8]{0:T(128)} %param.17) | copy-start | bytes 100
  8.3 1.7 %copy-start = (f32[1,3,6,256]{3,2,1,0:T(8,128)}, f32[1,3,6,256]{3,2,1,0:T(8,128)S(1)}, u32[]{:S(2)}) copy-start(f32[1,3,6,256]{3,2,1,0:T(8,128)S(1)} %maximum_bitcast_fusion.refs_3_) | copy-start | bytes 55300
  8.3 12.4 %collective-permute-start.2 = (f32[1,3,6,256]{3,2,1,0:T(8,128)S(1)}, f32[1,3,6,256]{3,2,1,0:T(8,128)S(1)}, u32[]{:S(2)}, u32[]{:S(2)}) collective-permute-start(f32[1,3,6,256]{3,2,1,0:T(8,128)S(1)} %maximum_bitcast_fusion.refs_3_), channel_id=1, source_target_pairs={{0,2},{2,0},{1,3},{3,1},{4,6},{6,4},{5,7},{7,5},{8,10},{10,8},{9,1... | collective-permute-start | bytes 55304 | tf_op jit(solution)/shard_map/ppermute | solution.py:267
  20.8 0.6 %copy-start.5 = (f32[1,3,6,256]{3,2,1,0:T(8,128)}, f32[1,3,6,256]{3,2,1,0:T(8,128)S(1)}, u32[]{:S(2)}) copy-start(f32[1,3,6,256]{3,2,1,0:T(8,128)S(1)} %collective-permute-done.2.refs_3_) | copy-start | bytes 55300

commit v6 on v5

--- a/solution.py
+++ b/solution.py
@@ -98,7 +98,7 @@
     return sin_v, cos_v
 
 
-def slices_kernel(*refs, field_x, carried, cap):
+def slices_kernel(*refs, field_x, carried, cap, final):
     (pos_ref, owner_ref, table_ref, pk_ref, a_ref, b_ref, prop_ref, last_ref,
      out_ref, wave_ref, pot_ref) = refs
     batch = wave_ref.shape[0]
@@ -197,10 +197,15 @@
 
     @pl.when((hop == pl.num_programs(0) - 1) & (layer == pl.num_programs(1) - 1))
     def _():
-        out_ref[...] = wave_ref[...]
-
-
-def run_slices(probe_pos, entry, table, packs, window, layers, field_x, cap, wave=None):
+        if final:
+            for p in range(batch):
+                out_ref[p, :, 0, :] = wave_ref[p, :, :w]
+                out_ref[p, :, 1, :] = wave_ref[p, :, w:]
+        else:
+            out_ref[...] = wave_ref[...]
+
+
+def run_slices(probe_pos, entry, table, packs, window, layers, field_x, cap, wave=None, final=False):
     batch = probe_pos.shape[0]
     hops = packs.shape[0]
     w = window
@@ -208,13 +213,14 @@
     prop = propagator(w)
     full = lambda shape: pl.BlockSpec(shape, lambda h, l, *_: (0,) * len(shape))
     carried = wave is not None
+    out_shape = (batch, w, 2, w) if final else (batch, w, 2 * w)
     last = wave if carried else jnp.asarray(start_spectrum(w))
     atoms = 3 * cap
     steps = batch * hops * layers
     flops = steps * 4 * 2 * w * (2 * w) * (2 * w) + batch * hops * 2 * w * atoms * layers * w
     return pl.pallas_call(
-        functools.partial(slices_kernel, field_x=float(field_x), carried=carried, cap=cap),
-        out_shape=jax.ShapeDtypeStruct((batch, w, 2 * w), jnp.bfloat16),
+        functools.partial(slices_kernel, field_x=float(field_x), carried=carried, cap=cap, final=final),
+        out_shape=jax.ShapeDtypeStruct(out_shape, jnp.bfloat16),
         grid_spec=pltpu.PrefetchScalarGridSpec(
             num_scalar_prefetch=2,
             grid=(hops, layers),
@@ -226,7 +232,7 @@
                 full((2, w, w)),
                 full(last.shape),
             ],
-            out_specs=full((batch, w, 2 * w)),
+            out_specs=full(out_shape),
             scratch_shapes=[
                 pltpu.VMEM((batch, w, 2 * w), jnp.bfloat16),
                 pltpu.VMEM((batch, w, layers * w), jnp.float32),
@@ -269,12 +275,13 @@
     ]
     table = jnp.stack([species_amp, 0.5 / (species_spread * species_spread)], 0)
     batch = probe_pos.shape[0]
-    wave = run_slices(probe_pos, entry, table, local, window, layers, field_x, cap)
+    wave = run_slices(probe_pos, entry, table, local, window, layers, field_x, cap, final=not later)
     if later:
         wave = run_slices(
-            probe_pos, entry, table, jnp.concatenate(later, 0), window, layers, field_x, cap, wave
+            probe_pos, entry, table, jnp.concatenate(later, 0), window, layers, field_x, cap, wave,
+            final=True,
         )
-    return wave.reshape(batch, window, 2, window)
+    return wave
 
 
 def solution(mesh):

time: 33.8 us -> 32.7 us (0.967)
  local copies, waits for them, and re-layouts: 3.92 us -> 1.96 us
  Pallas kernels: 20.9 us -> 21.8 us
    reshape x1 -> x0, local copies, waits for them, and re-layouts: 1.96 us -> none  [shards(): return wave.reshape(batch, window, 2, window)]
    pallas_call x2, Pallas kernels: 20.9 us -> 21.8 us  [run_slices(): pl.pallas_call(functools.partial(slices_kernel, field_x=float(field_x), c...]
  transfers between devices with their start and end apart: 3 -> 3, of which waited for: 1 -> 1; matrix products, arithmetic and copies ran while one was open for 2% -> 2% of each run, Pallas kernels for 32% -> 33%
where the time goes in v6:
time: 32.7 us; the launch traced here: 32.4 us
  Pallas kernels  21.8 us (67%)
  starting transfers between devices  6.89 us (21%)
  local copies, waits for them, and re-layouts  1.96 us (6%)
  other arithmetic  1.33 us (4%)
  waiting for transfers between devices  0.4 us (1%)
    pallas_call x2, Pallas kernels, run_slices(): pl.pallas_call(functools.partial(slices_kernel, field_x=float(field_x), c...  21.8 us
    ppermute x1, starting transfers between devices, shards(): lax.ppermute(packs[2], 'lat', [(i, (i + 1) % n_lat) for i in range(n_lat)])  3.1 us
    ppermute x1, starting transfers between devices, shards(): lax.ppermute(packs[0], 'lat', [((i + 1) % n_lat, i) for i in range(n_lat)])  2.09 us
    unnamed x14, local copies, waits for them, and re-layouts  1.95 us
    ppermute x1, starting transfers between devices, shards(): lax.ppermute(local, 'slc', [(i, (i - hop) % owners) for i in range(owners)])  1.69 us
    convert_element_type x1, other arithmetic, shards(): marg = jnp.transpose(margin[0, 0, :, 0], (1, 0, 2)).astype(f32)  0.71 us
  transfers between devices with their start and end apart: 3, of which 1 were waited for; matrix products, arithmetic and copies ran while one was open for 2% of the time, Pallas kernels for 33%

profile of v6, /device:TPU:0, one launch (start us, length us, event | category | flops | bytes accessed | tf_op | source)
XLA Modules:
  0.0 32.4 jit_solution(4225227881496787355)
XLA Ops:
  0.0 0.0 copy-start.2
  0.0 0.0 copy-start.3
  0.0 0.7 %fusion = f32[3,2,128]{2,1,0:T(2,128)S(1)} fusion(s32[1,1,2,1,3,128]{5,3,4,2,1,0:T(1,128)} %param.19), kind=kLoop, calls=%fused_computation.7 | loop fusion | flops 768 | bytes 6144 | tf_op jit(solution)/shard_map/convert_element_type | solution.py:264
  0.7 0.0 copy-done.2
  0.7 0.0 copy-done.3
  0.7 0.0 copy-start.1
  0.7 0.7 %copy-done.1 = f32[1,1,2,256]{3,2,1,0:T(2,128)S(1)} copy-done((f32[1,1,2,256]{3,2,1,0:T(2,128)S(1)}, f32[1,1,2,256]{3,2,1,0:T(2,128)}, u32[]{:S(2)}) %copy-start.1) | copy-done | bytes 2072
  1.5 0.0 copy-start.6
  1.5 3.1 %collective-permute-start = (f32[6,256]{1,0:T(8,128)S(1)}, f32[6,256]{1,0:T(8,128)S(1)}, u32[]{:S(2)}, u32[]{:S(2)}) collective-permute-start(f32[6,256]{1,0:T(8,128)S(1)} %get-tuple-element.5), channel_id=1, source_target_pairs={{0,4},{4,8},{8,12},{12,0},{1,5},{5,9},{9,13},{13,1},{2,6},{6,10},{... | collective-permute-start | bytes 18440 | tf_op jit(solution)/shard_map/ppermute | solution.py:267
  4.6 2.1 %collective-permute-start.1 = (f32[6,256]{1,0:T(8,128)S(1)}, f32[6,256]{1,0:T(8,128)S(1)}, u32[]{:S(2)}, u32[]{:S(2)}) collective-permute-start(f32[6,256]{1,0:T(8,128)S(1)} %get-tuple-element.6), channel_id=1, source_target_pairs={{4,0},{8,4},{12,8},{0,12},{5,1},{9,5},{13,9},{1,13},{6,2},{10,6},{... | collective-permute-start | bytes 18440 | tf_op jit(solution)/shard_map/ppermute | solution.py:268
  6.7 0.0 copy-done.6
  6.7 0.0 copy-start.4
  6.7 0.7 %copy-done.4 = f32[8]{0:T(128)S(1)} copy-done((f32[8]{0:T(128)S(1)}, f32[8]{0:T(128)}, u32[]{:S(2)}) %copy-start.4) | copy-done | bytes 56
  7.3 0.6 %pad_maximum_fusion.1.refs_2_ = f32[2,8]{1,0:T(2,128)} fusion(f32[1,8]{1,0:T(1,128)S(1)} %divide_bitcast_fusion, f32[1,8]{1,0:T(1,128)S(1)} %bitcast.24), kind=kLoop, calls=%fused_computation.8 | loop fusion | flops 16 | bytes 128 | tf_op jit(solution)/shard_map/stack | solution.py:276
  7.9 0.4 %collective-permute-done = f32[6,256]{1,0:T(8,128)S(1)} collective-permute-done((f32[6,256]{1,0:T(8,128)S(1)}, f32[6,256]{1,0:T(8,128)S(1)}, u32[]{:S(2)}, u32[]{:S(2)}) %collective-permute-start) | collective-permute-done | bytes 6176 | tf_op jit(solution)/shard_map/ppermute | solution.py:267
  8.3 0.0 collective-permute-done.1
  8.3 0.0 copy-start
  8.3 1.7 %collective-permute-start.2 = (f32[1,3,6,256]{3,2,1,0:T(8,128)S(1)}, f32[1,3,6,256]{3,2,1,0:T(8,128)S(1)}, u32[]{:S(2)}, u32[]{:S(2)}) collective-permute-start(f32[1,3,6,256]{3,2,1,0:T(8,128)S(1)} %maximum_bitcast_fusion.refs_3_), channel_id=1, source_target_pairs={{0,2},{2,0},{1,3},{3,1},{4,6},{6,4},{5,7},{7,5},{8,10},{10,8},{9,1... | collective-permute-start | bytes 55304 | tf_op jit(solution)/shard_map/ppermute | solution.py:273
  10.0 0.0 copy-done
  10.0 10.7 %shard_map.136.refs_7_ = bf16[2,256,512]{2,1,0:T(8,128)(2,1)} custom-call(s32[2,2]{1,0:T(2,128)} %refs_0_.3, s32[1]{0:T(128)} %bitcast.refs_1_, f32[2,8]{1,0:T(2,128)} %pad_maximum_fusion.1.refs_2_, f32[1,3,6,256]{3,2,1,0:T(8,128)} %copy-done, bf16[512,512]{1,0:T(8,128)(2,1)} %constant.17.clone.refs_4_, bf16[512,512]{1,0:T(8,128)(2,1)} %constant.18.clone.refs_5_, ...), custom_call_target="tpu_custom_call" | custom-call | flops 2348810240 | bytes 2359296 | tf_op jit(solution)/shard_map/pallas_call | solution.py:221
  20.8 0.0 collective-permute-done.2.refs_3_
  20.8 0.0 copy-start.5
  20.8 0.6 %copy-done.5 = f32[1,3,6,256]{3,2,1,0:T(8,128)} copy-done((f32[1,3,6,256]{3,2,1,0:T(8,128)}, f32[1,3,6,256]{3,2,1,0:T(8,128)S(1)}, u32[]{:S(2)}) %copy-start.5) | copy-done | bytes 18456
  21.4 11.1 %shard_map.137 = bf16[2,256,2,256]{3,2,1,0:T(2,128)(2,1)} custom-call(s32[2,2]{1,0:T(2,128)} %refs_0_.3, s32[1]{0:T(128)} %bitcast.refs_1_, f32[2,8]{1,0:T(2,128)} %pad_maximum_fusion.1.refs_2_, f32[1,3,6,256]{3,2,1,0:T(8,128)} %copy-done.5, bf16[512,512]{1,0:T(8,128)(2,1)} %constant.17.clone.refs_4_, bf16[512,512]{1,0:T(8,128)(2,1)} %constant.18.clone.refs_5_, ...), custom_call_target="tpu_custom_call" | custom-call | flops 2348810240 | bytes 2359296 | tf_op jit(solution)/shard_map/pallas_call | solution.py:221
  (7 shorter events, 0.0 us)
Async XLA Ops:
  0.0 0.7 %copy-start.2 = (s32[1,1,256]{2,1,0:T(1,128)S(1)}, s32[1,1,256]{2,1,0:T(1,128)}, u32[]{:S(2)}) copy-start(s32[1,1,256]{2,1,0:T(1,128)} %param.16) | copy-start | bytes 3076
  0.0 0.7 %copy-start.3 = (s32[1,1,256]{2,1,0:T(1,128)S(1)}, s32[1,1,256]{2,1,0:T(1,128)}, u32[]{:S(2)}) copy-start(s32[1,1,256]{2,1,0:T(1,128)} %param.15) | copy-start | bytes 3076
  0.7 0.7 %copy-start.1 = (f32[1,1,2,256]{3,2,1,0:T(2,128)S(1)}, f32[1,1,2,256]{3,2,1,0:T(2,128)}, u32[]{:S(2)}) copy-start(f32[1,1,2,256]{3,2,1,0:T(2,128)} %param.14) | copy-start | bytes 6148
  1.5 5.2 %copy-start.6 = (f32[8]{0:T(128)S(1)}, f32[8]{0:T(128)}, u32[]{:S(2)}) copy-start(f32[8]{0:T(128)} %param.18) | copy-start | bytes 100
  1.5 6.8 %collective-permute-start = (f32[6,256]{1,0:T(8,128)S(1)}, f32[6,256]{1,0:T(8,128)S(1)}, u32[]{:S(2)}, u32[]{:S(2)}) collective-permute-start(f32[6,256]{1,0:T(8,128)S(1)} %get-tuple-element.5), channel_id=1, source_target_pairs={{0,4},{4,8},{8,12},{12,0},{1,5},{5,9},{9,13},{13,1},{2,6},{6,10},{... | collective-permute-start | bytes 18440 | tf_op jit(solution)/shard_map/ppermute | solution.py:267
  4.6 3.7 %collective-permute-start.1 = (f32[6,256]{1,0:T(8,128)S(1)}, f32[6,256]{1,0:T(8,128)S(1)}, u32[]{:S(2)}, u32[]{:S(2)}) collective-permute-start(f32[6,256]{1,0:T(8,128)S(1)} %get-tuple-element.6), channel_id=1, source_target_pairs={{4,0},{8,4},{12,8},{0,12},{5,1},{9,5},{13,9},{1,13},{6,2},{10,6},{... | collective-permute-start | bytes 18440 | tf_op jit(solution)/shard_map/ppermute | solution.py:268
  6.7 0.7 %copy-start.4 = (f32[8]{0:T(128)S(1)}, f32[8]{0:T(128)}, u32[]{:S(2)}) copy-start(f32[8]{0:T(128)} %param.17) | copy-start | bytes 100
  8.3 1.7 %copy-start = (f32[1,3,6,256]{3,2,1,0:T(8,128)}, f32[1,3,6,256]{3,2,1,0:T(8,128)S(1)}, u32[]{:S(2)}) copy-start(f32[1,3,6,256]{3,2,1,0:T(8,128)S(1)} %maximum_bitcast_fusion.refs_3_) | copy-start | bytes 55300
  8.3 12.4 %collective-permute-start.2 = (f32[1,3,6,256]{3,2,1,0:T(8,128)S(1)}, f32[1,3,6,256]{3,2,1,0:T(8,128)S(1)}, u32[]{:S(2)}, u32[]{:S(2)}) collective-permute-start(f32[1,3,6,256]{3,2,1,0:T(8,128)S(1)} %maximum_bitcast_fusion.refs_3_), channel_id=1, source_target_pairs={{0,2},{2,0},{1,3},{3,1},{4,6},{6,4},{5,7},{7,5},{8,10},{10,8},{9,1... | collective-permute-start | bytes 55304 | tf_op jit(solution)/shard_map/ppermute | solution.py:273
  20.8 0.6 %copy-start.5 = (f32[1,3,6,256]{3,2,1,0:T(8,128)}, f32[1,3,6,256]{3,2,1,0:T(8,128)S(1)}, u32[]{:S(2)}) copy-start(f32[1,3,6,256]{3,2,1,0:T(8,128)S(1)} %collective-permute-done.2.refs_3_) | copy-start | bytes 55300

commit v7 on v6

--- a/solution.py
+++ b/solution.py
@@ -99,8 +99,8 @@
 
 
 def slices_kernel(*refs, field_x, carried, cap, final):
-    (pos_ref, owner_ref, table_ref, pk_ref, a_ref, b_ref, prop_ref, last_ref,
-     out_ref, wave_ref, pot_ref) = refs
+    (pos_ref, owner_ref, table_ref, pk_ref, a_hbm, b_hbm, prop_hbm, last_hbm,
+     out_ref, wave_ref, pot_ref, a_ref, b_ref, prop_ref, last_ref, sems) = refs
     batch = wave_ref.shape[0]
     w = prop_ref.shape[-1]
     layers = pot_ref.shape[-1] // w
@@ -112,16 +112,18 @@
     def dot(a, b):
         return jnp.dot(a, b, preferred_element_type=f32)
 
-    @pl.when((hop == 0) & (layer == 0))
+    first = (hop == 0) & (layer == 0)
+    copies = [
+        pltpu.make_async_copy(src, dst, sems.at[k])
+        for k, (src, dst) in enumerate(
+            [(a_hbm, a_ref), (b_hbm, b_ref), (prop_hbm, prop_ref), (last_hbm, last_ref)]
+        )
+    ]
+
+    @pl.when(first)
     def _():
-        if carried:
-            wave_ref[...] = last_ref[...]
-        else:
-            rows = dot(a_ref[...], last_ref[...]).astype(bf16)
-            rows = jnp.concatenate([rows[:w], rows[w:]], 1)
-            start = dot(rows, b_ref[...]).astype(bf16)
-            for p in range(batch):
-                wave_ref[p] = start
+        for copy in copies:
+            copy.start()
 
     @pl.when(layer == 0)
     def _():
@@ -173,6 +175,19 @@
             )
             pot_ref[p] = dot(across, weighted)
 
+    @pl.when(first)
+    def _():
+        for copy in copies:
+            copy.wait()
+        if carried:
+            wave_ref[...] = last_ref[...]
+        else:
+            rows = dot(a_ref[...], last_ref[...]).astype(bf16)
+            rows = jnp.concatenate([rows[:w], rows[w:]], 1)
+            start = dot(rows, b_ref[...]).astype(bf16)
+            for p in range(batch):
+                wave_ref[p] = start
+
     pr = prop_ref[0]
     pi = prop_ref[1]
     column = pl.ds(pl.multiple_of(layer * w, w), w)
@@ -227,15 +242,20 @@
             in_specs=[
                 pl.BlockSpec(memory_space=pltpu.SMEM),
                 pl.BlockSpec((1,) + packs.shape[1:], lambda h, l, *_: (h, 0, 0, 0)),
-                full((2 * w, 2 * w)),
-                full((2 * w, 2 * w)),
-                full((2, w, w)),
-                full(last.shape),
+                pl.BlockSpec(memory_space=pl.ANY),
+                pl.BlockSpec(memory_space=pl.ANY),
+                pl.BlockSpec(memory_space=pl.ANY),
+                pl.BlockSpec(memory_space=pl.ANY),
             ],
             out_specs=full(out_shape),
             scratch_shapes=[
                 pltpu.VMEM((batch, w, 2 * w), jnp.bfloat16),
                 pltpu.VMEM((batch, w, layers * w), jnp.float32),
+                pltpu.VMEM(a.shape, jnp.bfloat16),
+                pltpu.VMEM(b.shape, jnp.bfloat16),
+                pltpu.VMEM(prop.shape, jnp.float32),
+                pltpu.VMEM(last.shape, jnp.bfloat16),
+                pltpu.SemaphoreType.DMA((4,)),
             ],
         ),
         compiler_params=pltpu.CompilerParams(

time: 32.7 us -> 31.7 us (0.969)
  Pallas kernels: 21.8 us -> 20.7 us
    pallas_call x2, Pallas kernels: 21.8 us -> 20.7 us  [run_slices(): pl.pallas_call(functools.partial(slices_kernel, field_x=float(field_x), c...]
  transfers between devices with their start and end apart: 3 -> 3, of which waited for: 1 -> 1; matrix products, arithmetic and copies ran while one was open for 2% -> 2% of each run, Pallas kernels for 33% -> 32%
where the time goes in v7:
time: 31.7 us; the launch traced here: 31.4 us
  Pallas kernels  20.7 us (65%)
  starting transfers between devices  6.89 us (22%)
  local copies, waits for them, and re-layouts  1.96 us (6%)
  other arithmetic  1.33 us (4%)
  waiting for transfers between devices  0.4 us (1%)
    pallas_call x2, Pallas kernels, run_slices(): pl.pallas_call(functools.partial(slices_kernel, field_x=float(field_x), c...  20.7 us
    ppermute x1, starting transfers between devices, shards(): lax.ppermute(packs[2], 'lat', [(i, (i + 1) % n_lat) for i in range(n_lat)])  3.1 us
    ppermute x1, starting transfers between devices, shards(): lax.ppermute(packs[0], 'lat', [((i + 1) % n_lat, i) for i in range(n_lat)])  2.09 us
    unnamed x14, local copies, waits for them, and re-layouts  1.95 us
    ppermute x1, starting transfers between devices, shards(): lax.ppermute(local, 'slc', [(i, (i - hop) % owners) for i in range(owners)])  1.69 us
    convert_element_type x1, other arithmetic, shards(): marg = jnp.transpose(margin[0, 0, :, 0], (1, 0, 2)).astype(f32)  0.71 us
  transfers between devices with their start and end apart: 3, of which 1 were waited for; matrix products, arithmetic and copies ran while one was open for 2% of the time, Pallas kernels for 32%

profile of v7, /device:TPU:0, one launch (start us, length us, event | category | flops | bytes accessed | tf_op | source)
XLA Modules:
  0.0 31.4 jit_solution(13979848661344846611)
XLA Ops:
  0.0 0.0 copy-start.2
  0.0 0.0 copy-start.3
  0.0 0.7 %fusion = f32[3,2,128]{2,1,0:T(2,128)S(1)} fusion(s32[1,1,2,1,3,128]{5,3,4,2,1,0:T(1,128)} %param.19), kind=kLoop, calls=%fused_computation.7 | loop fusion | flops 768 | bytes 6144 | tf_op jit(solution)/shard_map/convert_element_type | solution.py:284
  0.7 0.0 copy-done.2
  0.7 0.0 copy-done.3
  0.7 0.0 copy-start.1
  0.7 0.7 %copy-done.1 = f32[1,1,2,256]{3,2,1,0:T(2,128)S(1)} copy-done((f32[1,1,2,256]{3,2,1,0:T(2,128)S(1)}, f32[1,1,2,256]{3,2,1,0:T(2,128)}, u32[]{:S(2)}) %copy-start.1) | copy-done | bytes 2072
  1.5 0.0 copy-start.6
  1.5 3.1 %collective-permute-start = (f32[6,256]{1,0:T(8,128)S(1)}, f32[6,256]{1,0:T(8,128)S(1)}, u32[]{:S(2)}, u32[]{:S(2)}) collective-permute-start(f32[6,256]{1,0:T(8,128)S(1)} %get-tuple-element.5), channel_id=1, source_target_pairs={{0,4},{4,8},{8,12},{12,0},{1,5},{5,9},{9,13},{13,1},{2,6},{6,10},{... | collective-permute-start | bytes 18440 | tf_op jit(solution)/shard_map/ppermute | solution.py:287
  4.6 2.1 %collective-permute-start.1 = (f32[6,256]{1,0:T(8,128)S(1)}, f32[6,256]{1,0:T(8,128)S(1)}, u32[]{:S(2)}, u32[]{:S(2)}) collective-permute-start(f32[6,256]{1,0:T(8,128)S(1)} %get-tuple-element.6), channel_id=1, source_target_pairs={{4,0},{8,4},{12,8},{0,12},{5,1},{9,5},{13,9},{1,13},{6,2},{10,6},{... | collective-permute-start | bytes 18440 | tf_op jit(solution)/shard_map/ppermute | solution.py:288
  6.7 0.0 copy-done.6
  6.7 0.0 copy-start.4
  6.7 0.7 %copy-done.4 = f32[8]{0:T(128)S(1)} copy-done((f32[8]{0:T(128)S(1)}, f32[8]{0:T(128)}, u32[]{:S(2)}) %copy-start.4) | copy-done | bytes 56
  7.3 0.6 %pad_maximum_fusion.1.refs_2_ = f32[2,8]{1,0:T(2,128)} fusion(f32[1,8]{1,0:T(1,128)S(1)} %divide_bitcast_fusion, f32[1,8]{1,0:T(1,128)S(1)} %bitcast.24), kind=kLoop, calls=%fused_computation.8 | loop fusion | flops 16 | bytes 128 | tf_op jit(solution)/shard_map/stack | solution.py:296
  7.9 0.4 %collective-permute-done = f32[6,256]{1,0:T(8,128)S(1)} collective-permute-done((f32[6,256]{1,0:T(8,128)S(1)}, f32[6,256]{1,0:T(8,128)S(1)}, u32[]{:S(2)}, u32[]{:S(2)}) %collective-permute-start) | collective-permute-done | bytes 6176 | tf_op jit(solution)/shard_map/ppermute | solution.py:287
  8.3 0.0 collective-permute-done.1
  8.3 0.0 copy-start
  8.3 1.7 %collective-permute-start.2 = (f32[1,3,6,256]{3,2,1,0:T(8,128)S(1)}, f32[1,3,6,256]{3,2,1,0:T(8,128)S(1)}, u32[]{:S(2)}, u32[]{:S(2)}) collective-permute-start(f32[1,3,6,256]{3,2,1,0:T(8,128)S(1)} %maximum_bitcast_fusion.refs_3_), channel_id=1, source_target_pairs={{0,2},{2,0},{1,3},{3,1},{4,6},{6,4},{5,7},{7,5},{8,10},{10,8},{9,1... | collective-permute-start | bytes 55304 | tf_op jit(solution)/shard_map/ppermute | solution.py:293
  10.0 0.0 copy-done
  10.0 10.2 %shard_map.136.refs_7_ = bf16[2,256,512]{2,1,0:T(8,128)(2,1)} custom-call(s32[2,2]{1,0:T(2,128)} %refs_0_.3, s32[1]{0:T(128)} %bitcast.refs_1_, f32[2,8]{1,0:T(2,128)} %pad_maximum_fusion.1.refs_2_, f32[1,3,6,256]{3,2,1,0:T(8,128)} %copy-done, bf16[512,512]{1,0:T(8,128)(2,1)} %constant.17.clone.refs_4_, bf16[512,512]{1,0:T(8,128)(2,1)} %constant.18.clone.refs_5_, ...), custom_call_target="tpu_custom_call" | custom-call | flops 2348810240 | bytes 2359296 | tf_op jit(solution)/shard_map/pallas_call | solution.py:236
  20.2 0.0 collective-permute-done.2.refs_3_
  20.2 0.0 copy-start.5
  20.2 0.6 %copy-done.5 = f32[1,3,6,256]{3,2,1,0:T(8,128)} copy-done((f32[1,3,6,256]{3,2,1,0:T(8,128)}, f32[1,3,6,256]{3,2,1,0:T(8,128)S(1)}, u32[]{:S(2)}) %copy-start.5) | copy-done | bytes 18456
  20.8 10.5 %shard_map.137 = bf16[2,256,2,256]{3,2,1,0:T(2,128)(2,1)} custom-call(s32[2,2]{1,0:T(2,128)} %refs_0_.3, s32[1]{0:T(128)} %bitcast.refs_1_, f32[2,8]{1,0:T(2,128)} %pad_maximum_fusion.1.refs_2_, f32[1,3,6,256]{3,2,1,0:T(8,128)} %copy-done.5, bf16[512,512]{1,0:T(8,128)(2,1)} %constant.17.clone.refs_4_, bf16[512,512]{1,0:T(8,128)(2,1)} %constant.18.clone.refs_5_, ...), custom_call_target="tpu_custom_call" | custom-call | flops 2348810240 | bytes 2359296 | tf_op jit(solution)/shard_map/pallas_call | solution.py:236
  (7 shorter events, 0.0 us)
Async XLA Ops:
  0.0 0.7 %copy-start.2 = (s32[1,1,256]{2,1,0:T(1,128)S(1)}, s32[1,1,256]{2,1,0:T(1,128)}, u32[]{:S(2)}) copy-start(s32[1,1,256]{2,1,0:T(1,128)} %param.16) | copy-start | bytes 3076
  0.0 0.7 %copy-start.3 = (s32[1,1,256]{2,1,0:T(1,128)S(1)}, s32[1,1,256]{2,1,0:T(1,128)}, u32[]{:S(2)}) copy-start(s32[1,1,256]{2,1,0:T(1,128)} %param.15) | copy-start | bytes 3076
  0.7 0.7 %copy-start.1 = (f32[1,1,2,256]{3,2,1,0:T(2,128)S(1)}, f32[1,1,2,256]{3,2,1,0:T(2,128)}, u32[]{:S(2)}) copy-start(f32[1,1,2,256]{3,2,1,0:T(2,128)} %param.14) | copy-start | bytes 6148
  1.5 5.2 %copy-start.6 = (f32[8]{0:T(128)S(1)}, f32[8]{0:T(128)}, u32[]{:S(2)}) copy-start(f32[8]{0:T(128)} %param.18) | copy-start | bytes 100
  1.5 6.8 %collective-permute-start = (f32[6,256]{1,0:T(8,128)S(1)}, f32[6,256]{1,0:T(8,128)S(1)}, u32[]{:S(2)}, u32[]{:S(2)}) collective-permute-start(f32[6,256]{1,0:T(8,128)S(1)} %get-tuple-element.5), channel_id=1, source_target_pairs={{0,4},{4,8},{8,12},{12,0},{1,5},{5,9},{9,13},{13,1},{2,6},{6,10},{... | collective-permute-start | bytes 18440 | tf_op jit(solution)/shard_map/ppermute | solution.py:287
  4.6 3.7 %collective-permute-start.1 = (f32[6,256]{1,0:T(8,128)S(1)}, f32[6,256]{1,0:T(8,128)S(1)}, u32[]{:S(2)}, u32[]{:S(2)}) collective-permute-start(f32[6,256]{1,0:T(8,128)S(1)} %get-tuple-element.6), channel_id=1, source_target_pairs={{4,0},{8,4},{12,8},{0,12},{5,1},{9,5},{13,9},{1,13},{6,2},{10,6},{... | collective-permute-start | bytes 18440 | tf_op jit(solution)/shard_map/ppermute | solution.py:288
  6.7 0.7 %copy-start.4 = (f32[8]{0:T(128)S(1)}, f32[8]{0:T(128)}, u32[]{:S(2)}) copy-start(f32[8]{0:T(128)} %param.17) | copy-start | bytes 100
  8.3 1.7 %copy-start = (f32[1,3,6,256]{3,2,1,0:T(8,128)}, f32[1,3,6,256]{3,2,1,0:T(8,128)S(1)}, u32[]{:S(2)}) copy-start(f32[1,3,6,256]{3,2,1,0:T(8,128)S(1)} %maximum_bitcast_fusion.refs_3_) | copy-start | bytes 55300
  8.3 11.9 %collective-permute-start.2 = (f32[1,3,6,256]{3,2,1,0:T(8,128)S(1)}, f32[1,3,6,256]{3,2,1,0:T(8,128)S(1)}, u32[]{:S(2)}, u32[]{:S(2)}) collective-permute-start(f32[1,3,6,256]{3,2,1,0:T(8,128)S(1)} %maximum_bitcast_fusion.refs_3_), channel_id=1, source_target_pairs={{0,2},{2,0},{1,3},{3,1},{4,6},{6,4},{5,7},{7,5},{8,10},{10,8},{9,1... | collective-permute-start | bytes 55304 | tf_op jit(solution)/shard_map/ppermute | solution.py:293
  20.2 0.6 %copy-start.5 = (f32[1,3,6,256]{3,2,1,0:T(8,128)}, f32[1,3,6,256]{3,2,1,0:T(8,128)S(1)}, u32[]{:S(2)}) copy-start(f32[1,3,6,256]{3,2,1,0:T(8,128)S(1)} %collective-permute-done.2.refs_3_) | copy-start | bytes 55300

commit v8 on v7

--- a/solution.py
+++ b/solution.py
@@ -163,11 +163,11 @@
         inverse_col = cols[:, 2:3]
         pixel_col = lax.broadcasted_iota(jnp.int32, (w, 1), 0).astype(f32)
         pixel_row = lax.broadcasted_iota(jnp.int32, (1, w), 1).astype(f32)
+        shift_x = pos_ref[0, 0].astype(f32)
+        dist_x = wrap(atom_x - shift_x - pixel_col + 0.5 * field_x, field_x) - 0.5 * field_x
+        across = jnp.exp(-dist_x * dist_x * inverse_row).astype(bf16)
         for p in range(batch):
-            shift_x = pos_ref[p, 0].astype(f32)
             shift_y = pos_ref[p, 1].astype(f32)
-            dist_x = wrap(atom_x - shift_x - pixel_col + 0.5 * field_x, field_x) - 0.5 * field_x
-            across = jnp.exp(-dist_x * dist_x * inverse_row).astype(bf16)
             dist_y = wrap(atom_y - shift_y - pixel_row + 0.5 * w, w) - 0.5 * w
             along = jnp.exp(-dist_y * dist_y * inverse_col)
             weighted = jnp.concatenate(
@@ -191,6 +191,7 @@
     pr = prop_ref[0]
     pi = prop_ref[1]
     column = pl.ds(pl.multiple_of(layer * w, w), w)
+    transmitted = []
     for p in range(batch):
         psi = wave_ref[p]
         wr = psi[:, :w].astype(f32)
@@ -199,16 +200,19 @@
         sv, cv = sincos(v)
         tr = (wr * cv - wi * sv).astype(bf16)
         ti = (wr * sv + wi * cv).astype(bf16)
-        rw = dot(jnp.concatenate([tr, ti], 1), a_ref[...]).astype(bf16)
-        sp = dot(b_ref[...], jnp.concatenate([rw[:, :w], rw[:, w:]], 0))
+        transmitted.append(jnp.concatenate([tr, ti], 1))
+    rowwise = [dot(t, a_ref[...]).astype(bf16) for t in transmitted]
+    spectra = [dot(b_ref[...], jnp.concatenate([rw[:, :w], rw[:, w:]], 0)) for rw in rowwise]
+    propagated = []
+    for sp in spectra:
         sr = sp[:w]
         si = sp[w:]
-        spb = jnp.concatenate(
-            [(sr * pr - si * pi).astype(bf16), (sr * pi + si * pr).astype(bf16)], 0
+        propagated.append(
+            jnp.concatenate([(sr * pr - si * pi).astype(bf16), (sr * pi + si * pr).astype(bf16)], 0)
         )
-        br = dot(a_ref[...], spb).astype(bf16)
-        psi = dot(jnp.concatenate([br[:w], br[w:]], 1), b_ref[...]).astype(bf16)
-        wave_ref[p] = psi
+    back = [dot(a_ref[...], spb).astype(bf16) for spb in propagated]
+    for p, br in enumerate(back):
+        wave_ref[p] = dot(jnp.concatenate([br[:w], br[w:]], 1), b_ref[...]).astype(bf16)
 
     @pl.when((hop == pl.num_programs(0) - 1) & (layer == pl.num_programs(1) - 1))
     def _():

time: 31.7 us -> 28.8 us (0.909)
  Pallas kernels: 20.7 us -> 17.7 us
    pallas_call x2, Pallas kernels: 20.7 us -> 17.7 us  [run_slices(): pl.pallas_call(functools.partial(slices_kernel, field_x=float(field_x), c...]
  transfers between devices with their start and end apart: 3 -> 3, of which waited for: 1 -> 1; matrix products, arithmetic and copies ran while one was open for 2% -> 2% of each run, Pallas kernels for 32% -> 31%
where the time goes in v8:
time: 28.8 us; the launch traced here: 28.4 us
  Pallas kernels  17.7 us (61%)
  starting transfers between devices  6.89 us (24%)
  local copies, waits for them, and re-layouts  1.96 us (7%)
  other arithmetic  1.33 us (5%)
  waiting for transfers between devices  0.4 us (1%)
    pallas_call x2, Pallas kernels, run_slices(): pl.pallas_call(functools.partial(slices_kernel, field_x=float(field_x), c...  17.7 us
    ppermute x1, starting transfers between devices, shards(): lax.ppermute(packs[2], 'lat', [(i, (i + 1) % n_lat) for i in range(n_lat)])  3.1 us
    ppermute x1, starting transfers between devices, shards(): lax.ppermute(packs[0], 'lat', [((i + 1) % n_lat, i) for i in range(n_lat)])  2.09 us
    unnamed x14, local copies, waits for them, and re-layouts  1.95 us
    ppermute x1, starting transfers between devices, shards(): lax.ppermute(local, 'slc', [(i, (i - hop) % owners) for i in range(owners)])  1.69 us
    convert_element_type x1, other arithmetic, shards(): marg = jnp.transpose(margin[0, 0, :, 0], (1, 0, 2)).astype(f32)  0.71 us
    another operation x2, other arithmetic, shards(): table = jnp.stack([species_amp, 0.5 / (species_spread * species_spread)], 0)  0.59 us
  transfers between devices with their start and end apart: 3, of which 1 were waited for; matrix products, arithmetic and copies ran while one was open for 2% of the time, Pallas kernels for 31%

profile of v8, /device:TPU:0, one launch (start us, length us, event | category | flops | bytes accessed | tf_op | source)
XLA Modules:
  0.0 28.4 jit_solution(6797946099868806514)
XLA Ops:
  0.0 0.0 copy-start.2
  0.0 0.0 copy-start.3
  0.0 0.7 %fusion = f32[3,2,128]{2,1,0:T(2,128)S(1)} fusion(s32[1,1,2,1,3,128]{5,3,4,2,1,0:T(1,128)} %param.19), kind=kLoop, calls=%fused_computation.7 | loop fusion | flops 768 | bytes 6144 | tf_op jit(solution)/shard_map/convert_element_type | solution.py:288
  0.7 0.0 copy-done.2
  0.7 0.0 copy-done.3
  0.7 0.0 copy-start.1
  0.7 0.7 %copy-done.1 = f32[1,1,2,256]{3,2,1,0:T(2,128)S(1)} copy-done((f32[1,1,2,256]{3,2,1,0:T(2,128)S(1)}, f32[1,1,2,256]{3,2,1,0:T(2,128)}, u32[]{:S(2)}) %copy-start.1) | copy-done | bytes 2072
  1.5 0.0 copy-start.6
  1.5 3.1 %collective-permute-start = (f32[6,256]{1,0:T(8,128)S(1)}, f32[6,256]{1,0:T(8,128)S(1)}, u32[]{:S(2)}, u32[]{:S(2)}) collective-permute-start(f32[6,256]{1,0:T(8,128)S(1)} %get-tuple-element.5), channel_id=1, source_target_pairs={{0,4},{4,8},{8,12},{12,0},{1,5},{5,9},{9,13},{13,1},{2,6},{6,10},{... | collective-permute-start | bytes 18440 | tf_op jit(solution)/shard_map/ppermute | solution.py:291
  4.6 2.1 %collective-permute-start.1 = (f32[6,256]{1,0:T(8,128)S(1)}, f32[6,256]{1,0:T(8,128)S(1)}, u32[]{:S(2)}, u32[]{:S(2)}) collective-permute-start(f32[6,256]{1,0:T(8,128)S(1)} %get-tuple-element.6), channel_id=1, source_target_pairs={{4,0},{8,4},{12,8},{0,12},{5,1},{9,5},{13,9},{1,13},{6,2},{10,6},{... | collective-permute-start | bytes 18440 | tf_op jit(solution)/shard_map/ppermute | solution.py:292
  6.7 0.0 copy-done.6
  6.7 0.0 copy-start.4
  6.7 0.7 %copy-done.4 = f32[8]{0:T(128)S(1)} copy-done((f32[8]{0:T(128)S(1)}, f32[8]{0:T(128)}, u32[]{:S(2)}) %copy-start.4) | copy-done | bytes 56
  7.3 0.6 %pad_maximum_fusion.1.refs_2_ = f32[2,8]{1,0:T(2,128)} fusion(f32[1,8]{1,0:T(1,128)S(1)} %divide_bitcast_fusion, f32[1,8]{1,0:T(1,128)S(1)} %bitcast.24), kind=kLoop, calls=%fused_computation.8 | loop fusion | flops 16 | bytes 128 | tf_op jit(solution)/shard_map/stack | solution.py:300
  7.9 0.4 %collective-permute-done = f32[6,256]{1,0:T(8,128)S(1)} collective-permute-done((f32[6,256]{1,0:T(8,128)S(1)}, f32[6,256]{1,0:T(8,128)S(1)}, u32[]{:S(2)}, u32[]{:S(2)}) %collective-permute-start) | collective-permute-done | bytes 6176 | tf_op jit(solution)/shard_map/ppermute | solution.py:291
  8.3 0.0 collective-permute-done.1
  8.3 0.0 copy-start
  8.3 1.7 %collective-permute-start.2 = (f32[1,3,6,256]{3,2,1,0:T(8,128)S(1)}, f32[1,3,6,256]{3,2,1,0:T(8,128)S(1)}, u32[]{:S(2)}, u32[]{:S(2)}) collective-permute-start(f32[1,3,6,256]{3,2,1,0:T(8,128)S(1)} %maximum_bitcast_fusion.refs_3_), channel_id=1, source_target_pairs={{0,2},{2,0},{1,3},{3,1},{4,6},{6,4},{5,7},{7,5},{8,10},{10,8},{9,1... | collective-permute-start | bytes 55304 | tf_op jit(solution)/shard_map/ppermute | solution.py:297
  10.0 0.0 copy-done
  10.0 8.7 %shard_map.136.refs_7_ = bf16[2,256,512]{2,1,0:T(8,128)(2,1)} custom-call(s32[2,2]{1,0:T(2,128)} %refs_0_.3, s32[1]{0:T(128)} %bitcast.refs_1_, f32[2,8]{1,0:T(2,128)} %pad_maximum_fusion.1.refs_2_, f32[1,3,6,256]{3,2,1,0:T(8,128)} %copy-done, bf16[512,512]{1,0:T(8,128)(2,1)} %constant.17.clone.refs_4_, bf16[512,512]{1,0:T(8,128)(2,1)} %constant.18.clone.refs_5_, ...), custom_call_target="tpu_custom_call" | custom-call | flops 2348810240 | bytes 2359296 | tf_op jit(solution)/shard_map/pallas_call | solution.py:240
  18.7 0.0 collective-permute-done.2.refs_3_
  18.7 0.0 copy-start.5
  18.7 0.6 %copy-done.5 = f32[1,3,6,256]{3,2,1,0:T(8,128)} copy-done((f32[1,3,6,256]{3,2,1,0:T(8,128)}, f32[1,3,6,256]{3,2,1,0:T(8,128)S(1)}, u32[]{:S(2)}) %copy-start.5) | copy-done | bytes 18456
  19.3 9.1 %shard_map.137 = bf16[2,256,2,256]{3,2,1,0:T(2,128)(2,1)} custom-call(s32[2,2]{1,0:T(2,128)} %refs_0_.3, s32[1]{0:T(128)} %bitcast.refs_1_, f32[2,8]{1,0:T(2,128)} %pad_maximum_fusion.1.refs_2_, f32[1,3,6,256]{3,2,1,0:T(8,128)} %copy-done.5, bf16[512,512]{1,0:T(8,128)(2,1)} %constant.17.clone.refs_4_, bf16[512,512]{1,0:T(8,128)(2,1)} %constant.18.clone.refs_5_, ...), custom_call_target="tpu_custom_call" | custom-call | flops 2348810240 | bytes 2359296 | tf_op jit(solution)/shard_map/pallas_call | solution.py:240
  (7 shorter events, 0.0 us)
Async XLA Ops:
  0.0 0.7 %copy-start.2 = (s32[1,1,256]{2,1,0:T(1,128)S(1)}, s32[1,1,256]{2,1,0:T(1,128)}, u32[]{:S(2)}) copy-start(s32[1,1,256]{2,1,0:T(1,128)} %param.16) | copy-start | bytes 3076
  0.0 0.7 %copy-start.3 = (s32[1,1,256]{2,1,0:T(1,128)S(1)}, s32[1,1,256]{2,1,0:T(1,128)}, u32[]{:S(2)}) copy-start(s32[1,1,256]{2,1,0:T(1,128)} %param.15) | copy-start | bytes 3076
  0.7 0.7 %copy-start.1 = (f32[1,1,2,256]{3,2,1,0:T(2,128)S(1)}, f32[1,1,2,256]{3,2,1,0:T(2,128)}, u32[]{:S(2)}) copy-start(f32[1,1,2,256]{3,2,1,0:T(2,128)} %param.14) | copy-start | bytes 6148
  1.5 5.2 %copy-start.6 = (f32[8]{0:T(128)S(1)}, f32[8]{0:T(128)}, u32[]{:S(2)}) copy-start(f32[8]{0:T(128)} %param.18) | copy-start | bytes 100
  1.5 6.8 %collective-permute-start = (f32[6,256]{1,0:T(8,128)S(1)}, f32[6,256]{1,0:T(8,128)S(1)}, u32[]{:S(2)}, u32[]{:S(2)}) collective-permute-start(f32[6,256]{1,0:T(8,128)S(1)} %get-tuple-element.5), channel_id=1, source_target_pairs={{0,4},{4,8},{8,12},{12,0},{1,5},{5,9},{9,13},{13,1},{2,6},{6,10},{... | collective-permute-start | bytes 18440 | tf_op jit(solution)/shard_map/ppermute | solution.py:291
  4.6 3.7 %collective-permute-start.1 = (f32[6,256]{1,0:T(8,128)S(1)}, f32[6,256]{1,0:T(8,128)S(1)}, u32[]{:S(2)}, u32[]{:S(2)}) collective-permute-start(f32[6,256]{1,0:T(8,128)S(1)} %get-tuple-element.6), channel_id=1, source_target_pairs={{4,0},{8,4},{12,8},{0,12},{5,1},{9,5},{13,9},{1,13},{6,2},{10,6},{... | collective-permute-start | bytes 18440 | tf_op jit(solution)/shard_map/ppermute | solution.py:292
  6.7 0.7 %copy-start.4 = (f32[8]{0:T(128)S(1)}, f32[8]{0:T(128)}, u32[]{:S(2)}) copy-start(f32[8]{0:T(128)} %param.17) | copy-start | bytes 100
  8.3 1.7 %copy-start = (f32[1,3,6,256]{3,2,1,0:T(8,128)}, f32[1,3,6,256]{3,2,1,0:T(8,128)S(1)}, u32[]{:S(2)}) copy-start(f32[1,3,6,256]{3,2,1,0:T(8,128)S(1)} %maximum_bitcast_fusion.refs_3_) | copy-start | bytes 55300
  8.3 10.4 %collective-permute-start.2 = (f32[1,3,6,256]{3,2,1,0:T(8,128)S(1)}, f32[1,3,6,256]{3,2,1,0:T(8,128)S(1)}, u32[]{:S(2)}, u32[]{:S(2)}) collective-permute-start(f32[1,3,6,256]{3,2,1,0:T(8,128)S(1)} %maximum_bitcast_fusion.refs_3_), channel_id=1, source_target_pairs={{0,2},{2,0},{1,3},{3,1},{4,6},{6,4},{5,7},{7,5},{8,10},{10,8},{9,1... | collective-permute-start | bytes 55304 | tf_op jit(solution)/shard_map/ppermute | solution.py:297
  18.7 0.6 %copy-start.5 = (f32[1,3,6,256]{3,2,1,0:T(8,128)}, f32[1,3,6,256]{3,2,1,0:T(8,128)S(1)}, u32[]{:S(2)}) copy-start(f32[1,3,6,256]{3,2,1,0:T(8,128)S(1)} %collective-permute-done.2.refs_3_) | copy-start | bytes 55300

commit v9 on v8

--- a/solution.py
+++ b/solution.py
@@ -201,18 +201,33 @@
         tr = (wr * cv - wi * sv).astype(bf16)
         ti = (wr * sv + wi * cv).astype(bf16)
         transmitted.append(jnp.concatenate([tr, ti], 1))
-    rowwise = [dot(t, a_ref[...]).astype(bf16) for t in transmitted]
-    spectra = [dot(b_ref[...], jnp.concatenate([rw[:, :w], rw[:, w:]], 0)) for rw in rowwise]
-    propagated = []
-    for sp in spectra:
-        sr = sp[:w]
-        si = sp[w:]
-        propagated.append(
-            jnp.concatenate([(sr * pr - si * pi).astype(bf16), (sr * pi + si * pr).astype(bf16)], 0)
-        )
-    back = [dot(a_ref[...], spb).astype(bf16) for spb in propagated]
-    for p, br in enumerate(back):
-        wave_ref[p] = dot(jnp.concatenate([br[:w], br[w:]], 1), b_ref[...]).astype(bf16)
+    rowwise = dot(jnp.concatenate(transmitted, 0), a_ref[...]).astype(bf16)
+    planar = jnp.concatenate(
+        [
+            jnp.concatenate([rowwise[p * w:(p + 1) * w, :w], rowwise[p * w:(p + 1) * w, w:]], 0)
+            for p in range(batch)
+        ],
+        1,
+    )
+    spectra = dot(b_ref[...], planar)
+    sr = spectra[:w]
+    si = spectra[w:]
+    prb = jnp.concatenate([pr] * batch, 1)
+    pib = jnp.concatenate([pi] * batch, 1)
+    propagated = jnp.concatenate(
+        [(sr * prb - si * pib).astype(bf16), (sr * pib + si * prb).astype(bf16)], 0
+    )
+    back = dot(a_ref[...], propagated).astype(bf16)
+    columns = jnp.concatenate(
+        [
+            jnp.concatenate([back[:w, p * w:(p + 1) * w], back[w:, p * w:(p + 1) * w]], 1)
+            for p in range(batch)
+        ],
+        0,
+    )
+    waves = dot(columns, b_ref[...]).astype(bf16)
+    for p in range(batch):
+        wave_ref[p] = waves[p * w:(p + 1) * w]
 
     @pl.when((hop == pl.num_programs(0) - 1) & (layer == pl.num_programs(1) - 1))
     def _():

time: 28.8 us -> 28.8 us (level)
  no operation moved by 1% of the time
where the time goes in v9:
time: 28.8 us; the launch traced here: 28.4 us
  Pallas kernels  17.8 us (62%)
  starting transfers between devices  6.89 us (24%)
  local copies, waits for them, and re-layouts  1.96 us (7%)
  other arithmetic  1.33 us (5%)
  waiting for transfers between devices  0.4 us (1%)
    pallas_call x2, Pallas kernels, run_slices(): pl.pallas_call(functools.partial(slices_kernel, field_x=float(field_x), c...  17.8 us
    ppermute x1, starting transfers between devices, shards(): lax.ppermute(packs[2], 'lat', [(i, (i + 1) % n_lat) for i in range(n_lat)])  3.1 us
    ppermute x1, starting transfers between devices, shards(): lax.ppermute(packs[0], 'lat', [((i + 1) % n_lat, i) for i in range(n_lat)])  2.09 us
    unnamed x14, local copies, waits for them, and re-layouts  1.95 us
    ppermute x1, starting transfers between devices, shards(): lax.ppermute(local, 'slc', [(i, (i - hop) % owners) for i in range(owners)])  1.69 us
    convert_element_type x1, other arithmetic, shards(): marg = jnp.transpose(margin[0, 0, :, 0], (1, 0, 2)).astype(f32)  0.71 us
    another operation x2, other arithmetic, shards(): table = jnp.stack([species_amp, 0.5 / (species_spread * species_spread)], 0)  0.59 us
  transfers between devices with their start and end apart: 3, of which 1 were waited for; matrix products, arithmetic and copies ran while one was open for 2% of the time, Pallas kernels for 31%

profile of v9, /device:TPU:0, one launch (start us, length us, event | category | flops | bytes accessed | tf_op | source)
XLA Modules:
  0.0 28.4 jit_solution(10521888987266882308)
XLA Ops:
  0.0 0.0 copy-start.2
  0.0 0.0 copy-start.3
  0.0 0.7 %fusion = f32[3,2,128]{2,1,0:T(2,128)S(1)} fusion(s32[1,1,2,1,3,128]{5,3,4,2,1,0:T(1,128)} %param.19), kind=kLoop, calls=%fused_computation.7 | loop fusion | flops 768 | bytes 6144 | tf_op jit(solution)/shard_map/convert_element_type | solution.py:303
  0.7 0.0 copy-done.2
  0.7 0.0 copy-done.3
  0.7 0.0 copy-start.1
  0.7 0.7 %copy-done.1 = f32[1,1,2,256]{3,2,1,0:T(2,128)S(1)} copy-done((f32[1,1,2,256]{3,2,1,0:T(2,128)S(1)}, f32[1,1,2,256]{3,2,1,0:T(2,128)}, u32[]{:S(2)}) %copy-start.1) | copy-done | bytes 2072
  1.5 0.0 copy-start.6
  1.5 3.1 %collective-permute-start = (f32[6,256]{1,0:T(8,128)S(1)}, f32[6,256]{1,0:T(8,128)S(1)}, u32[]{:S(2)}, u32[]{:S(2)}) collective-permute-start(f32[6,256]{1,0:T(8,128)S(1)} %get-tuple-element.5), channel_id=1, source_target_pairs={{0,4},{4,8},{8,12},{12,0},{1,5},{5,9},{9,13},{13,1},{2,6},{6,10},{... | collective-permute-start | bytes 18440 | tf_op jit(solution)/shard_map/ppermute | solution.py:306
  4.6 2.1 %collective-permute-start.1 = (f32[6,256]{1,0:T(8,128)S(1)}, f32[6,256]{1,0:T(8,128)S(1)}, u32[]{:S(2)}, u32[]{:S(2)}) collective-permute-start(f32[6,256]{1,0:T(8,128)S(1)} %get-tuple-element.6), channel_id=1, source_target_pairs={{4,0},{8,4},{12,8},{0,12},{5,1},{9,5},{13,9},{1,13},{6,2},{10,6},{... | collective-permute-start | bytes 18440 | tf_op jit(solution)/shard_map/ppermute | solution.py:307
  6.7 0.0 copy-done.6
  6.7 0.0 copy-start.4
  6.7 0.7 %copy-done.4 = f32[8]{0:T(128)S(1)} copy-done((f32[8]{0:T(128)S(1)}, f32[8]{0:T(128)}, u32[]{:S(2)}) %copy-start.4) | copy-done | bytes 56
  7.3 0.6 %pad_maximum_fusion.1.refs_2_ = f32[2,8]{1,0:T(2,128)} fusion(f32[1,8]{1,0:T(1,128)S(1)} %divide_bitcast_fusion, f32[1,8]{1,0:T(1,128)S(1)} %bitcast.24), kind=kLoop, calls=%fused_computation.8 | loop fusion | flops 16 | bytes 128 | tf_op jit(solution)/shard_map/stack | solution.py:315
  7.9 0.4 %collective-permute-done = f32[6,256]{1,0:T(8,128)S(1)} collective-permute-done((f32[6,256]{1,0:T(8,128)S(1)}, f32[6,256]{1,0:T(8,128)S(1)}, u32[]{:S(2)}, u32[]{:S(2)}) %collective-permute-start) | collective-permute-done | bytes 6176 | tf_op jit(solution)/shard_map/ppermute | solution.py:306
  8.3 0.0 collective-permute-done.1
  8.3 0.0 copy-start
  8.3 1.7 %collective-permute-start.2 = (f32[1,3,6,256]{3,2,1,0:T(8,128)S(1)}, f32[1,3,6,256]{3,2,1,0:T(8,128)S(1)}, u32[]{:S(2)}, u32[]{:S(2)}) collective-permute-start(f32[1,3,6,256]{3,2,1,0:T(8,128)S(1)} %maximum_bitcast_fusion.refs_3_), channel_id=1, source_target_pairs={{0,2},{2,0},{1,3},{3,1},{4,6},{6,4},{5,7},{7,5},{8,10},{10,8},{9,1... | collective-permute-start | bytes 55304 | tf_op jit(solution)/shard_map/ppermute | solution.py:312
  10.0 0.0 copy-done
  10.0 8.7 %shard_map.136.refs_7_ = bf16[2,256,512]{2,1,0:T(8,128)(2,1)} custom-call(s32[2,2]{1,0:T(2,128)} %refs_0_.3, s32[1]{0:T(128)} %bitcast.refs_1_, f32[2,8]{1,0:T(2,128)} %pad_maximum_fusion.1.refs_2_, f32[1,3,6,256]{3,2,1,0:T(8,128)} %copy-done, bf16[512,512]{1,0:T(8,128)(2,1)} %constant.17.clone.refs_4_, bf16[512,512]{1,0:T(8,128)(2,1)} %constant.18.clone.refs_5_, ...), custom_call_target="tpu_custom_call" | custom-call | flops 2348810240 | bytes 2359296 | tf_op jit(solution)/shard_map/pallas_call | solution.py:255
  18.7 0.0 collective-permute-done.2.refs_3_
  18.8 0.0 copy-start.5
  18.8 0.6 %copy-done.5 = f32[1,3,6,256]{3,2,1,0:T(8,128)} copy-done((f32[1,3,6,256]{3,2,1,0:T(8,128)}, f32[1,3,6,256]{3,2,1,0:T(8,128)S(1)}, u32[]{:S(2)}) %copy-start.5) | copy-done | bytes 18456
  19.4 9.1 %shard_map.137 = bf16[2,256,2,256]{3,2,1,0:T(2,128)(2,1)} custom-call(s32[2,2]{1,0:T(2,128)} %refs_0_.3, s32[1]{0:T(128)} %bitcast.refs_1_, f32[2,8]{1,0:T(2,128)} %pad_maximum_fusion.1.refs_2_, f32[1,3,6,256]{3,2,1,0:T(8,128)} %copy-done.5, bf16[512,512]{1,0:T(8,128)(2,1)} %constant.17.clone.refs_4_, bf16[512,512]{1,0:T(8,128)(2,1)} %constant.18.clone.refs_5_, ...), custom_call_target="tpu_custom_call" | custom-call | flops 2348810240 | bytes 2359296 | tf_op jit(solution)/shard_map/pallas_call | solution.py:255
  (7 shorter events, 0.0 us)
Async XLA Ops:
  0.0 0.7 %copy-start.2 = (s32[1,1,256]{2,1,0:T(1,128)S(1)}, s32[1,1,256]{2,1,0:T(1,128)}, u32[]{:S(2)}) copy-start(s32[1,1,256]{2,1,0:T(1,128)} %param.16) | copy-start | bytes 3076
  0.0 0.7 %copy-start.3 = (s32[1,1,256]{2,1,0:T(1,128)S(1)}, s32[1,1,256]{2,1,0:T(1,128)}, u32[]{:S(2)}) copy-start(s32[1,1,256]{2,1,0:T(1,128)} %param.15) | copy-start | bytes 3076
  0.7 0.7 %copy-start.1 = (f32[1,1,2,256]{3,2,1,0:T(2,128)S(1)}, f32[1,1,2,256]{3,2,1,0:T(2,128)}, u32[]{:S(2)}) copy-start(f32[1,1,2,256]{3,2,1,0:T(2,128)} %param.14) | copy-start | bytes 6148
  1.5 5.2 %copy-start.6 = (f32[8]{0:T(128)S(1)}, f32[8]{0:T(128)}, u32[]{:S(2)}) copy-start(f32[8]{0:T(128)} %param.18) | copy-start | bytes 100
  1.5 6.8 %collective-permute-start = (f32[6,256]{1,0:T(8,128)S(1)}, f32[6,256]{1,0:T(8,128)S(1)}, u32[]{:S(2)}, u32[]{:S(2)}) collective-permute-start(f32[6,256]{1,0:T(8,128)S(1)} %get-tuple-element.5), channel_id=1, source_target_pairs={{0,4},{4,8},{8,12},{12,0},{1,5},{5,9},{9,13},{13,1},{2,6},{6,10},{... | collective-permute-start | bytes 18440 | tf_op jit(solution)/shard_map/ppermute | solution.py:306
  4.6 3.7 %collective-permute-start.1 = (f32[6,256]{1,0:T(8,128)S(1)}, f32[6,256]{1,0:T(8,128)S(1)}, u32[]{:S(2)}, u32[]{:S(2)}) collective-permute-start(f32[6,256]{1,0:T(8,128)S(1)} %get-tuple-element.6), channel_id=1, source_target_pairs={{4,0},{8,4},{12,8},{0,12},{5,1},{9,5},{13,9},{1,13},{6,2},{10,6},{... | collective-permute-start | bytes 18440 | tf_op jit(solution)/shard_map/ppermute | solution.py:307
  6.7 0.7 %copy-start.4 = (f32[8]{0:T(128)S(1)}, f32[8]{0:T(128)}, u32[]{:S(2)}) copy-start(f32[8]{0:T(128)} %param.17) | copy-start | bytes 100
  8.3 1.7 %copy-start = (f32[1,3,6,256]{3,2,1,0:T(8,128)}, f32[1,3,6,256]{3,2,1,0:T(8,128)S(1)}, u32[]{:S(2)}) copy-start(f32[1,3,6,256]{3,2,1,0:T(8,128)S(1)} %maximum_bitcast_fusion.refs_3_) | copy-start | bytes 55300
  8.3 10.4 %collective-permute-start.2 = (f32[1,3,6,256]{3,2,1,0:T(8,128)S(1)}, f32[1,3,6,256]{3,2,1,0:T(8,128)S(1)}, u32[]{:S(2)}, u32[]{:S(2)}) collective-permute-start(f32[1,3,6,256]{3,2,1,0:T(8,128)S(1)} %maximum_bitcast_fusion.refs_3_), channel_id=1, source_target_pairs={{0,2},{2,0},{1,3},{3,1},{4,6},{6,4},{5,7},{7,5},{8,10},{10,8},{9,1... | collective-permute-start | bytes 55304 | tf_op jit(solution)/shard_map/ppermute | solution.py:312
  18.8 0.6 %copy-start.5 = (f32[1,3,6,256]{3,2,1,0:T(8,128)}, f32[1,3,6,256]{3,2,1,0:T(8,128)S(1)}, u32[]{:S(2)}) copy-start(f32[1,3,6,256]{3,2,1,0:T(8,128)S(1)} %collective-permute-done.2.refs_3_) | copy-start | bytes 55300

commit v10 on v8

--- a/solution.py
+++ b/solution.py
@@ -106,13 +106,12 @@
     layers = pot_ref.shape[-1] // w
     species_count = table_ref.shape[1]
     hop = pl.program_id(0)
-    layer = pl.program_id(1)
     f32, bf16 = jnp.float32, jnp.bfloat16
 
     def dot(a, b):
         return jnp.dot(a, b, preferred_element_type=f32)
 
-    first = (hop == 0) & (layer == 0)
+    first = hop == 0
     copies = [
         pltpu.make_async_copy(src, dst, sems.at[k])
         for k, (src, dst) in enumerate(
@@ -125,8 +124,7 @@
         for copy in copies:
             copy.start()
 
-    @pl.when(layer == 0)
-    def _():
+    def potentials():
         entry = owner_ref[0]
         blocks = []
         for slot in range(3):
@@ -175,6 +173,8 @@
             )
             pot_ref[p] = dot(across, weighted)
 
+    potentials()
+
     @pl.when(first)
     def _():
         for copy in copies:
@@ -190,31 +190,32 @@
 
     pr = prop_ref[0]
     pi = prop_ref[1]
-    column = pl.ds(pl.multiple_of(layer * w, w), w)
-    transmitted = []
-    for p in range(batch):
-        psi = wave_ref[p]
-        wr = psi[:, :w].astype(f32)
-        wi = psi[:, w:].astype(f32)
-        v = pot_ref[p, :, column]
-        sv, cv = sincos(v)
-        tr = (wr * cv - wi * sv).astype(bf16)
-        ti = (wr * sv + wi * cv).astype(bf16)
-        transmitted.append(jnp.concatenate([tr, ti], 1))
-    rowwise = [dot(t, a_ref[...]).astype(bf16) for t in transmitted]
-    spectra = [dot(b_ref[...], jnp.concatenate([rw[:, :w], rw[:, w:]], 0)) for rw in rowwise]
-    propagated = []
-    for sp in spectra:
-        sr = sp[:w]
-        si = sp[w:]
-        propagated.append(
-            jnp.concatenate([(sr * pr - si * pi).astype(bf16), (sr * pi + si * pr).astype(bf16)], 0)
-        )
-    back = [dot(a_ref[...], spb).astype(bf16) for spb in propagated]
-    for p, br in enumerate(back):
-        wave_ref[p] = dot(jnp.concatenate([br[:w], br[w:]], 1), b_ref[...]).astype(bf16)
-
-    @pl.when((hop == pl.num_programs(0) - 1) & (layer == pl.num_programs(1) - 1))
+    for layer in range(layers):
+        column = pl.ds(layer * w, w)
+        transmitted = []
+        for p in range(batch):
+            psi = wave_ref[p]
+            wr = psi[:, :w].astype(f32)
+            wi = psi[:, w:].astype(f32)
+            v = pot_ref[p, :, column]
+            sv, cv = sincos(v)
+            tr = (wr * cv - wi * sv).astype(bf16)
+            ti = (wr * sv + wi * cv).astype(bf16)
+            transmitted.append(jnp.concatenate([tr, ti], 1))
+        rowwise = [dot(t, a_ref[...]).astype(bf16) for t in transmitted]
+        spectra = [dot(b_ref[...], jnp.concatenate([rw[:, :w], rw[:, w:]], 0)) for rw in rowwise]
+        propagated = []
+        for sp in spectra:
+            sr = sp[:w]
+            si = sp[w:]
+            propagated.append(
+                jnp.concatenate([(sr * pr - si * pi).astype(bf16), (sr * pi + si * pr).astype(bf16)], 0)
+            )
+        back = [dot(a_ref[...], spb).astype(bf16) for spb in propagated]
+        for p, br in enumerate(back):
+            wave_ref[p] = dot(jnp.concatenate([br[:w], br[w:]], 1), b_ref[...]).astype(bf16)
+
+    @pl.when(hop == pl.num_programs(0) - 1)
     def _():
         if final:
             for p in range(batch):
@@ -230,7 +231,7 @@
     w = window
     a, b = dft_blocks(w)
     prop = propagator(w)
-    full = lambda shape: pl.BlockSpec(shape, lambda h, l, *_: (0,) * len(shape))
+    full = lambda shape: pl.BlockSpec(shape, lambda h, *_: (0,) * len(shape))
     carried = wave is not None
     out_shape = (batch, w, 2, w) if final else (batch, w, 2 * w)
     last = wave if carried else jnp.asarray(start_spectrum(w))
@@ -242,10 +243,10 @@
         out_shape=jax.ShapeDtypeStruct(out_shape, jnp.bfloat16),
         grid_spec=pltpu.PrefetchScalarGridSpec(
             num_scalar_prefetch=2,
-            grid=(hops, layers),
+            grid=(hops,),
             in_specs=[
                 pl.BlockSpec(memory_space=pltpu.SMEM),
-                pl.BlockSpec((1,) + packs.shape[1:], lambda h, l, *_: (h, 0, 0, 0)),
+                pl.BlockSpec((1,) + packs.shape[1:], lambda h, *_: (h, 0, 0, 0)),
                 pl.BlockSpec(memory_space=pl.ANY),
                 pl.BlockSpec(memory_space=pl.ANY),
                 pl.BlockSpec(memory_space=pl.ANY),
@@ -263,7 +264,7 @@
             ],
         ),
         compiler_params=pltpu.CompilerParams(
-            dimension_semantics=("arbitrary", "arbitrary"),
+            dimension_semantics=("arbitrary",),
         ),
         cost_estimate=pl.CostEstimate(
             flops=flops,

time: 28.8 us -> 27.9 us (0.969)
  Pallas kernels: 17.7 us -> 16.9 us
    pallas_call x2, Pallas kernels: 17.7 us -> 16.9 us  [run_slices(): pl.pallas_call(functools.partial(slices_kernel, field_x=float(field_x), c...]
where the time goes in v10:
time: 27.9 us; the launch traced here: 27.5 us
  Pallas kernels  16.9 us (61%)
  starting transfers between devices  6.89 us (25%)
  local copies, waits for them, and re-layouts  1.96 us (7%)
  other arithmetic  1.33 us (5%)
  waiting for transfers between devices  0.4 us (1%)
    pallas_call x2, Pallas kernels, run_slices(): pl.pallas_call(functools.partial(slices_kernel, field_x=float(field_x), c...  16.9 us
    ppermute x1, starting transfers between devices, shards(): lax.ppermute(packs[2], 'lat', [(i, (i + 1) % n_lat) for i in range(n_lat)])  3.1 us
    ppermute x1, starting transfers between devices, shards(): lax.ppermute(packs[0], 'lat', [((i + 1) % n_lat, i) for i in range(n_lat)])  2.09 us
    unnamed x14, local copies, waits for them, and re-layouts  1.95 us
    ppermute x1, starting transfers between devices, shards(): lax.ppermute(local, 'slc', [(i, (i - hop) % owners) for i in range(owners)])  1.69 us
    convert_element_type x1, other arithmetic, shards(): marg = jnp.transpose(margin[0, 0, :, 0], (1, 0, 2)).astype(f32)  0.71 us
    another operation x2, other arithmetic, shards(): table = jnp.stack([species_amp, 0.5 / (species_spread * species_spread)], 0)  0.59 us
  transfers between devices with their start and end apart: 3, of which 1 were waited for; matrix products, arithmetic and copies ran while one was open for 2% of the time, Pallas kernels for 31%

profile of v10, /device:TPU:0, one launch (start us, length us, event | category | flops | bytes accessed | tf_op | source)
XLA Modules:
  0.0 27.5 jit_solution(17219523145771847233)
XLA Ops:
  0.0 0.0 copy-start.2
  0.0 0.0 copy-start.3
  0.0 0.7 %fusion = f32[3,2,128]{2,1,0:T(2,128)S(1)} fusion(s32[1,1,2,1,3,128]{5,3,4,2,1,0:T(1,128)} %param.19), kind=kLoop, calls=%fused_computation.7 | loop fusion | flops 768 | bytes 6144 | tf_op jit(solution)/shard_map/convert_element_type | solution.py:289
  0.7 0.0 copy-done.2
  0.7 0.0 copy-done.3
  0.7 0.0 copy-start.1
  0.7 0.7 %copy-done.1 = f32[1,1,2,256]{3,2,1,0:T(2,128)S(1)} copy-done((f32[1,1,2,256]{3,2,1,0:T(2,128)S(1)}, f32[1,1,2,256]{3,2,1,0:T(2,128)}, u32[]{:S(2)}) %copy-start.1) | copy-done | bytes 2072
  1.5 0.0 copy-start.6
  1.5 3.1 %collective-permute-start = (f32[6,256]{1,0:T(8,128)S(1)}, f32[6,256]{1,0:T(8,128)S(1)}, u32[]{:S(2)}, u32[]{:S(2)}) collective-permute-start(f32[6,256]{1,0:T(8,128)S(1)} %get-tuple-element.5), channel_id=1, source_target_pairs={{0,4},{4,8},{8,12},{12,0},{1,5},{5,9},{9,13},{13,1},{2,6},{6,10},{... | collective-permute-start | bytes 18440 | tf_op jit(solution)/shard_map/ppermute | solution.py:292
  4.6 2.1 %collective-permute-start.1 = (f32[6,256]{1,0:T(8,128)S(1)}, f32[6,256]{1,0:T(8,128)S(1)}, u32[]{:S(2)}, u32[]{:S(2)}) collective-permute-start(f32[6,256]{1,0:T(8,128)S(1)} %get-tuple-element.6), channel_id=1, source_target_pairs={{4,0},{8,4},{12,8},{0,12},{5,1},{9,5},{13,9},{1,13},{6,2},{10,6},{... | collective-permute-start | bytes 18440 | tf_op jit(solution)/shard_map/ppermute | solution.py:293
  6.7 0.0 copy-done.6
  6.7 0.0 copy-start.4
  6.7 0.7 %copy-done.4 = f32[8]{0:T(128)S(1)} copy-done((f32[8]{0:T(128)S(1)}, f32[8]{0:T(128)}, u32[]{:S(2)}) %copy-start.4) | copy-done | bytes 56
  7.3 0.6 %pad_maximum_fusion.1.refs_2_ = f32[2,8]{1,0:T(2,128)} fusion(f32[1,8]{1,0:T(1,128)S(1)} %divide_bitcast_fusion, f32[1,8]{1,0:T(1,128)S(1)} %bitcast.24), kind=kLoop, calls=%fused_computation.8 | loop fusion | flops 16 | bytes 128 | tf_op jit(solution)/shard_map/stack | solution.py:301
  7.9 0.4 %collective-permute-done = f32[6,256]{1,0:T(8,128)S(1)} collective-permute-done((f32[6,256]{1,0:T(8,128)S(1)}, f32[6,256]{1,0:T(8,128)S(1)}, u32[]{:S(2)}, u32[]{:S(2)}) %collective-permute-start) | collective-permute-done | bytes 6176 | tf_op jit(solution)/shard_map/ppermute | solution.py:292
  8.3 0.0 collective-permute-done.1
  8.3 0.0 copy-start
  8.3 1.7 %collective-permute-start.2 = (f32[1,3,6,256]{3,2,1,0:T(8,128)S(1)}, f32[1,3,6,256]{3,2,1,0:T(8,128)S(1)}, u32[]{:S(2)}, u32[]{:S(2)}) collective-permute-start(f32[1,3,6,256]{3,2,1,0:T(8,128)S(1)} %maximum_bitcast_fusion.refs_3_), channel_id=1, source_target_pairs={{0,2},{2,0},{1,3},{3,1},{4,6},{6,4},{5,7},{7,5},{8,10},{10,8},{9,1... | collective-permute-start | bytes 55304 | tf_op jit(solution)/shard_map/ppermute | solution.py:298
  10.0 0.0 copy-done
  10.0 8.5 %shard_map.136.refs_7_ = bf16[2,256,512]{2,1,0:T(8,128)(2,1)} custom-call(s32[2,2]{1,0:T(2,128)} %refs_0_.3, s32[1]{0:T(128)} %bitcast.refs_1_, f32[2,8]{1,0:T(2,128)} %pad_maximum_fusion.1.refs_2_, f32[1,3,6,256]{3,2,1,0:T(8,128)} %copy-done, bf16[512,512]{1,0:T(8,128)(2,1)} %constant.17.clone.refs_4_, bf16[512,512]{1,0:T(8,128)(2,1)} %constant.18.clone.refs_5_, ...), custom_call_target="tpu_custom_call" | custom-call | flops 2348810240 | bytes 2359296 | tf_op jit(solution)/shard_map/pallas_call | solution.py:241
  18.6 0.0 collective-permute-done.2.refs_3_
  18.6 0.0 copy-start.5
  18.6 0.6 %copy-done.5 = f32[1,3,6,256]{3,2,1,0:T(8,128)} copy-done((f32[1,3,6,256]{3,2,1,0:T(8,128)}, f32[1,3,6,256]{3,2,1,0:T(8,128)S(1)}, u32[]{:S(2)}) %copy-start.5) | copy-done | bytes 18456
  19.2 8.3 %shard_map.137 = bf16[2,256,2,256]{3,2,1,0:T(2,128)(2,1)} custom-call(s32[2,2]{1,0:T(2,128)} %refs_0_.3, s32[1]{0:T(128)} %bitcast.refs_1_, f32[2,8]{1,0:T(2,128)} %pad_maximum_fusion.1.refs_2_, f32[1,3,6,256]{3,2,1,0:T(8,128)} %copy-done.5, bf16[512,512]{1,0:T(8,128)(2,1)} %constant.17.clone.refs_4_, bf16[512,512]{1,0:T(8,128)(2,1)} %constant.18.clone.refs_5_, ...), custom_call_target="tpu_custom_call" | custom-call | flops 2348810240 | bytes 2359296 | tf_op jit(solution)/shard_map/pallas_call | solution.py:241
  (7 shorter events, 0.0 us)
Async XLA Ops:
  0.0 0.7 %copy-start.2 = (s32[1,1,256]{2,1,0:T(1,128)S(1)}, s32[1,1,256]{2,1,0:T(1,128)}, u32[]{:S(2)}) copy-start(s32[1,1,256]{2,1,0:T(1,128)} %param.16) | copy-start | bytes 3076
  0.0 0.7 %copy-start.3 = (s32[1,1,256]{2,1,0:T(1,128)S(1)}, s32[1,1,256]{2,1,0:T(1,128)}, u32[]{:S(2)}) copy-start(s32[1,1,256]{2,1,0:T(1,128)} %param.15) | copy-start | bytes 3076
  0.7 0.7 %copy-start.1 = (f32[1,1,2,256]{3,2,1,0:T(2,128)S(1)}, f32[1,1,2,256]{3,2,1,0:T(2,128)}, u32[]{:S(2)}) copy-start(f32[1,1,2,256]{3,2,1,0:T(2,128)} %param.14) | copy-start | bytes 6148
  1.5 5.2 %copy-start.6 = (f32[8]{0:T(128)S(1)}, f32[8]{0:T(128)}, u32[]{:S(2)}) copy-start(f32[8]{0:T(128)} %param.18) | copy-start | bytes 100
  1.5 6.8 %collective-permute-start = (f32[6,256]{1,0:T(8,128)S(1)}, f32[6,256]{1,0:T(8,128)S(1)}, u32[]{:S(2)}, u32[]{:S(2)}) collective-permute-start(f32[6,256]{1,0:T(8,128)S(1)} %get-tuple-element.5), channel_id=1, source_target_pairs={{0,4},{4,8},{8,12},{12,0},{1,5},{5,9},{9,13},{13,1},{2,6},{6,10},{... | collective-permute-start | bytes 18440 | tf_op jit(solution)/shard_map/ppermute | solution.py:292
  4.6 3.7 %collective-permute-start.1 = (f32[6,256]{1,0:T(8,128)S(1)}, f32[6,256]{1,0:T(8,128)S(1)}, u32[]{:S(2)}, u32[]{:S(2)}) collective-permute-start(f32[6,256]{1,0:T(8,128)S(1)} %get-tuple-element.6), channel_id=1, source_target_pairs={{4,0},{8,4},{12,8},{0,12},{5,1},{9,5},{13,9},{1,13},{6,2},{10,6},{... | collective-permute-start | bytes 18440 | tf_op jit(solution)/shard_map/ppermute | solution.py:293
  6.7 0.7 %copy-start.4 = (f32[8]{0:T(128)S(1)}, f32[8]{0:T(128)}, u32[]{:S(2)}) copy-start(f32[8]{0:T(128)} %param.17) | copy-start | bytes 100
  8.3 1.7 %copy-start = (f32[1,3,6,256]{3,2,1,0:T(8,128)}, f32[1,3,6,256]{3,2,1,0:T(8,128)S(1)}, u32[]{:S(2)}) copy-start(f32[1,3,6,256]{3,2,1,0:T(8,128)S(1)} %maximum_bitcast_fusion.refs_3_) | copy-start | bytes 55300
  8.3 10.2 %collective-permute-start.2 = (f32[1,3,6,256]{3,2,1,0:T(8,128)S(1)}, f32[1,3,6,256]{3,2,1,0:T(8,128)S(1)}, u32[]{:S(2)}, u32[]{:S(2)}) collective-permute-start(f32[1,3,6,256]{3,2,1,0:T(8,128)S(1)} %maximum_bitcast_fusion.refs_3_), channel_id=1, source_target_pairs={{0,2},{2,0},{1,3},{3,1},{4,6},{6,4},{5,7},{7,5},{8,10},{10,8},{9,1... | collective-permute-start | bytes 55304 | tf_op jit(solution)/shard_map/ppermute | solution.py:298
  18.6 0.6 %copy-start.5 = (f32[1,3,6,256]{3,2,1,0:T(8,128)}, f32[1,3,6,256]{3,2,1,0:T(8,128)S(1)}, u32[]{:S(2)}) copy-start(f32[1,3,6,256]{3,2,1,0:T(8,128)S(1)} %collective-permute-done.2.refs_3_) | copy-start | bytes 55300

commit v11 on v10

--- a/solution.py
+++ b/solution.py
@@ -99,12 +99,12 @@
 
 
 def slices_kernel(*refs, field_x, carried, cap, final):
-    (pos_ref, owner_ref, table_ref, pk_ref, a_hbm, b_hbm, prop_hbm, last_hbm,
+    (pos_ref, owner_ref, amp_ref, spread_ref, pk_ref, a_hbm, b_hbm, prop_hbm, last_hbm,
      out_ref, wave_ref, pot_ref, a_ref, b_ref, prop_ref, last_ref, sems) = refs
     batch = wave_ref.shape[0]
     w = prop_ref.shape[-1]
     layers = pot_ref.shape[-1] // w
-    species_count = table_ref.shape[1]
+    species_count = amp_ref.shape[0]
     hop = pl.program_id(0)
     f32, bf16 = jnp.float32, jnp.bfloat16
 
@@ -128,16 +128,17 @@
         entry = owner_ref[0]
         blocks = []
         for slot in range(3):
-            raw = pk_ref[0, slot, 0:4, :]
-            listed = pk_ref[0, slot, pl.ds(4 + entry, 1), :][:, :cap]
+            raw = pk_ref[hop, slot, 0:4, :]
+            listed = pk_ref[hop, slot, pl.ds(4 + entry, 1), :][:, :cap]
             species = raw[2:3]
             slab = raw[3:4]
             amplitude = jnp.zeros_like(species)
-            inverse = jnp.zeros_like(species)
+            spread = jnp.zeros_like(species)
             for k in range(species_count):
                 match = species == float(k)
-                amplitude = jnp.where(match, table_ref[0, k], amplitude)
-                inverse = jnp.where(match, table_ref[1, k], inverse)
+                amplitude = jnp.where(match, amp_ref[k], amplitude)
+                spread = jnp.where(match, spread_ref[k], spread)
+            inverse = 0.5 / (spread * spread)
             zero = jnp.zeros_like(species)
             per_layer = [jnp.where(slab == float(l), amplitude, zero) for l in range(layers)]
             fields = jnp.concatenate(
@@ -225,7 +226,7 @@
             out_ref[...] = wave_ref[...]
 
 
-def run_slices(probe_pos, entry, table, packs, window, layers, field_x, cap, wave=None, final=False):
+def run_slices(probe_pos, entry, amp, spread, packs, window, layers, field_x, cap, wave=None, final=False):
     batch = probe_pos.shape[0]
     hops = packs.shape[0]
     w = window
@@ -246,7 +247,8 @@
             grid=(hops,),
             in_specs=[
                 pl.BlockSpec(memory_space=pltpu.SMEM),
-                pl.BlockSpec((1,) + packs.shape[1:], lambda h, *_: (h, 0, 0, 0)),
+                pl.BlockSpec(memory_space=pltpu.SMEM),
+                pl.BlockSpec(memory_space=pltpu.VMEM),
                 pl.BlockSpec(memory_space=pl.ANY),
                 pl.BlockSpec(memory_space=pl.ANY),
                 pl.BlockSpec(memory_space=pl.ANY),
@@ -271,7 +273,7 @@
             transcendentals=steps * 2 * w * w + batch * hops * 2 * atoms * w,
             bytes_accessed=2 * (2 * w) ** 2 * 2 + 3 * w * w * 4 + batch * w * w * 4,
         ),
-    )(probe_pos, entry, table, packs, jnp.asarray(a), jnp.asarray(b), jnp.asarray(prop), last)
+    )(probe_pos, entry, amp, spread, packs, jnp.asarray(a), jnp.asarray(b), jnp.asarray(prop), last)
 
 
 def shards(atom_xy, atom_species, atom_slab, species_amp, species_spread, margin, probe_pos):
@@ -298,12 +300,11 @@
         lax.ppermute(local, "slc", [(i, (i - hop) % owners) for i in range(owners)])
         for hop in range(1, owners)
     ]
-    table = jnp.stack([species_amp, 0.5 / (species_spread * species_spread)], 0)
     batch = probe_pos.shape[0]
-    wave = run_slices(probe_pos, entry, table, local, window, layers, field_x, cap, final=not later)
+    wave = run_slices(probe_pos, entry, species_amp, species_spread, local, window, layers, field_x, cap, final=not later)
     if later:
         wave = run_slices(
-            probe_pos, entry, table, jnp.concatenate(later, 0), window, layers, field_x, cap, wave,
+            probe_pos, entry, species_amp, species_spread, jnp.concatenate(later, 0), window, layers, field_x, cap, wave,
             final=True,
         )
     return wave

time: 27.9 us -> 27.9 us (level)
  waiting for transfers between devices: 0.4 us -> 1.65 us
  local copies, waits for them, and re-layouts: 1.96 us -> 1.3 us
  other arithmetic: 1.33 us -> 0.74 us
    ppermute x1, waiting for transfers between devices: 0.4 us -> 1.65 us  [shards(): lax.ppermute(packs[2], 'lat', [(i, (i + 1) % n_lat) for i in range(n_lat)])]
    unnamed x14 -> x10, local copies, waits for them, and re-layouts: 1.95 us -> 1.29 us
    another operation x2 -> x0, other arithmetic: 0.59 us -> none  [shards(): table = jnp.stack([species_amp, 0.5 / (species_spread * species_spread)], 0)]
  transfers between devices with their start and end apart: 3 -> 3, of which waited for: 1 -> 1; matrix products, arithmetic and copies ran while one was open for 2% -> 0% of each run, Pallas kernels for 31% -> 31%
where the time goes in v11:
time: 27.9 us; the launch traced here: 27.6 us
  Pallas kernels  16.9 us (61%)
  starting transfers between devices  6.89 us (25%)
  waiting for transfers between devices  1.65 us (6%)
  local copies, waits for them, and re-layouts  1.3 us (5%)
  other arithmetic  0.74 us (3%)
    pallas_call x2, Pallas kernels, run_slices(): pl.pallas_call(functools.partial(slices_kernel, field_x=float(field_x), c...  16.9 us
    ppermute x1, starting transfers between devices, shards(): lax.ppermute(packs[2], 'lat', [(i, (i + 1) % n_lat) for i in range(n_lat)])  3.1 us
    ppermute x1, starting transfers between devices, shards(): lax.ppermute(packs[0], 'lat', [((i + 1) % n_lat, i) for i in range(n_lat)])  2.09 us
    ppermute x1, starting transfers between devices, shards(): lax.ppermute(local, 'slc', [(i, (i - hop) % owners) for i in range(owners)])  1.69 us
    ppermute x1, waiting for transfers between devices, shards(): lax.ppermute(packs[2], 'lat', [(i, (i + 1) % n_lat) for i in range(n_lat)])  1.65 us
    unnamed x10, local copies, waits for them, and re-layouts  1.29 us
    convert_element_type x1, other arithmetic, shards(): marg = jnp.transpose(margin[0, 0, :, 0], (1, 0, 2)).astype(f32)  0.71 us
  transfers between devices with their start and end apart: 3, of which 1 were waited for; matrix products, arithmetic and copies ran while one was open for 0% of the time, Pallas kernels for 31%

profile of v11, /device:TPU:0, one launch (start us, length us, event | category | flops | bytes accessed | tf_op | source)
XLA Modules:
  0.0 27.6 jit_solution(16349630086742306887)
XLA Ops:
  0.0 0.0 copy-start.2
  0.0 0.0 copy-start.3
  0.0 0.7 %fusion = f32[3,2,128]{2,1,0:T(2,128)S(1)} fusion(s32[1,1,2,1,3,128]{5,3,4,2,1,0:T(1,128)} %param.19), kind=kLoop, calls=%fused_computation.7 | loop fusion | flops 768 | bytes 6144 | tf_op jit(solution)/shard_map/convert_element_type | solution.py:291
  0.7 0.0 copy-done.2
  0.7 0.0 copy-done.3
  0.7 0.0 copy-start.1
  0.7 0.7 %copy-done.1 = f32[1,1,2,256]{3,2,1,0:T(2,128)S(1)} copy-done((f32[1,1,2,256]{3,2,1,0:T(2,128)S(1)}, f32[1,1,2,256]{3,2,1,0:T(2,128)}, u32[]{:S(2)}) %copy-start.1) | copy-done | bytes 2072
  1.5 3.1 %collective-permute-start = (f32[6,256]{1,0:T(8,128)S(1)}, f32[6,256]{1,0:T(8,128)S(1)}, u32[]{:S(2)}, u32[]{:S(2)}) collective-permute-start(f32[6,256]{1,0:T(8,128)S(1)} %get-tuple-element.5), channel_id=1, source_target_pairs={{0,4},{4,8},{8,12},{12,0},{1,5},{5,9},{9,13},{13,1},{2,6},{6,10},{... | collective-permute-start | bytes 18440 | tf_op jit(solution)/shard_map/ppermute | solution.py:294
  4.6 2.1 %collective-permute-start.1 = (f32[6,256]{1,0:T(8,128)S(1)}, f32[6,256]{1,0:T(8,128)S(1)}, u32[]{:S(2)}, u32[]{:S(2)}) collective-permute-start(f32[6,256]{1,0:T(8,128)S(1)} %get-tuple-element.6), channel_id=1, source_target_pairs={{4,0},{8,4},{12,8},{0,12},{5,1},{9,5},{13,9},{1,13},{6,2},{10,6},{... | collective-permute-start | bytes 18440 | tf_op jit(solution)/shard_map/ppermute | solution.py:295
  6.7 1.6 %collective-permute-done = f32[6,256]{1,0:T(8,128)S(1)} collective-permute-done((f32[6,256]{1,0:T(8,128)S(1)}, f32[6,256]{1,0:T(8,128)S(1)}, u32[]{:S(2)}, u32[]{:S(2)}) %collective-permute-start) | collective-permute-done | bytes 6176 | tf_op jit(solution)/shard_map/ppermute | solution.py:294
  8.3 0.0 collective-permute-done.1
  8.3 0.0 copy-start
  8.3 1.7 %collective-permute-start.2 = (f32[1,3,6,256]{3,2,1,0:T(8,128)S(1)}, f32[1,3,6,256]{3,2,1,0:T(8,128)S(1)}, u32[]{:S(2)}, u32[]{:S(2)}) collective-permute-start(f32[1,3,6,256]{3,2,1,0:T(8,128)S(1)} %maximum_bitcast_fusion.refs_4_), channel_id=1, source_target_pairs={{0,2},{2,0},{1,3},{3,1},{4,6},{6,4},{5,7},{7,5},{8,10},{10,8},{9,1... | collective-permute-start | bytes 55304 | tf_op jit(solution)/shard_map/ppermute | solution.py:300
  10.0 0.0 copy-done
  10.0 8.6 %shard_map.136.refs_8_ = bf16[2,256,512]{2,1,0:T(8,128)(2,1)} custom-call(s32[2,2]{1,0:T(2,128)} %refs_0_.3, s32[1]{0:T(128)} %bitcast.refs_1_, f32[8]{0:T(128)} %refs_2_.3, f32[8]{0:T(128)} %refs_3_.3, f32[1,3,6,256]{3,2,1,0:T(8,128)} %copy-done, bf16[512,512]{1,0:T(8,128)(2,1)} %constant.15.clone.refs_5_, bf16[512,512]{1,0:T(8,128)(2,1)} %constant.16.clone.refs_6_, ...), custom_call_target="tpu_custom_call" | custom-call | flops 2348810240 | bytes 2359296 | tf_op jit(solution)/shard_map/pallas_call | solution.py:242
  18.6 0.0 collective-permute-done.2.refs_4_
  18.6 0.0 copy-start.4
  18.6 0.6 %copy-done.4 = f32[1,3,6,256]{3,2,1,0:T(8,128)} copy-done((f32[1,3,6,256]{3,2,1,0:T(8,128)}, f32[1,3,6,256]{3,2,1,0:T(8,128)S(1)}, u32[]{:S(2)}) %copy-start.4) | copy-done | bytes 18456
  19.2 8.3 %shard_map.137 = bf16[2,256,2,256]{3,2,1,0:T(2,128)(2,1)} custom-call(s32[2,2]{1,0:T(2,128)} %refs_0_.3, s32[1]{0:T(128)} %bitcast.refs_1_, f32[8]{0:T(128)} %refs_2_.3, f32[8]{0:T(128)} %refs_3_.3, f32[1,3,6,256]{3,2,1,0:T(8,128)} %copy-done.4, bf16[512,512]{1,0:T(8,128)(2,1)} %constant.15.clone.refs_5_, bf16[512,512]{1,0:T(8,128)(2,1)} %constant.16.clone.refs_6_, ...), custom_call_target="tpu_custom_call" | custom-call | flops 2348810240 | bytes 2359296 | tf_op jit(solution)/shard_map/pallas_call | solution.py:242
  (6 shorter events, 0.0 us)
Async XLA Ops:
  0.0 0.7 %copy-start.2 = (s32[1,1,256]{2,1,0:T(1,128)S(1)}, s32[1,1,256]{2,1,0:T(1,128)}, u32[]{:S(2)}) copy-start(s32[1,1,256]{2,1,0:T(1,128)} %param.16) | copy-start | bytes 3076
  0.0 0.7 %copy-start.3 = (s32[1,1,256]{2,1,0:T(1,128)S(1)}, s32[1,1,256]{2,1,0:T(1,128)}, u32[]{:S(2)}) copy-start(s32[1,1,256]{2,1,0:T(1,128)} %param.15) | copy-start | bytes 3076
  0.7 0.7 %copy-start.1 = (f32[1,1,2,256]{3,2,1,0:T(2,128)S(1)}, f32[1,1,2,256]{3,2,1,0:T(2,128)}, u32[]{:S(2)}) copy-start(f32[1,1,2,256]{3,2,1,0:T(2,128)} %param.14) | copy-start | bytes 6148
  1.5 6.8 %collective-permute-start = (f32[6,256]{1,0:T(8,128)S(1)}, f32[6,256]{1,0:T(8,128)S(1)}, u32[]{:S(2)}, u32[]{:S(2)}) collective-permute-start(f32[6,256]{1,0:T(8,128)S(1)} %get-tuple-element.5), channel_id=1, source_target_pairs={{0,4},{4,8},{8,12},{12,0},{1,5},{5,9},{9,13},{13,1},{2,6},{6,10},{... | collective-permute-start | bytes 18440 | tf_op jit(solution)/shard_map/ppermute | solution.py:294
  4.6 3.7 %collective-permute-start.1 = (f32[6,256]{1,0:T(8,128)S(1)}, f32[6,256]{1,0:T(8,128)S(1)}, u32[]{:S(2)}, u32[]{:S(2)}) collective-permute-start(f32[6,256]{1,0:T(8,128)S(1)} %get-tuple-element.6), channel_id=1, source_target_pairs={{4,0},{8,4},{12,8},{0,12},{5,1},{9,5},{13,9},{1,13},{6,2},{10,6},{... | collective-permute-start | bytes 18440 | tf_op jit(solution)/shard_map/ppermute | solution.py:295
  8.3 1.7 %copy-start = (f32[1,3,6,256]{3,2,1,0:T(8,128)}, f32[1,3,6,256]{3,2,1,0:T(8,128)S(1)}, u32[]{:S(2)}) copy-start(f32[1,3,6,256]{3,2,1,0:T(8,128)S(1)} %maximum_bitcast_fusion.refs_4_) | copy-start | bytes 55300
  8.3 10.3 %collective-permute-start.2 = (f32[1,3,6,256]{3,2,1,0:T(8,128)S(1)}, f32[1,3,6,256]{3,2,1,0:T(8,128)S(1)}, u32[]{:S(2)}, u32[]{:S(2)}) collective-permute-start(f32[1,3,6,256]{3,2,1,0:T(8,128)S(1)} %maximum_bitcast_fusion.refs_4_), channel_id=1, source_target_pairs={{0,2},{2,0},{1,3},{3,1},{4,6},{6,4},{5,7},{7,5},{8,10},{10,8},{9,1... | collective-permute-start | bytes 55304 | tf_op jit(solution)/shard_map/ppermute | solution.py:300
  18.6 0.6 %copy-start.4 = (f32[1,3,6,256]{3,2,1,0:T(8,128)}, f32[1,3,6,256]{3,2,1,0:T(8,128)S(1)}, u32[]{:S(2)}) copy-start(f32[1,3,6,256]{3,2,1,0:T(8,128)S(1)} %collective-permute-done.2.refs_4_) | copy-start | bytes 55300

commit v12 on v11

--- a/solution.py
+++ b/solution.py
@@ -191,30 +191,54 @@
 
     pr = prop_ref[0]
     pi = prop_ref[1]
-    for layer in range(layers):
-        column = pl.ds(layer * w, w)
-        transmitted = []
-        for p in range(batch):
+    def transmit(p, layer):
+        def stage(_):
             psi = wave_ref[p]
             wr = psi[:, :w].astype(f32)
             wi = psi[:, w:].astype(f32)
-            v = pot_ref[p, :, column]
-            sv, cv = sincos(v)
+            sv, cv = sincos(pot_ref[p, :, pl.ds(layer * w, w)])
             tr = (wr * cv - wi * sv).astype(bf16)
             ti = (wr * sv + wi * cv).astype(bf16)
-            transmitted.append(jnp.concatenate([tr, ti], 1))
-        rowwise = [dot(t, a_ref[...]).astype(bf16) for t in transmitted]
-        spectra = [dot(b_ref[...], jnp.concatenate([rw[:, :w], rw[:, w:]], 0)) for rw in rowwise]
-        propagated = []
-        for sp in spectra:
-            sr = sp[:w]
-            si = sp[w:]
-            propagated.append(
-                jnp.concatenate([(sr * pr - si * pi).astype(bf16), (sr * pi + si * pr).astype(bf16)], 0)
-            )
-        back = [dot(a_ref[...], spb).astype(bf16) for spb in propagated]
-        for p, br in enumerate(back):
+            return jnp.concatenate([tr, ti], 1)
+        return stage
+
+    def rowwise(t):
+        return dot(t, a_ref[...]).astype(bf16)
+
+    def spectrum(rw):
+        return dot(b_ref[...], jnp.concatenate([rw[:, :w], rw[:, w:]], 0))
+
+    def propagate(sp):
+        sr = sp[:w]
+        si = sp[w:]
+        return jnp.concatenate(
+            [(sr * pr - si * pi).astype(bf16), (sr * pi + si * pr).astype(bf16)], 0
+        )
+
+    def back_rows(spb):
+        return dot(a_ref[...], spb).astype(bf16)
+
+    def store(p):
+        def stage(br):
             wave_ref[p] = dot(jnp.concatenate([br[:w], br[w:]], 1), b_ref[...]).astype(bf16)
+            return None
+        return stage
+
+    chains = [
+        [
+            stage
+            for layer in range(layers)
+            for stage in (transmit(p, layer), rowwise, spectrum, propagate, back_rows, store(p))
+        ]
+        for p in range(batch)
+    ]
+    values = [None] * batch
+    length = len(chains[0])
+    for t in range(length + batch - 1):
+        for p in range(batch):
+            k = t - p
+            if 0 <= k < length:
+                values[p] = chains[p][k](values[p])
 
     @pl.when(hop == pl.num_programs(0) - 1)
     def _():

time: 27.9 us -> 28.2 us (1.011)
  no operation moved by 1% of the time
where the time goes in v12:
time: 28.2 us; the launch traced here: 27.8 us
  Pallas kernels  17.1 us (61%)
  starting transfers between devices  6.89 us (24%)
  waiting for transfers between devices  1.65 us (6%)
  local copies, waits for them, and re-layouts  1.3 us (5%)
  other arithmetic  0.74 us (3%)
    pallas_call x2, Pallas kernels, run_slices(): pl.pallas_call(functools.partial(slices_kernel, field_x=float(field_x), c...  17.1 us
    ppermute x1, starting transfers between devices, shards(): lax.ppermute(packs[2], 'lat', [(i, (i + 1) % n_lat) for i in range(n_lat)])  3.1 us
    ppermute x1, starting transfers between devices, shards(): lax.ppermute(packs[0], 'lat', [((i + 1) % n_lat, i) for i in range(n_lat)])  2.09 us
    ppermute x1, starting transfers between devices, shards(): lax.ppermute(local, 'slc', [(i, (i - hop) % owners) for i in range(owners)])  1.69 us
    ppermute x1, waiting for transfers between devices, shards(): lax.ppermute(packs[2], 'lat', [(i, (i + 1) % n_lat) for i in range(n_lat)])  1.65 us
    unnamed x10, local copies, waits for them, and re-layouts  1.29 us
    convert_element_type x1, other arithmetic, shards(): marg = jnp.transpose(margin[0, 0, :, 0], (1, 0, 2)).astype(f32)  0.71 us
  transfers between devices with their start and end apart: 3, of which 1 were waited for; matrix products, arithmetic and copies ran while one was open for 0% of the time, Pallas kernels for 31%

profile of v12, /device:TPU:0, one launch (start us, length us, event | category | flops | bytes accessed | tf_op | source)
XLA Modules:
  0.0 27.8 jit_solution(17238363989261188190)
XLA Ops:
  0.0 0.0 copy-start.2
  0.0 0.0 copy-start.3
  0.0 0.7 %fusion = f32[3,2,128]{2,1,0:T(2,128)S(1)} fusion(s32[1,1,2,1,3,128]{5,3,4,2,1,0:T(1,128)} %param.19), kind=kLoop, calls=%fused_computation.7 | loop fusion | flops 768 | bytes 6144 | tf_op jit(solution)/shard_map/convert_element_type | solution.py:315
  0.7 0.0 copy-done.2
  0.7 0.0 copy-done.3
  0.7 0.0 copy-start.1
  0.7 0.7 %copy-done.1 = f32[1,1,2,256]{3,2,1,0:T(2,128)S(1)} copy-done((f32[1,1,2,256]{3,2,1,0:T(2,128)S(1)}, f32[1,1,2,256]{3,2,1,0:T(2,128)}, u32[]{:S(2)}) %copy-start.1) | copy-done | bytes 2072
  1.5 3.1 %collective-permute-start = (f32[6,256]{1,0:T(8,128)S(1)}, f32[6,256]{1,0:T(8,128)S(1)}, u32[]{:S(2)}, u32[]{:S(2)}) collective-permute-start(f32[6,256]{1,0:T(8,128)S(1)} %get-tuple-element.5), channel_id=1, source_target_pairs={{0,4},{4,8},{8,12},{12,0},{1,5},{5,9},{9,13},{13,1},{2,6},{6,10},{... | collective-permute-start | bytes 18440 | tf_op jit(solution)/shard_map/ppermute | solution.py:318
  4.6 2.1 %collective-permute-start.1 = (f32[6,256]{1,0:T(8,128)S(1)}, f32[6,256]{1,0:T(8,128)S(1)}, u32[]{:S(2)}, u32[]{:S(2)}) collective-permute-start(f32[6,256]{1,0:T(8,128)S(1)} %get-tuple-element.6), channel_id=1, source_target_pairs={{4,0},{8,4},{12,8},{0,12},{5,1},{9,5},{13,9},{1,13},{6,2},{10,6},{... | collective-permute-start | bytes 18440 | tf_op jit(solution)/shard_map/ppermute | solution.py:319
  6.7 1.6 %collective-permute-done = f32[6,256]{1,0:T(8,128)S(1)} collective-permute-done((f32[6,256]{1,0:T(8,128)S(1)}, f32[6,256]{1,0:T(8,128)S(1)}, u32[]{:S(2)}, u32[]{:S(2)}) %collective-permute-start) | collective-permute-done | bytes 6176 | tf_op jit(solution)/shard_map/ppermute | solution.py:318
  8.3 0.0 collective-permute-done.1
  8.3 0.0 copy-start
  8.3 1.7 %collective-permute-start.2 = (f32[1,3,6,256]{3,2,1,0:T(8,128)S(1)}, f32[1,3,6,256]{3,2,1,0:T(8,128)S(1)}, u32[]{:S(2)}, u32[]{:S(2)}) collective-permute-start(f32[1,3,6,256]{3,2,1,0:T(8,128)S(1)} %maximum_bitcast_fusion.refs_4_), channel_id=1, source_target_pairs={{0,2},{2,0},{1,3},{3,1},{4,6},{6,4},{5,7},{7,5},{8,10},{10,8},{9,1... | collective-permute-start | bytes 55304 | tf_op jit(solution)/shard_map/ppermute | solution.py:324
  10.0 0.0 copy-done
  10.0 8.6 %shard_map.136.refs_8_ = bf16[2,256,512]{2,1,0:T(8,128)(2,1)} custom-call(s32[2,2]{1,0:T(2,128)} %refs_0_.3, s32[1]{0:T(128)} %bitcast.refs_1_, f32[8]{0:T(128)} %refs_2_.3, f32[8]{0:T(128)} %refs_3_.3, f32[1,3,6,256]{3,2,1,0:T(8,128)} %copy-done, bf16[512,512]{1,0:T(8,128)(2,1)} %constant.15.clone.refs_5_, bf16[512,512]{1,0:T(8,128)(2,1)} %constant.16.clone.refs_6_, ...), custom_call_target="tpu_custom_call" | custom-call | flops 2348810240 | bytes 2359296 | tf_op jit(solution)/shard_map/pallas_call | solution.py:266
  18.7 0.0 collective-permute-done.2.refs_4_
  18.7 0.0 copy-start.4
  18.7 0.6 %copy-done.4 = f32[1,3,6,256]{3,2,1,0:T(8,128)} copy-done((f32[1,3,6,256]{3,2,1,0:T(8,128)}, f32[1,3,6,256]{3,2,1,0:T(8,128)S(1)}, u32[]{:S(2)}) %copy-start.4) | copy-done | bytes 18456
  19.3 8.5 %shard_map.137 = bf16[2,256,2,256]{3,2,1,0:T(2,128)(2,1)} custom-call(s32[2,2]{1,0:T(2,128)} %refs_0_.3, s32[1]{0:T(128)} %bitcast.refs_1_, f32[8]{0:T(128)} %refs_2_.3, f32[8]{0:T(128)} %refs_3_.3, f32[1,3,6,256]{3,2,1,0:T(8,128)} %copy-done.4, bf16[512,512]{1,0:T(8,128)(2,1)} %constant.15.clone.refs_5_, bf16[512,512]{1,0:T(8,128)(2,1)} %constant.16.clone.refs_6_, ...), custom_call_target="tpu_custom_call" | custom-call | flops 2348810240 | bytes 2359296 | tf_op jit(solution)/shard_map/pallas_call | solution.py:266
  (6 shorter events, 0.0 us)
Async XLA Ops:
  0.0 0.7 %copy-start.2 = (s32[1,1,256]{2,1,0:T(1,128)S(1)}, s32[1,1,256]{2,1,0:T(1,128)}, u32[]{:S(2)}) copy-start(s32[1,1,256]{2,1,0:T(1,128)} %param.16) | copy-start | bytes 3076
  0.0 0.7 %copy-start.3 = (s32[1,1,256]{2,1,0:T(1,128)S(1)}, s32[1,1,256]{2,1,0:T(1,128)}, u32[]{:S(2)}) copy-start(s32[1,1,256]{2,1,0:T(1,128)} %param.15) | copy-start | bytes 3076
  0.7 0.7 %copy-start.1 = (f32[1,1,2,256]{3,2,1,0:T(2,128)S(1)}, f32[1,1,2,256]{3,2,1,0:T(2,128)}, u32[]{:S(2)}) copy-start(f32[1,1,2,256]{3,2,1,0:T(2,128)} %param.14) | copy-start | bytes 6148
  1.5 6.8 %collective-permute-start = (f32[6,256]{1,0:T(8,128)S(1)}, f32[6,256]{1,0:T(8,128)S(1)}, u32[]{:S(2)}, u32[]{:S(2)}) collective-permute-start(f32[6,256]{1,0:T(8,128)S(1)} %get-tuple-element.5), channel_id=1, source_target_pairs={{0,4},{4,8},{8,12},{12,0},{1,5},{5,9},{9,13},{13,1},{2,6},{6,10},{... | collective-permute-start | bytes 18440 | tf_op jit(solution)/shard_map/ppermute | solution.py:318
  4.6 3.7 %collective-permute-start.1 = (f32[6,256]{1,0:T(8,128)S(1)}, f32[6,256]{1,0:T(8,128)S(1)}, u32[]{:S(2)}, u32[]{:S(2)}) collective-permute-start(f32[6,256]{1,0:T(8,128)S(1)} %get-tuple-element.6), channel_id=1, source_target_pairs={{4,0},{8,4},{12,8},{0,12},{5,1},{9,5},{13,9},{1,13},{6,2},{10,6},{... | collective-permute-start | bytes 18440 | tf_op jit(solution)/shard_map/ppermute | solution.py:319
  8.3 1.7 %copy-start = (f32[1,3,6,256]{3,2,1,0:T(8,128)}, f32[1,3,6,256]{3,2,1,0:T(8,128)S(1)}, u32[]{:S(2)}) copy-start(f32[1,3,6,256]{3,2,1,0:T(8,128)S(1)} %maximum_bitcast_fusion.refs_4_) | copy-start | bytes 55300
  8.3 10.3 %collective-permute-start.2 = (f32[1,3,6,256]{3,2,1,0:T(8,128)S(1)}, f32[1,3,6,256]{3,2,1,0:T(8,128)S(1)}, u32[]{:S(2)}, u32[]{:S(2)}) collective-permute-start(f32[1,3,6,256]{3,2,1,0:T(8,128)S(1)} %maximum_bitcast_fusion.refs_4_), channel_id=1, source_target_pairs={{0,2},{2,0},{1,3},{3,1},{4,6},{6,4},{5,7},{7,5},{8,10},{10,8},{9,1... | collective-permute-start | bytes 55304 | tf_op jit(solution)/shard_map/ppermute | solution.py:324
  18.7 0.6 %copy-start.4 = (f32[1,3,6,256]{3,2,1,0:T(8,128)}, f32[1,3,6,256]{3,2,1,0:T(8,128)S(1)}, u32[]{:S(2)}) copy-start(f32[1,3,6,256]{3,2,1,0:T(8,128)S(1)} %collective-permute-done.2.refs_4_) | copy-start | bytes 55300
